TPU v7x, 32 devices: a whole 2x2x4 slice. The times are simulated.
32 devices in a mesh: ctx: 8 (over z, x), head: 4 (over y, core).
Axes of the slice: x: 2, y: 2, z: 4, core: 2. Of those that a mesh axis runs over, the one named last changes fastest.
Arguments:
- queries: bfloat16 [4096, 4096], P('ctx', 'head'), may hold values from -6 to 6
- key_states: bfloat16 [4096, 4096], P('ctx', 'head'), may hold values from -6 to 6
- value_states: bfloat16 [4096, 4096], P('ctx', 'head'), may hold values from -6 to 6
- transition_vectors: bfloat16 [4096, 4096], P('ctx', 'head'), may hold values from -6 to 6
- beta_logit: float32 [4096, 32], P('ctx', 'head'), may hold values from -6 to 6
- document_ids: int32 [4096], P('ctx'), may hold values from 0 to 7, as said below
- out_weight: bfloat16 [4096, 4096], P('head'), may hold values from -0.09375 to 0.09375
Outputs:
- layer_out: bfloat16 [4096, 4096], P(('ctx', 'head'))
Inputs may be any that keep to these rules, and one draw needn't show every extreme that they name: `document_ids`: document ids never fall along the sequence; document 0 is the first 2304 tokens; the other documents have 1 or more tokens each and together fill the rest.
All inputs are finite; a program needn't handle non-finite values.
Results may differ from a plain program's by a relative error of at most 0.022.
Values may be sent and summed in bfloat16 or wider, within the bound.
No kernel may reach another device: no remote copies, remote signals or barrier semaphores. Data moves between devices by JAX's collectives and lax.ppermute only.
A program may use at most 128 MiB of HBM per device.

v0:
```python
import jax
import jax.numpy as jnp
from jax import lax
from jax.sharding import PartitionSpec as P

epsilon = 1e-06
masked_value = -1e30
highest = lax.Precision.HIGHEST


def tile_inverse(tiles):
    width = tiles.shape[-1]
    row_ids = jnp.arange(width)[:, None]
    col_ids = jnp.arange(width)[None, :]
    identity = jnp.eye(width, dtype=jnp.float32)
    leaf_part = jnp.where((row_ids // 8) == (col_ids // 8), tiles, 0.0)
    square = jnp.matmul(leaf_part, leaf_part, precision=highest)
    fourth = jnp.matmul(square, square, precision=highest)
    inverse = jnp.matmul(identity - leaf_part, identity + square, precision=highest)
    inverse = jnp.matmul(inverse, identity + fourth, precision=highest)
    size = 8
    while size < width:
        pair_lower = (
            ((row_ids // (2 * size)) == (col_ids // (2 * size)))
            & ((row_ids // size) % 2 == 1)
            & ((col_ids // size) % 2 == 0)
        )
        corner = jnp.where(pair_lower, tiles, 0.0)
        inverse = inverse - jnp.matmul(
            inverse, jnp.matmul(corner, inverse, precision=highest), precision=highest
        )
        size *= 2
    return inverse


def unit_lower_inverse(strict_lower):
    rows_total = strict_lower.shape[0]
    tile = 128
    count = rows_total // tile
    blocks = [
        strict_lower[q * tile:(q + 1) * tile, q * tile:(q + 1) * tile][None] for q in range(count)
    ]
    inverses = list(tile_inverse(jnp.concatenate(blocks, axis=0)))
    size = tile
    while size < rows_total:
        merged = []
        for p in range(len(inverses) // 2):
            first = inverses[2 * p]
            second = inverses[2 * p + 1]
            start = 2 * p * size
            lower = strict_lower[start + size:start + 2 * size, start:start + size]
            corner = -jnp.dot(second, jnp.dot(lower, first, precision=highest), precision=highest)
            top = jnp.concatenate([first, jnp.zeros_like(first)], axis=1)
            bottom = jnp.concatenate([corner, second], axis=1)
            merged.append(jnp.concatenate([top, bottom], axis=0))
        inverses = merged
        size *= 2
    return inverses[0]


def lower_solve(strict_lower, right):
    rows_total = strict_lower.shape[0]
    tile = 128
    count = rows_total // tile
    if rows_total % tile or count & (count - 1):
        unit_lower = strict_lower + jnp.eye(rows_total, dtype=jnp.float32)
        return lax.linalg.triangular_solve(
            unit_lower, right, left_side=True, lower=True, unit_diagonal=True
        )
    return jnp.dot(unit_lower_inverse(strict_lower), right, precision=highest)


def shard_operators(query_block, key_block, vector_block, strength):
    block_rows = key_block.shape[0]
    head_width = key_block.shape[1]
    row_ids = jnp.arange(block_rows)
    strict = row_ids[:, None] > row_ids[None, :]
    causal = row_ids[:, None] >= row_ids[None, :]
    intersections = jnp.dot(vector_block, vector_block.T, precision=highest)
    strict_lower = jnp.where(strict, intersections * strength[None, :], 0.0)
    key_proj = jnp.where(strict, jnp.dot(vector_block, key_block.T, precision=highest), 0.0)
    solved = lower_solve(strict_lower, jnp.concatenate([key_proj, vector_block], axis=1))
    key_solve = solved[:, :block_rows]
    vector_solve = solved[:, block_rows:]
    weighted = strength[:, None] * vector_block
    keys_end = (key_block - jnp.dot(key_solve.T, weighted, precision=highest)).astype(jnp.bfloat16)
    transfer = jnp.eye(head_width, dtype=jnp.float32) - jnp.dot(
        vector_block.T, strength[:, None] * vector_solve, precision=highest
    )
    query_dots = jnp.where(causal, jnp.dot(query_block, vector_block.T, precision=highest), 0.0)
    scaled_dots = query_dots * strength[None, :]
    intra_scores = jnp.dot(query_block, key_block.T, precision=highest) - jnp.dot(
        scaled_dots, key_solve, precision=highest
    )
    rotated = query_block - jnp.dot(scaled_dots, vector_solve, precision=highest)
    return (intra_scores, keys_end, transfer, rotated)


def on_device(
    queries, key_states, value_states, transition_vectors, beta_logit, document_ids, out_weight
):
    block_rows = queries.shape[0]
    head_count = beta_logit.shape[1]
    head_width = queries.shape[1] // head_count
    score_scale = head_width ** (-0.5)

    def split_heads(flat):
        return jnp.transpose(flat.reshape(block_rows, head_count, head_width), (1, 0, 2))

    query_heads = split_heads(queries).astype(jnp.float32)
    key_heads = split_heads(key_states).astype(jnp.float32)
    value_heads = split_heads(value_states)
    vector_heads = split_heads(transition_vectors).astype(jnp.float32)
    value_columns = jnp.transpose(value_states.reshape(block_rows, head_count, head_width), (1, 2, 0))
    value_columns, vector_heads = lax.optimization_barrier((value_columns, vector_heads))
    unit_vectors = vector_heads / jnp.sqrt(
        jnp.sum(vector_heads * vector_heads, axis=2, keepdims=True) + epsilon
    )
    strength = 2.0 * jax.nn.sigmoid(beta_logit.T)
    every_value = lax.all_gather(value_columns, "ctx", axis=2, tiled=True)
    intra_scores, keys_end, transfer, rotated = jax.vmap(shard_operators)(
        query_heads, key_heads, unit_vectors, strength
    )
    every_value, keys_end = lax.optimization_barrier((every_value, keys_end))
    row_ids = jnp.arange(block_rows)
    causal = row_ids[:, None] >= row_ids[None, :]
    doc_float = (document_ids + 1).astype(jnp.float32)
    same_doc = doc_float[:, None] == doc_float[None, :]
    own_scores = jnp.where((causal & same_doc)[None], intra_scores * score_scale, masked_value)
    running_max = jnp.max(own_scores, axis=2)
    weights = jnp.exp(own_scores - running_max[..., None])
    running_sum = jnp.sum(weights, axis=2)
    accumulated = jnp.einsum(
        "hqk,hkd->hqd",
        weights.astype(jnp.bfloat16),
        value_heads,
        preferred_element_type=jnp.float32,
    )
    ctx_index = lax.axis_index("ctx")
    ctx_count = lax.axis_size("ctx")

    def attend(carried, key_pair, value_pair, transfer_in, key_docs):
        turned, running_max, running_sum, accumulated = carried
        scores = jnp.einsum(
            "hqd,hkd->hqk",
            turned.astype(jnp.bfloat16),
            key_pair,
            preferred_element_type=jnp.float32,
        )
        allowed = doc_float[:, None] == key_docs[None, :]
        scores = jnp.where(allowed[None], scores * score_scale, masked_value)
        new_max = jnp.maximum(running_max, jnp.max(scores, axis=2))
        factor = jnp.exp(running_max - new_max)
        weights = jnp.exp(scores - new_max[..., None])
        running_sum = running_sum * factor + jnp.sum(weights, axis=2)
        accumulated = accumulated * factor[..., None] + jnp.einsum(
            "hqk,hdk->hqd",
            weights.astype(jnp.bfloat16),
            value_pair,
            preferred_element_type=jnp.float32,
        )
        turned = jnp.einsum("hqd,hde->hqe", turned, transfer_in, precision=highest)
        return (turned, new_max, running_sum, accumulated)

    carried = (rotated, running_max, running_sum, accumulated)
    doc_rows = doc_float.reshape(-1, head_width)
    pad_rows = (-doc_rows.shape[0]) % 8
    doc_rows = jnp.concatenate([doc_rows, jnp.zeros((pad_rows, head_width), jnp.float32)], axis=0)
    meta_rows = jnp.concatenate(
        [transfer.reshape(head_count * head_width, head_width), doc_rows], axis=0
    ).astype(jnp.bfloat16)
    first_doc = doc_float[0]
    is_live = jnp.bool_(True)
    for offset in range(1, ctx_count):
        pairs = [(s, s + offset) for s in range(ctx_count - offset)]
        key_pair = lax.ppermute(keys_end, "ctx", pairs)
        meta_in = lax.ppermute(meta_rows, "ctx", pairs).astype(jnp.float32)
        transfer_in = meta_in[: head_count * head_width].reshape(head_count, head_width, head_width)
        key_docs = meta_in[head_count * head_width :].reshape(-1)[:block_rows]
        source = jnp.maximum(ctx_index - offset, 0)
        value_pair = lax.dynamic_slice_in_dim(every_value, source * block_rows, block_rows, 2)
        is_live = is_live & (ctx_index - offset >= 0) & (key_docs[block_rows - 1] == first_doc)
        carried = lax.cond(
            is_live,
            lambda inner, k=key_pair, v=value_pair, t=transfer_in, d=key_docs: attend(inner, k, v, t, d),
            lambda inner: inner,
            carried,
        )
    attended = (carried[3] / carried[2][..., None]).astype(jnp.bfloat16)
    token_rows = jnp.transpose(attended, (1, 0, 2)).reshape(block_rows, head_count * head_width)
    return lax.psum_scatter(
        jnp.dot(token_rows, out_weight, preferred_element_type=jnp.float32).astype(jnp.bfloat16),
        "head",
        scatter_dimension=0,
        tiled=True,
    )


def solution(mesh):
    return jax.shard_map(
        on_device,
        mesh=mesh,
        in_specs=(
            P("ctx", "head"),
            P("ctx", "head"),
            P("ctx", "head"),
            P("ctx", "head"),
            P("ctx", "head"),
            P("ctx"),
            P("head", None),
        ),
        out_specs=P(("ctx", "head"), None),
        check_vma=False,
    )
```

profile of v0, /device:TPU:16, one launch (start us, length us, event | category | flops | bytes accessed | tf_op | source)
XLA Modules:
  0.0 461.6 jit_solution(17616836672786985320)
XLA Ops:
  17.9 7.3 %multiply_select_fusion.8 = f32[8,512,512]{2,1,0:T(8,128)S(1)} fusion(f32[8,512]{1,0:T(8,128)S(1)} %multiply_bitcast_fusion, pred[512,512]{1,0:T(8,128)(4,1)S(1)} %iota_compare_fusion.4, f32[8,512,128]{2,1,0:T(8,128)S(1)} %broadcast_divide_fusion), kind=kOutput, calls=%fused_computation.148 | convolution fusion | flops 3225419776 | bytes 10764288 | tf_op jit(solution)/shard_map/vmap()/dot_general | solution.py:79
  63.9 6.1 %broadcast_select_fusion = f32[8,512,512]{2,1,0:T(8,128)} fusion(pred[512,512]{1,0:T(8,128)(4,1)S(1)} %iota_compare_fusion.4, f32[8,512,128]{2,1,0:T(8,128)S(1)} %broadcast_divide_fusion, bf16[512,8,128]{2,0,1:T(8,128)(2,1)S(1)} %copy.52), kind=kOutput, calls=%fused_computation.163 | convolution fusion | flops 3223322624 | bytes 11796480 | tf_op jit(solution)/shard_map/vmap()/dot_general | solution.py:81
  70.0 24.4 %fusion.109 = f32[8,512,640]{2,1,0:T(8,128)} fusion(f32[8,512,128]{2,1,0:T(8,128)S(1)} %broadcast_divide_fusion, f32[8,512,512]{2,1,0:T(8,128)} %broadcast_select_fusion, f32[8,256,256]{2,1,0:T(8,128)S(1)} %select_maximum_fusion.2, f32[8,128,128]{2,1,0:T(8,128)S(1)} %get-tuple-element.490, f32[8,128,128]{2,1,0:T(8,128)S(1)} %convolution_negate_fusion, ...), kind=kOutput, calls=%fused_computation.130 | convolution fusion | flops 16121331712 | bytes 27262976 | tf_op jit(solution)/shard_map/vmap()/dot_general | solution.py:70
  94.3 5.6 %fusion.189 = bf16[8,128,128]{2,1,0:T(8,128)(2,1)S(1)} fusion(f32[8,512,128]{2,1,0:T(8,128)S(1)} %broadcast_divide_fusion, f32[8,512,640]{2,1,0:T(8,128)} %fusion.109, f32[8,512]{1,0:T(8,128)S(1)} %multiply_bitcast_fusion, f32[128,128]{1,0:T(8,128)S(1)} %get-tuple-element.511), kind=kOutput, calls=%fused_computation.215 | convolution fusion | flops 806092800 | bytes 4538368 | tf_op jit(solution)/shard_map/vmap()/dot_general | solution.py:87
  104.7 3.5 collective-permute-start.1
  115.8 5.0 %fusion.193 = f32[8,512,512]{1,2,0:T(8,128)S(1)} fusion(f32[8,512,128]{2,1,0:T(8,128)S(1)} %broadcast_divide_fusion, bf16[512,8,128]{2,0,1:T(8,128)(2,1)} %copy.55), kind=kOutput, calls=%fused_computation.217 | convolution fusion | flops 3221225472 | bytes 11534336 | tf_op jit(solution)/shard_map/vmap()/dot_general | solution.py:90
  120.8 15.3 %subtract_convert_fusion = bf16[8,512,128]{2,1,0:T(8,128)(2,1)} fusion(f32[8,512,128]{2,1,0:T(8,128)S(1)} %broadcast_divide_fusion, f32[8,512,640]{2,1,0:T(8,128)S(1)} %copy-done.1, bf16[512,8,128]{2,0,1:T(8,128)(2,1)S(1)} %copy-done.6, f32[8,512]{1,0:T(8,128)S(1)} %multiply_bitcast_fusion), kind=kOutput, calls=%fused_computation.195 | convolution fusion | flops 3223322624 | bytes 12599296 | tf_op jit(solution)/shard_map/vmap()/dot_general | solution.py:86
  136.1 8.5 %convert_subtract_fusion = f32[8,512,128]{2,1,0:T(8,128)S(1)} fusion(f32[8,512,640]{2,1,0:T(8,128)S(1)} %copy-done.1, f32[8,512,512]{1,2,0:T(8,128)S(1)} %fusion.193, f32[8,512]{1,0:T(8,128)S(1)} %multiply_bitcast_fusion, pred[512,512]{1,0:T(8,128)(4,1)S(1)} %iota_compare_fusion.3, bf16[512,8,128]{2,0,1:T(8,128)(2,1)S(1)} %copy-done.7), kind=kOutput, calls=%fused_computation.197 | convolution fusion | flops 3226468352 | bytes 13910016 | tf_op jit(solution)/shard_map/vmap()/dot_general | solution.py:95
  144.6 18.7 %fusion.124 = f32[8,512,512]{1,2,0:T(8,128)} fusion(f32[8,512,640]{2,1,0:T(8,128)S(1)} %copy-done.1, f32[8,512,512]{1,2,0:T(8,128)S(1)} %fusion.193, f32[8,512]{1,0:T(8,128)S(1)} %multiply_bitcast_fusion, pred[512,512]{1,0:T(8,128)(4,1)} %copy-done.20), kind=kOutput, calls=%fused_computation.151 | convolution fusion | flops 12889096192 | bytes 25444352 | tf_op jit(solution)/shard_map/vmap()/dot_general | solution.py:92
  163.4 6.0 %fusion.216 = (f32[8,512]{1,0:T(8,128)S(1)}, f32[8,512,512]{1,2,0:T(8,128)S(1)}) fusion(f32[8,512,512]{1,2,0:T(8,128)} %fusion.124, bf16[512,8,128]{2,0,1:T(8,128)(2,1)} %copy-done.5, bf16[512,8,128]{2,0,1:T(8,128)(2,1)} %copy.55, pred[512,512]{0,1:T(8,128)(4,1)} %copy.57), kind=kOutput, calls=%fused_computation.316 | convolution fusion | flops 545255424 | bytes 19152896 | tf_op jit(solution)/shard_map/vmap()/dot_general | solution.py:92
  179.5 4.5 fusion.127
  196.8 36.0 %collective-permute-start.9 = (bf16[8,512,128]{2,1,0:T(8,128)(2,1)}, bf16[8,512,128]{2,1,0:T(8,128)(2,1)}, u32[]{:S(2)}, u32[]{:S(2)}) collective-permute-start(bf16[8,512,128]{2,1,0:T(8,128)(2,1)} %subtract_convert_fusion), channel_id=1, source_target_pairs={{0,12},{4,16},{8,20},{12,24},{16,28},{1,13},{5,17},{9,21},{13,25},... | collective-permute-start | bytes 3145736 | tf_op jit(solution)/shard_map/ppermute | solution.py:176
  255.2 4.9 %constant_dynamic-slice_fusion = (bf16[8,128,512]{2,1,0:T(8,128)(2,1)}, bf16[8,128,512]{2,1,0:T(8,128)(2,1)}, bf16[8,128,512]{2,1,0:T(8,128)(2,1)}, bf16[8,128,512]{2,1,0:T(8,128)(2,1)}, bf16[8,128,512]{2,1,0:T(8,128)(2,1)}) fusion(bf16[8,128,4096]{2,1,0:T(8,128)(2,1)} %all-gather.2.cloned.1.call-done, s32[]{:T(128)S(6)} %select_n.287, s32[]{:T(128)S(6)} %select_n.286, ...), kind=kLoop, calls=%fused_computation.278 | loop fusion | bytes 10485780 | tf_op jit(solution)/shard_map/dynamic_slice | solution.py:181
  260.2 12.0 %conditional.7 = ((f32[8,512,128]{2,1,0:T(8,128)S(1)}, f32[8,512]{1,0:T(8,128)S(1)}, f32[8,512]{1,0:T(8,128)S(1)}, f32[8,512,128]{2,1,0:T(8,128)})) conditional(s32[]{:T(128)} %convert_element_type.156, (f32[8,512,128]{2,1,0:T(8,128)S(1)}, f32[8,512]{1,0:T(8,128)S(1)}, f32[8,512]{1,0:T(8,128)S(1)}, f32[8,512,128]{2,1,0:T(8,128)}) %tuple.62, ...), branch_computations={%region_3.4_spmd, %region_4.7_spmd} | conditional | flops 1903960064 | bytes 66850968 | solution.py:183
  267.2 3.4 multiply_add_fusion
  272.2 11.8 %conditional.8 = ((f32[8,512,128]{2,1,0:T(8,128)S(1)}, f32[8,512]{1,0:T(8,128)S(1)}, f32[8,512]{1,0:T(8,128)S(1)}, f32[8,512,128]{2,1,0:T(8,128)})) conditional(s32[]{:T(128)} %convert_element_type.155, (f32[8,512,128]{2,1,0:T(8,128)S(1)}, f32[8,512]{1,0:T(8,128)S(1)}, f32[8,512]{1,0:T(8,128)S(1)}, f32[8,512,128]{2,1,0:T(8,128)}) %get-tuple-element.565, ...), branch_computations={%region_7.8_spmd, %region_8.11_spmd} | conditional | flops 1903960064 | bytes 66850968 | solution.py:183
  279.2 3.4 multiply_add_fusion.2
  284.0 12.2 %conditional.9 = ((f32[8,512,128]{2,1,0:T(8,128)S(1)}, f32[8,512]{1,0:T(8,128)S(1)}, f32[8,512]{1,0:T(8,128)S(1)}, f32[8,512,128]{2,1,0:T(8,128)})) conditional(s32[]{:T(128)} %convert_element_type.154, (f32[8,512,128]{2,1,0:T(8,128)S(1)}, f32[8,512]{1,0:T(8,128)S(1)}, f32[8,512]{1,0:T(8,128)S(1)}, ...), branch_computations={%region_11.12_spmd, %region_12.15_spmd} | conditional | flops 1903960064 | bytes 66850968 | solution.py:183
  291.4 3.4 multiply_add_fusion.4
  296.2 11.9 %conditional.10 = ((f32[8,512,128]{2,1,0:T(8,128)S(1)}, f32[8,512]{1,0:T(8,128)S(1)}, f32[8,512]{1,0:T(8,128)S(1)}, f32[8,512,128]{2,1,0:T(8,128)})) conditional(s32[]{:T(128)} %convert_element_type.153, (f32[8,512,128]{2,1,0:T(8,128)S(1)}, f32[8,512]{1,0:T(8,128)S(1)}, f32[8,512]{1,0:T(8,128)S(1)}, ...), branch_computations={%region_15.16_spmd, %region_16.19_spmd} | conditional | flops 1903960064 | bytes 66850968 | solution.py:183
  308.3 6.6 %conditional.12 = ((f32[8,512,128]{2,1,0:T(8,128)S(1)}, f32[8,512]{1,0:T(8,128)S(1)}, f32[8,512]{1,0:T(8,128)S(1)}, f32[8,512,128]{2,1,0:T(8,128)})) conditional(s32[]{:T(128)} %convert_element_type.151, (f32[8,512,128]{2,1,0:T(8,128)S(1)}, f32[8,512]{1,0:T(8,128)S(1)}, f32[8,512]{1,0:T(8,128)S(1)}, ...), branch_computations={%region_23.24_spmd, %region_24.27_spmd} | conditional | flops 1903960064 | bytes 78385280 | solution.py:183
  315.0 7.1 %conditional.13 = (f32[8,512]{1,0:T(8,128)S(1)}, f32[8,512,128]{1,2,0:T(8,128)S(1)}) conditional(s32[]{:T(128)} %convert_element_type.150, (f32[8,512]{1,0:T(8,128)S(1)}, f32[8,512,128]{2,1,0:T(8,128)}) %tuple.70, (f32[512]{0:T(512)S(1)}, f32[512]{0:T(512)S(1)}, f32[8,512,128]{2,1,0:T(8,128)S(1)}, bf16[8,512,128]{2,1,0:T(8,128)(2,1)}, ...), branch_computations={%region_27.28_spmd, %region_28.31_spmd} | conditional | flops 1098653696 | bytes 80973952 | solution.py:183
  322.4 9.5 %convolution_convert_fusion = bf16[512,4096]{1,0:T(8,128)(2,1)} fusion(bf16[512,1024]{0,1:T(8,128)(2,1)S(1)} %bitcast.159, bf16[1024,4096]{1,0:T(8,128)(2,1)} %param.27), kind=kOutput, calls=%fused_computation.156 | convolution fusion | flops 4297064448 | bytes 13631488 | tf_op jit(solution)/shard_map/dot_general | solution.py:192
  332.0 122.7 %reduce-scatter.2.cloned.1.call-done = bf16[128,4096]{1,0:T(8,128)(2,1)} async-done(((bf16[512,4096]{1,0:T(8,128)(2,1)}), bf16[128,4096]{1,0:T(8,128)(2,1)}) %reduce-scatter.2.cloned.1.call-update) | async-done | bytes 1048592 | tf_op jit(solution)/shard_map/reduce_scatter | solution.py:191
  (204 shorter events, 137.4 us)
Async XLA Ops:
  6.5 169.1 %all-gather.2.cloned.1.call-start = ((), (), s32[]{:S(2)}) async-start(), calls=%async_computation.1 | async-start | bytes 9437184 | tf_op jit(solution)/shard_map/all_gather | solution.py:120
  10.0 444.6 %reduce-scatter.2.cloned.1.call-start = ((), (), s32[]{:S(2)}) async-start(), calls=%async_computation.2 | async-start | bytes 5242880 | tf_op jit(solution)/shard_map/reduce_scatter | solution.py:191
  13.6 3.3 copy-start.33
  16.8 47.1 %copy-start.5 = (bf16[512,8,128]{2,0,1:T(8,128)(2,1)}, bf16[512,8,128]{2,0,1:T(8,128)(2,1)S(1)}, u32[]{:S(2)}) copy-start(bf16[512,8,128]{2,0,1:T(8,128)(2,1)S(1)} %copy.52) | copy-start | bytes 3145732
  101.3 76.3 %collective-permute-start = (bf16[1032,128]{1,0:T(8,128)(2,1)}, bf16[1032,128]{1,0:T(8,128)(2,1)}, u32[]{:S(2)}, u32[]{:S(2)}) collective-permute-start(bf16[1032,128]{1,0:T(8,128)(2,1)} %concatenate.48), channel_id=1, source_target_pairs={{0,4},{4,8},{8,12},{12,16},{16,20},{20,24},{24,28},{1,5},{5,9},{9,... | collective-permute-start | bytes 792584 | tf_op jit(solution)/shard_map/ppermute | solution.py:177
  104.7 80.9 %collective-permute-start.1 = (bf16[1032,128]{1,0:T(8,128)(2,1)}, bf16[1032,128]{1,0:T(8,128)(2,1)}, u32[]{:S(2)}, u32[]{:S(2)}) collective-permute-start(bf16[1032,128]{1,0:T(8,128)(2,1)} %concatenate.48), channel_id=1, source_target_pairs={{0,8},{4,12},{8,16},{12,20},{16,24},{20,28},{1,9},{5,13},{9,17},{1... | collective-permute-start | bytes 792584 | tf_op jit(solution)/shard_map/ppermute | solution.py:177
  108.2 79.1 %collective-permute-start.2 = (bf16[1032,128]{1,0:T(8,128)(2,1)}, bf16[1032,128]{1,0:T(8,128)(2,1)}, u32[]{:S(2)}, u32[]{:S(2)}) collective-permute-start(bf16[1032,128]{1,0:T(8,128)(2,1)} %concatenate.48), channel_id=1, source_target_pairs={{0,12},{4,16},{8,20},{12,24},{16,28},{1,13},{5,17},{9,21},{13,25},... | collective-permute-start | bytes 792584 | tf_op jit(solution)/shard_map/ppermute | solution.py:177
  110.1 77.8 %collective-permute-start.3 = (bf16[1032,128]{1,0:T(8,128)(2,1)}, bf16[1032,128]{1,0:T(8,128)(2,1)}, u32[]{:S(2)}, u32[]{:S(2)}) collective-permute-start(bf16[1032,128]{1,0:T(8,128)(2,1)} %concatenate.48), channel_id=1, source_target_pairs={{0,16},{4,20},{8,24},{12,28},{1,17},{5,21},{9,25},{13,29},{2,18},{... | collective-permute-start | bytes 792584 | tf_op jit(solution)/shard_map/ppermute | solution.py:177
  115.8 20.3 %copy-start.20 = (pred[512,512]{1,0:T(8,128)(4,1)}, pred[512,512]{1,0:T(8,128)(4,1)S(1)}, u32[]{:S(2)}) copy-start(pred[512,512]{1,0:T(8,128)(4,1)S(1)} %iota_compare_fusion.3) | copy-start | bytes 786436
  115.8 5.0 %copy-start.1 = (f32[8,512,640]{2,1,0:T(8,128)S(1)}, f32[8,512,640]{2,1,0:T(8,128)}, u32[]{:S(2)}) copy-start(f32[8,512,640]{2,1,0:T(8,128)} %fusion.109) | copy-start | bytes 31457284
  115.8 5.0 %copy-start.6 = (bf16[512,8,128]{2,0,1:T(8,128)(2,1)S(1)}, bf16[512,8,128]{2,0,1:T(8,128)(2,1)}, u32[]{:S(2)}) copy-start(bf16[512,8,128]{2,0,1:T(8,128)(2,1)} %copy-done.5) | copy-start | bytes 3145732
  120.8 15.3 %copy-start.7 = (bf16[512,8,128]{2,0,1:T(8,128)(2,1)S(1)}, bf16[512,8,128]{2,0,1:T(8,128)(2,1)}, u32[]{:S(2)}) copy-start(bf16[512,8,128]{2,0,1:T(8,128)(2,1)} %copy.55) | copy-start | bytes 3145732
  163.3 9.2 %copy-start.8 = (bf16[512,1024]{0,1:T(8,128)(2,1)S(1)}, bf16[512,1024]{0,1:T(8,128)(2,1)}, u32[]{:S(2)}) copy-start(bf16[512,1024]{0,1:T(8,128)(2,1)} %copy.39) | copy-start | bytes 3145732
  169.3 3.3 copy-start
  175.7 60.1 %collective-permute-start.7 = (bf16[8,512,128]{2,1,0:T(8,128)(2,1)}, bf16[8,512,128]{2,1,0:T(8,128)(2,1)}, u32[]{:S(2)}, u32[]{:S(2)}) collective-permute-start(bf16[8,512,128]{2,1,0:T(8,128)(2,1)} %subtract_convert_fusion), channel_id=1, source_target_pairs={{0,4},{4,8},{8,12},{12,16},{16,20},{20,24},{24,28},{1,5},{5,9},{9,... | collective-permute-start | bytes 3145736 | tf_op jit(solution)/shard_map/ppermute | solution.py:176
  177.6 59.9 %collective-permute-start.8 = (bf16[8,512,128]{2,1,0:T(8,128)(2,1)}, bf16[8,512,128]{2,1,0:T(8,128)(2,1)}, u32[]{:S(2)}, u32[]{:S(2)}) collective-permute-start(bf16[8,512,128]{2,1,0:T(8,128)(2,1)} %subtract_convert_fusion), channel_id=1, source_target_pairs={{0,8},{4,12},{8,16},{12,20},{16,24},{20,28},{1,9},{5,13},{9,17},{1... | collective-permute-start | bytes 3145736 | tf_op jit(solution)/shard_map/ppermute | solution.py:176
  185.6 11.2 %collective-permute-start.4 = (bf16[1032,128]{1,0:T(8,128)(2,1)}, bf16[1032,128]{1,0:T(8,128)(2,1)S(1)}, u32[]{:S(2)}, u32[]{:S(2)}) collective-permute-start(bf16[1032,128]{1,0:T(8,128)(2,1)} %concatenate.48), channel_id=1, source_target_pairs={{0,20},{4,24},{8,28},{1,21},{5,25},{9,29},{2,22},{6,26},{10,30},{3... | collective-permute-start | bytes 792584 | tf_op jit(solution)/shard_map/ppermute | solution.py:177
  187.3 45.5 %collective-permute-start.5 = (bf16[1032,128]{1,0:T(8,128)(2,1)}, bf16[1032,128]{1,0:T(8,128)(2,1)S(1)}, u32[]{:S(2)}, u32[]{:S(2)}) collective-permute-start(bf16[1032,128]{1,0:T(8,128)(2,1)} %concatenate.48), channel_id=1, source_target_pairs={{0,24},{4,28},{1,25},{5,29},{2,26},{6,30},{3,27},{7,31}} | collective-permute-start | bytes 792584 | tf_op jit(solution)/shard_map/ppermute | solution.py:177
  188.0 46.2 %collective-permute-start.6 = (bf16[1032,128]{1,0:T(8,128)(2,1)}, bf16[1032,128]{1,0:T(8,128)(2,1)}, u32[]{:S(2)}, u32[]{:S(2)}) collective-permute-start(bf16[1032,128]{1,0:T(8,128)(2,1)} %concatenate.48), channel_id=1, source_target_pairs={{0,28},{1,29},{2,30},{3,31}} | collective-permute-start | bytes 792584 | tf_op jit(solution)/shard_map/ppermute | solution.py:177
  196.8 87.2 %collective-permute-start.9 = (bf16[8,512,128]{2,1,0:T(8,128)(2,1)}, bf16[8,512,128]{2,1,0:T(8,128)(2,1)}, u32[]{:S(2)}, u32[]{:S(2)}) collective-permute-start(bf16[8,512,128]{2,1,0:T(8,128)(2,1)} %subtract_convert_fusion), channel_id=1, source_target_pairs={{0,12},{4,16},{8,20},{12,24},{16,28},{1,13},{5,17},{9,21},{13,25},... | collective-permute-start | bytes 3145736 | tf_op jit(solution)/shard_map/ppermute | solution.py:176
  232.8 63.3 %collective-permute-start.10 = (bf16[8,512,128]{2,1,0:T(8,128)(2,1)}, bf16[8,512,128]{2,1,0:T(8,128)(2,1)}, u32[]{:S(2)}, u32[]{:S(2)}) collective-permute-start(bf16[8,512,128]{2,1,0:T(8,128)(2,1)} %subtract_convert_fusion), channel_id=1, source_target_pairs={{0,16},{4,20},{8,24},{12,28},{1,17},{5,21},{9,25},{13,29},{2,18},{... | collective-permute-start | bytes 3145736 | tf_op jit(solution)/shard_map/ppermute | solution.py:176
  234.1 74.0 %collective-permute-start.11 = (bf16[8,512,128]{2,1,0:T(8,128)(2,1)}, bf16[8,512,128]{2,1,0:T(8,128)(2,1)}, u32[]{:S(2)}, u32[]{:S(2)}) collective-permute-start(bf16[8,512,128]{2,1,0:T(8,128)(2,1)} %subtract_convert_fusion), channel_id=1, source_target_pairs={{0,20},{4,24},{8,28},{1,21},{5,25},{9,29},{2,22},{6,26},{10,30},{3... | collective-permute-start | bytes 3145736 | tf_op jit(solution)/shard_map/ppermute | solution.py:176
  235.8 72.5 %collective-permute-start.12 = (bf16[8,512,128]{2,1,0:T(8,128)(2,1)}, bf16[8,512,128]{2,1,0:T(8,128)(2,1)}, u32[]{:S(2)}, u32[]{:S(2)}) collective-permute-start(bf16[8,512,128]{2,1,0:T(8,128)(2,1)} %subtract_convert_fusion), channel_id=1, source_target_pairs={{0,24},{4,28},{1,25},{5,29},{2,26},{6,30},{3,27},{7,31}} | collective-permute-start | bytes 3145736 | tf_op jit(solution)/shard_map/ppermute | solution.py:176
  237.5 77.5 %collective-permute-start.13 = (bf16[8,512,128]{2,1,0:T(8,128)(2,1)}, bf16[8,512,128]{2,1,0:T(8,128)(2,1)}, u32[]{:S(2)}, u32[]{:S(2)}) collective-permute-start(bf16[8,512,128]{2,1,0:T(8,128)(2,1)} %subtract_convert_fusion), channel_id=1, source_target_pairs={{0,28},{1,29},{2,30},{3,31}} | collective-permute-start | bytes 3145736 | tf_op jit(solution)/shard_map/ppermute | solution.py:176
  (20 other events, 37.9 us)
Sparse Core Ops, SparseCore 0:
  10.1 128.7 all-gather.1
  332.1 122.5 reduce-scatter.1
where the time goes:
time: 467 us; the launch traced here: 462 us
  matrix products  177 us (38%)
  waiting for transfers between devices  123 us (26%)
  starting transfers between devices  59 us (13%)
  local copies, waits for them, and re-layouts  42.2 us (9%)
  other arithmetic  24.1 us (5%)
  between operations  22.9 us (5%)
  loops' own time  13.3 us (3%)
    reduce_scatter x1, waiting for transfers between devices, on_device(): lax.psum_scatter(jnp.dot(token_rows, out_weight, preferred_element_type=j...  123 us
    ppermute x7, starting transfers between devices, on_device(): key_pair = lax.ppermute(keys_end, 'ctx', pairs)  46.1 us
    dot_general x1, matrix products, lower_solve(): return jnp.dot(unit_lower_inverse(strict_lower), right, precision=highest)  24.4 us
    dot_general x1, matrix products, shard_operators(): jnp.dot(scaled_dots, key_solve, precision=highest)  18.7 us
    dot_general x1, matrix products, shard_operators(): jnp.dot(key_solve.T, weighted, precision=highest)  15.3 us
    dot_general x4, matrix products, attend(): jnp.einsum('hqk,hdk->hqd', weights.astype(jnp.bfloat16), value_pair, pref...  13.7 us
    another operation x7, loops' own time, on_device(): lax.cond(is_live, lambda inner, k=key_pair, v=value_pair, t=transfer_in,...  13.3 us
    ppermute x7, starting transfers between devices, on_device(): meta_in = lax.ppermute(meta_rows, 'ctx', pairs).astype(jnp.float32)  12.8 us
  transfers between devices with their start and end apart: 16, of which 1 were waited for; matrix products, arithmetic and copies ran while one was open for 47% of the time, Pallas kernels for 0%

commit v1 on v0

--- a/solution.py
+++ b/solution.py
@@ -170,15 +170,16 @@
         [transfer.reshape(head_count * head_width, head_width), doc_rows], axis=0
     ).astype(jnp.bfloat16)
     first_doc = doc_float[0]
+    every_key = lax.all_gather(keys_end, "ctx", axis=1, tiled=True)
     is_live = jnp.bool_(True)
     for offset in range(1, ctx_count):
         pairs = [(s, s + offset) for s in range(ctx_count - offset)]
-        key_pair = lax.ppermute(keys_end, "ctx", pairs)
         meta_in = lax.ppermute(meta_rows, "ctx", pairs).astype(jnp.float32)
         transfer_in = meta_in[: head_count * head_width].reshape(head_count, head_width, head_width)
         key_docs = meta_in[head_count * head_width :].reshape(-1)[:block_rows]
         source = jnp.maximum(ctx_index - offset, 0)
         value_pair = lax.dynamic_slice_in_dim(every_value, source * block_rows, block_rows, 2)
+        key_pair = lax.dynamic_slice_in_dim(every_key, source * block_rows, block_rows, 1)
         is_live = is_live & (ctx_index - offset >= 0) & (key_docs[block_rows - 1] == first_doc)
         carried = lax.cond(
             is_live,

time: 467 us -> 430 us (0.921)
  starting transfers between devices: 59 us -> 11.8 us
  local copies, waits for them, and re-layouts: 42.2 us -> 51.4 us
  waiting for transfers between devices: 123 us -> 132 us
    reduce_scatter x1, waiting for transfers between devices: 123 us -> 43.7 us  [on_device(): lax.psum_scatter(jnp.dot(token_rows, out_weight, preferred_element_type=j...]
    all_gather x0 -> x1, waiting for transfers between devices: none -> 63.5 us  [on_device(): every_key = lax.all_gather(keys_end, 'ctx', axis=1, tiled=True)]
    ppermute x7 -> x0, starting transfers between devices: 46.1 us -> none  [on_device(): key_pair = lax.ppermute(keys_end, 'ctx', pairs)]
    all_gather x1, waiting for transfers between devices: 0.01 us -> 24.6 us  [on_device(): every_value = lax.all_gather(value_columns, 'ctx', axis=2, tiled=True)]
    dot_general x4, matrix products: 11.3 us -> 6.38 us  [attend(): jnp.einsum('hqd,hkd->hqk', turned.astype(jnp.bfloat16), key_pair, preferr...]
    cond x40 -> x48, local copies, waits for them, and re-layouts: 6.1 us -> 10.7 us
    unnamed x28 -> x26, local copies, waits for them, and re-layouts: 9.55 us -> 8.1 us
  transfers between devices with their start and end apart: 16 -> 10, of which waited for: 1 -> 3; matrix products, arithmetic and copies ran while one was open for 47% -> 43% of each run, Pallas kernels for 0% -> 0%
where the time goes in v1:
time: 430 us; the launch traced here: 425 us
  matrix products  175 us (41%)
  waiting for transfers between devices  132 us (31%)
  local copies, waits for them, and re-layouts  51.4 us (12%)
  between operations  23.2 us (5%)
  other arithmetic  20.8 us (5%)
  starting transfers between devices  11.8 us (3%)
  loops' own time  11.1 us (3%)
    all_gather x1, waiting for transfers between devices, on_device(): every_key = lax.all_gather(keys_end, 'ctx', axis=1, tiled=True)  63.5 us
    reduce_scatter x1, waiting for transfers between devices, on_device(): lax.psum_scatter(jnp.dot(token_rows, out_weight, preferred_element_type=j...  43.7 us
    all_gather x1, waiting for transfers between devices, on_device(): every_value = lax.all_gather(value_columns, 'ctx', axis=2, tiled=True)  24.6 us
    dot_general x1, matrix products, lower_solve(): return jnp.dot(unit_lower_inverse(strict_lower), right, precision=highest)  24.5 us
    dot_general x1, matrix products, shard_operators(): jnp.dot(scaled_dots, key_solve, precision=highest)  18.7 us
    dot_general x1, matrix products, shard_operators(): jnp.dot(key_solve.T, weighted, precision=highest)  17 us
    dot_general x4, matrix products, attend(): jnp.einsum('hqk,hdk->hqd', weights.astype(jnp.bfloat16), value_pair, pref...  13.7 us
    ppermute x7, starting transfers between devices, on_device(): meta_in = lax.ppermute(meta_rows, 'ctx', pairs).astype(jnp.float32)  11.5 us
  transfers between devices with their start and end apart: 10, of which 3 were waited for; matrix products, arithmetic and copies ran while one was open for 43% of the time, Pallas kernels for 0%

profile of v1, /device:TPU:16, one launch (start us, length us, event | category | flops | bytes accessed | tf_op | source)
XLA Modules:
  0.0 425.1 jit_solution(17200153514316921172)
XLA Ops:
  18.1 7.3 %multiply_select_fusion.6 = f32[8,512,512]{2,1,0:T(8,128)S(1)} fusion(f32[8,512]{1,0:T(8,128)S(1)} %multiply_bitcast_fusion, pred[512,512]{1,0:T(8,128)(4,1)S(1)} %iota_compare_fusion.4, f32[8,512,128]{2,1,0:T(8,128)S(1)} %broadcast_divide_fusion), kind=kOutput, calls=%fused_computation.152 | convolution fusion | flops 3225419776 | bytes 10764288 | tf_op jit(solution)/shard_map/vmap()/dot_general | solution.py:79
  63.6 6.1 %broadcast_select_fusion = f32[8,512,512]{2,1,0:T(8,128)} fusion(pred[512,512]{1,0:T(8,128)(4,1)S(1)} %iota_compare_fusion.4, f32[8,512,128]{2,1,0:T(8,128)S(1)} %broadcast_divide_fusion, bf16[512,8,128]{2,0,1:T(8,128)(2,1)S(1)} %copy.52), kind=kOutput, calls=%fused_computation.167 | convolution fusion | flops 3223322624 | bytes 11796480 | tf_op jit(solution)/shard_map/vmap()/dot_general | solution.py:81
  69.6 24.5 %fusion.113 = f32[8,512,640]{2,1,0:T(8,128)} fusion(f32[8,512,128]{2,1,0:T(8,128)S(1)} %broadcast_divide_fusion, f32[8,512,512]{2,1,0:T(8,128)} %broadcast_select_fusion, f32[8,256,256]{2,1,0:T(8,128)S(1)} %select_maximum_fusion.2, f32[8,128,128]{2,1,0:T(8,128)} %copy-done.29, f32[8,128,128]{2,1,0:T(8,128)S(1)} %convolution_negate_fusion, ...), kind=kOutput, calls=%fused_computation.134 | convolution fusion | flops 16121331712 | bytes 27262976 | tf_op jit(solution)/shard_map/vmap()/dot_general | solution.py:70
  94.1 17.0 %subtract_convert_fusion = bf16[8,512,128]{2,1,0:T(8,128)(2,1)} fusion(f32[8,512,128]{2,1,0:T(8,128)S(1)} %broadcast_divide_fusion, f32[8,512,640]{2,1,0:T(8,128)} %fusion.113, bf16[512,8,128]{2,0,1:T(8,128)(2,1)S(1)} %copy.52, f32[8,512]{1,0:T(8,128)S(1)} %multiply_bitcast_fusion), kind=kOutput, calls=%fused_computation.199 | convolution fusion | flops 3223322624 | bytes 12599296 | tf_op jit(solution)/shard_map/vmap()/dot_general | solution.py:86
  111.2 24.6 %all-gather.3.cloned.1.call-done = bf16[8,128,4096]{2,1,0:T(8,128)(2,1)} async-done(((bf16[8,128,512]{2,1,0:T(8,128)(2,1)}), bf16[8,128,4096]{2,1,0:T(8,128)(2,1)}) %all-gather.3.cloned.1.call-update) | async-done | bytes 8388624 | tf_op jit(solution)/shard_map/all_gather | solution.py:120
  136.0 5.6 %fusion.193 = bf16[8,128,128]{2,1,0:T(8,128)(2,1)S(1)} fusion(f32[8,512,128]{2,1,0:T(8,128)S(1)} %broadcast_divide_fusion, f32[8,512,640]{2,1,0:T(8,128)} %fusion.113, f32[8,512]{1,0:T(8,128)S(1)} %multiply_bitcast_fusion, f32[128,128]{1,0:T(8,128)S(1)} %get-tuple-element.550), kind=kOutput, calls=%fused_computation.219 | convolution fusion | flops 806092800 | bytes 4538368 | tf_op jit(solution)/shard_map/vmap()/dot_general | solution.py:87
  158.3 4.8 %fusion.197 = f32[8,512,512]{1,2,0:T(8,128)S(1)} fusion(f32[8,512,128]{2,1,0:T(8,128)S(1)} %broadcast_divide_fusion, bf16[512,8,128]{2,0,1:T(8,128)(2,1)} %copy.55), kind=kOutput, calls=%fused_computation.221 | convolution fusion | flops 3221225472 | bytes 11534336 | tf_op jit(solution)/shard_map/vmap()/dot_general | solution.py:90
  163.2 18.7 %fusion.128 = f32[8,512,512]{1,2,0:T(8,128)} fusion(f32[8,512,640]{2,1,0:T(8,128)} %fusion.113, f32[8,512,512]{1,2,0:T(8,128)S(1)} %fusion.197, f32[8,512]{1,0:T(8,128)S(1)} %multiply_bitcast_fusion, pred[512,512]{1,0:T(8,128)(4,1)S(1)} %iota_compare_fusion.3), kind=kOutput, calls=%fused_computation.155 | convolution fusion | flops 12889096192 | bytes 25444352 | tf_op jit(solution)/shard_map/vmap()/dot_general | solution.py:92
  181.8 5.4 %fusion.220 = (f32[8,512]{1,0:T(8,128)S(1)}, f32[8,512,512]{1,2,0:T(8,128)S(1)}) fusion(f32[8,512,512]{1,2,0:T(8,128)} %fusion.128, bf16[512,8,128]{2,0,1:T(8,128)(2,1)S(1)} %copy.52, bf16[512,8,128]{2,0,1:T(8,128)(2,1)S(1)} %copy-done.2, pred[512,512]{0,1:T(8,128)(4,1)S(1)} %copy-done.30), kind=kOutput, calls=%fused_computation.325 | convolution fusion | flops 545255424 | bytes 19152896 | tf_op jit(solution)/shard_map/vmap()/dot_general | solution.py:92
  190.5 9.6 %convert_subtract_fusion = f32[8,512,128]{2,1,0:T(8,128)S(1)} fusion(f32[8,512,640]{2,1,0:T(8,128)} %fusion.113, f32[8,512,512]{1,2,0:T(8,128)S(1)} %fusion.197, f32[8,512]{1,0:T(8,128)S(1)} %multiply_bitcast_fusion, pred[512,512]{1,0:T(8,128)(4,1)S(1)} %iota_compare_fusion.3, bf16[512,8,128]{2,0,1:T(8,128)(2,1)S(1)} %copy-done.3), kind=kOutput, calls=%fused_computation.201 | convolution fusion | flops 3226468352 | bytes 13910016 | tf_op jit(solution)/shard_map/vmap()/dot_general | solution.py:95
  231.9 4.9 %constant_dynamic-slice_fusion = (bf16[8,128,512]{2,1,0:T(8,128)(2,1)}, bf16[8,128,512]{2,1,0:T(8,128)(2,1)}, bf16[8,128,512]{2,1,0:T(8,128)(2,1)}, bf16[8,128,512]{2,1,0:T(8,128)(2,1)}, bf16[8,128,512]{2,1,0:T(8,128)(2,1)}) fusion(bf16[8,128,4096]{2,1,0:T(8,128)(2,1)} %all-gather.3.cloned.1.call-done, s32[]{:T(128)S(6)} %select_n.294, s32[]{:T(128)S(6)} %select_n.293, ...), kind=kLoop, calls=%fused_computation.258 | loop fusion | bytes 10485780 | tf_op jit(solution)/shard_map/dynamic_slice | solution.py:181
  236.9 63.5 %all-gather.5.cloned.1.call-done = bf16[8,4096,128]{2,1,0:T(8,128)(2,1)} async-done(((bf16[8,512,128]{2,1,0:T(8,128)(2,1)}), bf16[8,4096,128]{2,1,0:T(8,128)(2,1)}) %all-gather.5.cloned.1.call-update) | async-done | bytes 8388624 | tf_op jit(solution)/shard_map/all_gather | solution.py:173
  300.4 4.7 %constant_dynamic-slice_fusion.1 = (bf16[8,512,128]{2,1,0:T(8,128)(2,1)S(1)}, bf16[8,512,128]{2,1,0:T(8,128)(2,1)}, bf16[8,512,128]{2,1,0:T(8,128)(2,1)}, bf16[8,512,128]{2,1,0:T(8,128)(2,1)}, bf16[8,512,128]{2,1,0:T(8,128)(2,1)}) fusion(bf16[8,4096,128]{2,1,0:T(8,128)(2,1)} %all-gather.5.cloned.1.call-done, s32[]{:T(128)S(6)} %select_n.294, ...), kind=kLoop, calls=%fused_computation.259 | loop fusion | bytes 10485780 | tf_op jit(solution)/shard_map/dynamic_slice | solution.py:182
  305.1 11.7 %conditional.7 = ((f32[8,512,128]{2,1,0:T(8,128)S(1)}, f32[8,512]{1,0:T(8,128)S(1)}, f32[8,512]{1,0:T(8,128)S(1)}, f32[8,512,128]{2,1,0:T(8,128)})) conditional(s32[]{:T(128)} %convert_element_type.160, (f32[8,512,128]{2,1,0:T(8,128)S(1)}, f32[8,512]{1,0:T(8,128)S(1)}, f32[8,512]{1,0:T(8,128)S(1)}, f32[8,512,128]{2,1,0:T(8,128)}) %tuple.66, ...), branch_computations={%region_3.4_spmd, %region_4.7_spmd} | conditional | flops 1903960064 | bytes 71045296 | solution.py:184
  311.9 3.4 multiply_add_fusion
  316.8 12.1 %conditional.8 = ((f32[8,512,128]{2,1,0:T(8,128)S(1)}, f32[8,512]{1,0:T(8,128)S(1)}, f32[8,512]{1,0:T(8,128)S(1)}, f32[8,512,128]{2,1,0:T(8,128)})) conditional(s32[]{:T(128)} %convert_element_type.159, (f32[8,512,128]{2,1,0:T(8,128)S(1)}, f32[8,512]{1,0:T(8,128)S(1)}, f32[8,512]{1,0:T(8,128)S(1)}, f32[8,512,128]{2,1,0:T(8,128)}) %get-tuple-element.604, ...), branch_computations={%region_7.8_spmd, %region_8.11_spmd} | conditional | flops 1903960064 | bytes 71045296 | solution.py:184
  323.7 3.4 multiply_add_fusion.2
  328.9 11.7 %conditional.9 = ((f32[8,512,128]{2,1,0:T(8,128)S(1)}, f32[8,512]{1,0:T(8,128)S(1)}, f32[8,512]{1,0:T(8,128)S(1)}, f32[8,512,128]{2,1,0:T(8,128)})) conditional(s32[]{:T(128)} %convert_element_type.158, (f32[8,512,128]{2,1,0:T(8,128)S(1)}, f32[8,512]{1,0:T(8,128)S(1)}, f32[8,512]{1,0:T(8,128)S(1)}, ...), branch_computations={%region_11.12_spmd, %region_12.15_spmd} | conditional | flops 1903960064 | bytes 71045296 | solution.py:184
  335.8 3.4 multiply_add_fusion.4
  340.6 11.9 %conditional.10 = ((f32[8,512,128]{2,1,0:T(8,128)S(1)}, f32[8,512]{1,0:T(8,128)S(1)}, f32[8,512]{1,0:T(8,128)S(1)}, f32[8,512,128]{2,1,0:T(8,128)})) conditional(s32[]{:T(128)} %convert_element_type.157, (f32[8,512,128]{2,1,0:T(8,128)S(1)}, f32[8,512]{1,0:T(8,128)S(1)}, f32[8,512]{1,0:T(8,128)S(1)}, ...), branch_computations={%region_15.16_spmd, %region_16.19_spmd} | conditional | flops 1903960064 | bytes 71045296 | solution.py:184
  352.7 5.7 %conditional.12 = ((f32[8,512,128]{2,1,0:T(8,128)S(1)}, f32[8,512]{1,0:T(8,128)S(1)}, f32[8,512]{1,0:T(8,128)S(1)}, f32[8,512,128]{2,1,0:T(8,128)})) conditional(s32[]{:T(128)} %convert_element_type.155, (f32[8,512,128]{2,1,0:T(8,128)S(1)}, f32[8,512]{1,0:T(8,128)S(1)}, f32[8,512]{1,0:T(8,128)S(1)}, ...), branch_computations={%region_23.24_spmd, %region_24.27_spmd} | conditional | flops 1903960064 | bytes 72110296 | solution.py:184
  358.4 6.1 %conditional.13 = (f32[8,512]{1,0:T(8,128)S(1)}, f32[8,512,128]{1,2,0:T(8,128)S(1)}) conditional(s32[]{:T(128)} %convert_element_type.154, (f32[8,512]{1,0:T(8,128)S(1)}, f32[8,512,128]{2,1,0:T(8,128)}) %tuple.74, (f32[512]{0:T(512)S(1)}, f32[512]{0:T(512)S(1)}, s32[]{:T(128)}, bf16[8,4096,128]{2,1,0:T(8,128)(2,1)}, f32[8,512,128]{2,1,0:T(8,128)S(1)}, ...), branch_computations={%region_27.28_spmd, %region_28.31_spmd} | conditional | flops 1098653696 | bytes 47419504 | solution.py:184
  364.8 9.5 %convolution_convert_fusion = bf16[512,4096]{1,0:T(8,128)(2,1)} fusion(bf16[512,1024]{0,1:T(8,128)(2,1)S(1)} %bitcast.179, bf16[1024,4096]{1,0:T(8,128)(2,1)} %param.27), kind=kOutput, calls=%fused_computation.160 | convolution fusion | flops 4297064448 | bytes 13631488 | tf_op jit(solution)/shard_map/dot_general | solution.py:193
  374.3 43.7 %reduce-scatter.2.cloned.1.call-done = bf16[128,4096]{1,0:T(8,128)(2,1)} async-done(((bf16[512,4096]{1,0:T(8,128)(2,1)}), bf16[128,4096]{1,0:T(8,128)(2,1)}) %reduce-scatter.2.cloned.1.call-update) | async-done | bytes 1048592 | tf_op jit(solution)/shard_map/reduce_scatter | solution.py:192
  (200 shorter events, 130.8 us)
Async XLA Ops:
  6.5 2.4 copy-start.36
  6.5 129.2 %all-gather.3.cloned.1.call-start = ((), (), s32[]{:S(2)}) async-start(), calls=%async_computation.1 | async-start | bytes 9437184 | tf_op jit(solution)/shard_map/all_gather | solution.py:120
  10.0 4.8 %copy-start = (f32[512,8,128]{2,0,1:T(8,128)}, f32[512,8,128]{2,0,1:T(8,128)S(1)}, u32[]{:S(2)}) copy-start(f32[512,8,128]{2,0,1:T(8,128)S(1)} %copy.41) | copy-start | bytes 6291460
  10.0 290.4 %all-gather.5.cloned.1.call-start = ((), (), s32[]{:S(2)}) async-start(), calls=%async_computation.2 | async-start | bytes 9437184 | tf_op jit(solution)/shard_map/all_gather | solution.py:173
  12.9 2.9 copy-start.38
  54.3 7.0 %copy-start.29 = (f32[8,128,128]{2,1,0:T(8,128)}, f32[8,128,128]{2,1,0:T(8,128)S(1)}, u32[]{:S(2)}) copy-start(f32[8,128,128]{2,1,0:T(8,128)S(1)} %get-tuple-element.529) | copy-start | bytes 1572868
  94.1 41.9 %copy-start.39 = (s32[512]{0:T(512)S(1)}, s32[512]{0:T(512)}, u32[]{:S(2)}) copy-start(s32[512]{0:T(512)} %param.26) | copy-start | bytes 6148
  135.7 282.3 %reduce-scatter.2.cloned.1.call-start = ((), (), s32[]{:S(2)}) async-start(), calls=%async_computation.3 | async-start | bytes 5242880 | tf_op jit(solution)/shard_map/reduce_scatter | solution.py:192
  143.0 59.0 %collective-permute-start = (bf16[1032,128]{1,0:T(8,128)(2,1)}, bf16[1032,128]{1,0:T(8,128)(2,1)}, u32[]{:S(2)}, u32[]{:S(2)}) collective-permute-start(bf16[1032,128]{1,0:T(8,128)(2,1)} %concatenate.48), channel_id=1, source_target_pairs={{0,4},{4,8},{8,12},{12,16},{16,20},{20,24},{24,28},{1,5},{5,9},{9,... | collective-permute-start | bytes 792584 | tf_op jit(solution)/shard_map/ppermute | solution.py:177
  145.5 58.2 %collective-permute-start.1 = (bf16[1032,128]{1,0:T(8,128)(2,1)}, bf16[1032,128]{1,0:T(8,128)(2,1)}, u32[]{:S(2)}, u32[]{:S(2)}) collective-permute-start(bf16[1032,128]{1,0:T(8,128)(2,1)} %concatenate.48), channel_id=1, source_target_pairs={{0,8},{4,12},{8,16},{12,20},{16,24},{20,28},{1,9},{5,13},{9,17},{1... | collective-permute-start | bytes 792584 | tf_op jit(solution)/shard_map/ppermute | solution.py:177
  147.9 58.2 %collective-permute-start.2 = (bf16[1032,128]{1,0:T(8,128)(2,1)}, bf16[1032,128]{1,0:T(8,128)(2,1)}, u32[]{:S(2)}, u32[]{:S(2)}) collective-permute-start(bf16[1032,128]{1,0:T(8,128)(2,1)} %concatenate.48), channel_id=1, source_target_pairs={{0,12},{4,16},{8,20},{12,24},{16,28},{1,13},{5,17},{9,21},{13,25},... | collective-permute-start | bytes 792584 | tf_op jit(solution)/shard_map/ppermute | solution.py:177
  149.8 57.3 %collective-permute-start.3 = (bf16[1032,128]{1,0:T(8,128)(2,1)}, bf16[1032,128]{1,0:T(8,128)(2,1)}, u32[]{:S(2)}, u32[]{:S(2)}) collective-permute-start(bf16[1032,128]{1,0:T(8,128)(2,1)} %concatenate.48), channel_id=1, source_target_pairs={{0,16},{4,20},{8,24},{12,28},{1,17},{5,21},{9,25},{13,29},{2,18},{... | collective-permute-start | bytes 792584 | tf_op jit(solution)/shard_map/ppermute | solution.py:177
  151.1 57.0 %collective-permute-start.4 = (bf16[1032,128]{1,0:T(8,128)(2,1)}, bf16[1032,128]{1,0:T(8,128)(2,1)}, u32[]{:S(2)}, u32[]{:S(2)}) collective-permute-start(bf16[1032,128]{1,0:T(8,128)(2,1)} %concatenate.48), channel_id=1, source_target_pairs={{0,20},{4,24},{8,28},{1,21},{5,25},{9,29},{2,22},{6,26},{10,30},{3... | collective-permute-start | bytes 792584 | tf_op jit(solution)/shard_map/ppermute | solution.py:177
  163.1 18.7 %copy-start.2 = (bf16[512,8,128]{2,0,1:T(8,128)(2,1)S(1)}, bf16[512,8,128]{2,0,1:T(8,128)(2,1)}, u32[]{:S(2)}) copy-start(bf16[512,8,128]{2,0,1:T(8,128)(2,1)} %copy.55) | copy-start | bytes 3145732
  163.1 18.7 %copy-start.30 = (pred[512,512]{0,1:T(8,128)(4,1)S(1)}, pred[512,512]{0,1:T(8,128)(4,1)}, u32[]{:S(2)}) copy-start(pred[512,512]{0,1:T(8,128)(4,1)} %copy.57) | copy-start | bytes 786436
  181.8 5.4 %copy-start.4 = (bf16[512,1024]{0,1:T(8,128)(2,1)S(1)}, bf16[512,1024]{0,1:T(8,128)(2,1)}, u32[]{:S(2)}) copy-start(bf16[512,1024]{0,1:T(8,128)(2,1)} %copy.39) | copy-start | bytes 3145732
  187.2 3.2 copy-start.3
  200.1 1.9 copy-start.37
  202.0 16.4 %collective-permute-start.5 = (bf16[1032,128]{1,0:T(8,128)(2,1)S(1)}, bf16[1032,128]{1,0:T(8,128)(2,1)S(1)}, u32[]{:S(2)}, u32[]{:S(2)}) collective-permute-start(bf16[1032,128]{1,0:T(8,128)(2,1)S(1)} %copy-done.37), channel_id=1, source_target_pairs={{0,24},{4,28},{1,25},{5,29},{2,26},{6,30},{3,27},{7,31}} | collective-permute-start | bytes 792584 | tf_op jit(solution)/shard_map/ppermute | solution.py:177
  203.7 16.7 %collective-permute-start.6 = (bf16[1032,128]{1,0:T(8,128)(2,1)S(1)}, bf16[1032,128]{1,0:T(8,128)(2,1)}, u32[]{:S(2)}, u32[]{:S(2)}) collective-permute-start(bf16[1032,128]{1,0:T(8,128)(2,1)S(1)} %copy-done.37), channel_id=1, source_target_pairs={{0,28},{1,29},{2,30},{3,31}} | collective-permute-start | bytes 792584 | tf_op jit(solution)/shard_map/ppermute | solution.py:177
  218.4 11.8 %copy-start.22 = (f32[1032,128]{1,0:T(8,128)}, f32[1032,128]{1,0:T(8,128)S(1)}, u32[]{:S(2)}) copy-start(f32[1032,128]{1,0:T(8,128)S(1)} %convert_element_type.153) | copy-start | bytes 1585156
  310.1 1.8 copy-start.35
  321.8 1.8 copy-start.34
  333.9 1.8 copy-start.33
  (17 other events, 26.0 us)
Sparse Core Ops, SparseCore 0:
  10.1 125.5 all-gather.2
  137.9 162.4 all-gather.4
  374.4 43.5 reduce-scatter.1

commit v2 on v1

--- a/solution.py
+++ b/solution.py
@@ -172,29 +172,57 @@
     first_doc = doc_float[0]
     every_key = lax.all_gather(keys_end, "ctx", axis=1, tiled=True)
     is_live = jnp.bool_(True)
+    steps = []
     for offset in range(1, ctx_count):
         pairs = [(s, s + offset) for s in range(ctx_count - offset)]
         meta_in = lax.ppermute(meta_rows, "ctx", pairs).astype(jnp.float32)
         transfer_in = meta_in[: head_count * head_width].reshape(head_count, head_width, head_width)
         key_docs = meta_in[head_count * head_width :].reshape(-1)[:block_rows]
-        source = jnp.maximum(ctx_index - offset, 0)
-        value_pair = lax.dynamic_slice_in_dim(every_value, source * block_rows, block_rows, 2)
-        key_pair = lax.dynamic_slice_in_dim(every_key, source * block_rows, block_rows, 1)
         is_live = is_live & (ctx_index - offset >= 0) & (key_docs[block_rows - 1] == first_doc)
-        carried = lax.cond(
-            is_live,
-            lambda inner, k=key_pair, v=value_pair, t=transfer_in, d=key_docs: attend(inner, k, v, t, d),
-            lambda inner: inner,
-            carried,
-        )
+        steps.append((offset, transfer_in, key_docs, is_live))
+
+    def chain(index, inner):
+        if index == len(steps):
+            return inner
+        offset, transfer_in, key_docs, step_live = steps[index]
+
+        def take(inner):
+            source = jnp.maximum(ctx_index - offset, 0)
+            value_pair = lax.dynamic_slice_in_dim(every_value, source * block_rows, block_rows, 2)
+            key_pair = lax.dynamic_slice_in_dim(every_key, source * block_rows, block_rows, 1)
+            return chain(index + 1, attend(inner, key_pair, value_pair, transfer_in, key_docs))
+
+        return lax.cond(step_live, take, lambda inner: inner, inner)
+
+    carried = chain(0, carried)
     attended = (carried[3] / carried[2][..., None]).astype(jnp.bfloat16)
     token_rows = jnp.transpose(attended, (1, 0, 2)).reshape(block_rows, head_count * head_width)
-    return lax.psum_scatter(
-        jnp.dot(token_rows, out_weight, preferred_element_type=jnp.float32).astype(jnp.bfloat16),
-        "head",
-        scatter_dimension=0,
-        tiled=True,
-    )
+    projected = jnp.dot(token_rows, out_weight, preferred_element_type=jnp.float32)
+    return scatter_sum(projected).astype(jnp.bfloat16)
+
+
+def scatter_sum(projected):
+    head_count = lax.axis_size("head")
+    if head_count % 2:
+        return lax.psum_scatter(projected, "head", scatter_dimension=0, tiled=True)
+    chips = head_count // 2
+    rows = projected.shape[0] // head_count
+    head_index = lax.axis_index("head")
+    core = head_index % 2
+    chip = head_index // 2
+    grouped = projected.reshape(chips, 2, rows, projected.shape[1])
+    mine = lax.dynamic_index_in_dim(grouped, core, 1, keepdims=False)
+    other = lax.dynamic_index_in_dim(grouped, 1 - core, 1, keepdims=False)
+    partner = [(h, h ^ 1) for h in range(head_count)]
+    chip_sum = mine + lax.ppermute(other.astype(jnp.bfloat16), "head", partner).astype(jnp.float32)
+    total = lax.dynamic_index_in_dim(chip_sum, chip, 0, keepdims=False)
+    for shift in range(1, chips):
+        pairs = [
+            (2 * y + c, 2 * ((y + shift) % chips) + c) for y in range(chips) for c in range(2)
+        ]
+        outgoing = lax.dynamic_index_in_dim(chip_sum, (chip + shift) % chips, 0, keepdims=False)
+        total = total + lax.ppermute(outgoing.astype(jnp.bfloat16), "head", pairs).astype(jnp.float32)
+    return total
 
 
 def solution(mesh):

time: 430 us -> 440 us (1.023)
  local copies, waits for them, and re-layouts: 51.4 us -> 32 us
  matrix products: 175 us -> 192 us
  other arithmetic: 20.8 us -> 34.9 us
  between operations: 23.2 us -> 15.5 us
    reduce_scatter x1 -> x0, waiting for transfers between devices: 43.7 us -> none  [on_device(): lax.psum_scatter(jnp.dot(token_rows, out_weight, preferred_element_type=j...]
    ppermute x0 -> x2, waiting for transfers between devices: none -> 28 us  [the longest x1 23.7 us: scatter_sum(): lax.ppermute(outgoing.astype(jnp.bfloat16), 'head', pairs)]
    cond x49 -> x14, local copies, waits for them, and re-layouts: 12.6 us -> 0.03 us
    ppermute x7, waiting for transfers between devices: 0.02 us -> 11.4 us  [on_device(): meta_in = lax.ppermute(meta_rows, 'ctx', pairs).astype(jnp.float32)]
    dynamic_slice x2 -> x0, local copies, waits for them, and re-layouts: 9.61 us -> none  [the longest x1 4.94 us: on_device(): lax.dynamic_slice_in_dim(every_value, source * block_rows, block_rows, 2)]
    dot_general x4, matrix products: 13.7 us -> 22.8 us  [attend(): jnp.einsum('hqk,hdk->hqd', weights.astype(jnp.bfloat16), value_pair, pref...]
    slice x5 -> x4, local copies, waits for them, and re-layouts: 9.02 us -> 0.14 us  [on_device(): meta_in[:head_count * head_width]]
    unnamed x26 -> x30, local copies, waits for them, and re-layouts: 8.1 us -> 16.6 us
  transfers between devices with their start and end apart: 10 -> 11, of which waited for: 3 -> 5; matrix products, arithmetic and copies ran while one was open for 43% -> 38% of each run, Pallas kernels for 0% -> 0%
where the time goes in v2:
time: 440 us; the launch traced here: 437 us
  matrix products  192 us (44%)
  waiting for transfers between devices  136 us (31%)
  other arithmetic  34.9 us (8%)
  local copies, waits for them, and re-layouts  32 us (7%)
  between operations  15.5 us (4%)
  starting transfers between devices  13.8 us (3%)
  loops' own time  13 us (3%)
    all_gather x1, waiting for transfers between devices, on_device(): every_key = lax.all_gather(keys_end, 'ctx', axis=1, tiled=True)  72 us
    dot_general x1, matrix products, lower_solve(): return jnp.dot(unit_lower_inverse(strict_lower), right, precision=highest)  24.5 us
    all_gather x1, waiting for transfers between devices, on_device(): every_value = lax.all_gather(value_columns, 'ctx', axis=2, tiled=True)  24.2 us
    ppermute x1, waiting for transfers between devices, scatter_sum(): lax.ppermute(outgoing.astype(jnp.bfloat16), 'head', pairs)  23.7 us
    dot_general x4, matrix products, attend(): jnp.einsum('hqk,hdk->hqd', weights.astype(jnp.bfloat16), value_pair, pref...  22.8 us
    dot_general x1, matrix products, shard_operators(): jnp.dot(scaled_dots, key_solve, precision=highest)  18.3 us
    dot_general x1, matrix products, shard_operators(): jnp.dot(key_solve.T, weighted, precision=highest)  17.2 us
    unnamed x30, local copies, waits for them, and re-layouts  16.6 us
  transfers between devices with their start and end apart: 11, of which 5 were waited for; matrix products, arithmetic and copies ran while one was open for 38% of the time, Pallas kernels for 0%

profile of v2, /device:TPU:16, one launch (start us, length us, event | category | flops | bytes accessed | tf_op | source)
XLA Modules:
  0.0 436.9 jit_solution(1459864181278461923)
XLA Ops:
  18.2 7.3 %multiply_select_fusion.2 = f32[8,512,512]{2,1,0:T(8,128)S(1)} fusion(f32[8,512]{1,0:T(8,128)S(1)} %multiply_bitcast_fusion, pred[512,512]{1,0:T(8,128)(4,1)S(1)} %iota_compare_fusion.4, f32[8,512,128]{2,1,0:T(8,128)S(1)} %broadcast_divide_fusion), kind=kOutput, calls=%fused_computation.181 | convolution fusion | flops 3225419776 | bytes 10764288 | tf_op jit(solution)/shard_map/vmap()/dot_general | solution.py:79
  63.8 6.1 %broadcast_select_fusion = f32[8,512,512]{2,1,0:T(8,128)} fusion(pred[512,512]{1,0:T(8,128)(4,1)S(1)} %iota_compare_fusion.4, f32[8,512,128]{2,1,0:T(8,128)S(1)} %broadcast_divide_fusion, bf16[512,8,128]{2,0,1:T(8,128)(2,1)S(1)} %copy.52), kind=kOutput, calls=%fused_computation.197 | convolution fusion | flops 3223322624 | bytes 11796480 | tf_op jit(solution)/shard_map/vmap()/dot_general | solution.py:81
  69.8 24.5 %fusion.136 = f32[8,512,640]{2,1,0:T(8,128)} fusion(f32[8,512,128]{2,1,0:T(8,128)S(1)} %broadcast_divide_fusion, f32[8,512,512]{2,1,0:T(8,128)} %broadcast_select_fusion, f32[8,256,256]{2,1,0:T(8,128)S(1)} %select_maximum_fusion.2, f32[8,128,128]{2,1,0:T(8,128)} %copy-done.18, f32[8,128,128]{2,1,0:T(8,128)S(1)} %convolution_negate_fusion, ...), kind=kOutput, calls=%fused_computation.161 | convolution fusion | flops 16121331712 | bytes 27262976 | tf_op jit(solution)/shard_map/vmap()/dot_general | solution.py:70
  94.4 17.2 %subtract_convert_fusion = bf16[8,512,128]{2,1,0:T(8,128)(2,1)} fusion(f32[8,512,128]{2,1,0:T(8,128)S(1)} %broadcast_divide_fusion, f32[8,512,640]{2,1,0:T(8,128)} %fusion.136, bf16[512,8,128]{2,0,1:T(8,128)(2,1)S(1)} %copy.52, f32[8,512]{1,0:T(8,128)S(1)} %multiply_bitcast_fusion), kind=kOutput, calls=%fused_computation.233 | convolution fusion | flops 3223322624 | bytes 12599296 | tf_op jit(solution)/shard_map/vmap()/dot_general | solution.py:86
  111.6 24.2 %all-gather.3.cloned.1.call-done = bf16[8,128,4096]{2,1,0:T(8,128)(2,1)} async-done(((bf16[8,128,512]{2,1,0:T(8,128)(2,1)}), bf16[8,128,4096]{2,1,0:T(8,128)(2,1)}) %all-gather.3.cloned.1.call-update) | async-done | bytes 8388624 | tf_op jit(solution)/shard_map/all_gather | solution.py:120
  135.8 5.6 %fusion.216 = bf16[8,128,128]{2,1,0:T(8,128)(2,1)S(1)} fusion(f32[8,512,128]{2,1,0:T(8,128)S(1)} %broadcast_divide_fusion, f32[8,512,640]{2,1,0:T(8,128)} %fusion.136, f32[8,512]{1,0:T(8,128)S(1)} %multiply_bitcast_fusion, f32[128,128]{1,0:T(8,128)S(1)} %get-tuple-element.2191), kind=kOutput, calls=%fused_computation.252 | convolution fusion | flops 806092800 | bytes 4538368 | tf_op jit(solution)/shard_map/vmap()/dot_general | solution.py:87
  155.7 4.9 %fusion.247 = f32[8,512,512]{1,2,0:T(8,128)S(1)} fusion(f32[8,512,128]{2,1,0:T(8,128)S(1)} %broadcast_divide_fusion, bf16[8,512,128]{1,2,0:T(8,128)(2,1)} %bitcast.228), kind=kOutput, calls=%fused_computation.349 | convolution fusion | flops 3221225472 | bytes 11534336 | tf_op jit(solution)/shard_map/vmap()/dot_general | solution.py:90
  163.9 18.3 %fusion.153 = f32[8,512,512]{1,2,0:T(8,128)S(1)} fusion(f32[8,512,640]{2,1,0:T(8,128)} %fusion.136, f32[8,512,512]{1,2,0:T(8,128)S(1)} %fusion.247, f32[8,512]{1,0:T(8,128)S(1)} %multiply_bitcast_fusion, pred[512,512]{1,0:T(8,128)(4,1)S(1)} %iota_compare_fusion.3), kind=kOutput, calls=%fused_computation.184 | convolution fusion | flops 12889096192 | bytes 25444352 | tf_op jit(solution)/shard_map/vmap()/dot_general | solution.py:92
  188.6 10.8 %fusion.157 = f32[8,512,128]{2,1,0:T(8,128)S(1)} fusion(f32[8,512,512]{1,2,0:T(8,128)} %copy-done, f32[8,512]{1,0:T(8,128)S(1)} %multiply_bitcast_fusion, pred[512,512]{1,0:T(8,128)(4,1)S(1)} %iota_compare_fusion.3, f32[8,512,640]{2,1,0:T(8,128)} %fusion.136), kind=kOutput, calls=%fused_computation.188 | convolution fusion | flops 3225419776 | bytes 12861440 | tf_op jit(solution)/shard_map/vmap()/dot_general | solution.py:95
  214.1 11.4 %collective-permute-done.2 = bf16[1032,128]{1,0:T(8,128)(2,1)} collective-permute-done((bf16[1032,128]{1,0:T(8,128)(2,1)}, bf16[1032,128]{1,0:T(8,128)(2,1)}, u32[]{:S(2)}, u32[]{:S(2)}) %collective-permute-start.2) | collective-permute-done | bytes 264224 | tf_op jit(solution)/shard_map/ppermute | solution.py:178
  228.5 72.0 %all-gather.5.cloned.1.call-done = bf16[8,4096,128]{2,1,0:T(8,128)(2,1)} async-done(((bf16[8,512,128]{2,1,0:T(8,128)(2,1)}), bf16[8,4096,128]{2,1,0:T(8,128)(2,1)}) %all-gather.5.cloned.1.call-update) | async-done | bytes 8388624 | tf_op jit(solution)/shard_map/all_gather | solution.py:173
  300.5 77.9 %conditional.7 = ((f32[8,512]{1,0:T(8,128)S(1)}, f32[8,512,128]{2,1,0:T(8,128)})) conditional(s32[]{:T(128)} %convert_element_type.193, (f32[8,512]{1,0:T(8,128)S(1)}, f32[8,512,128]{2,1,0:T(8,128)}) %tuple.93, (pred[]{:T(512)}, f32[512]{0:T(512)S(1)}, f32[512]{0:T(512)S(1)}, f32[8,512,128]{1,2,0:T(8,128)}, f32[8,512,128]{2,1,0:T(8,128)S(1)}, ...), branch_computations={%region_3.4_spmd, %region_4.31_spmd.clone.clone} | conditional | flops 12522938368 | bytes 343537824 | solution.py:195
  310.3 5.7 %multiply_add_fusion.12 = f32[8,512,128]{2,1,0:T(8,128)} fusion(f32[8,512,128]{2,1,0:T(8,128)} %get-tuple-element.1774, f32[8,512,512]{1,2,0:T(8,128)S(1)} %get-tuple-element.2162, f32[8,512]{1,0:T(8,128)S(1)} %max.77, pred[512,512]{0,1:T(8,128)(4,1)S(1)} %broadcast_compare_fusion.6, bf16[8,128,4096]{2,1,0:T(8,128)(2,1)} %get-tuple-element.1775, ...), kind=kOutput, calls=%fused_computation.145 | convolution fusion | flops 546308096 | bytes 13926404 | tf_op jit(solution)/shard_map/cond/branch_1_fun/hqk,hdk->hqd/dot_general | solution.py:156
  319.9 54.9 %conditional.13 = ((f32[8,512]{1,0:T(8,128)S(1)}, f32[8,512,128]{2,1,0:T(8,128)})) conditional(s32[]{:T(128)} %convert_element_type.229, (f32[8,512]{1,0:T(8,128)S(1)}, f32[8,512,128]{2,1,0:T(8,128)}) %tuple.131, (pred[]{:T(512)}, f32[512]{0:T(512)S(1)}, f32[512]{0:T(512)S(1)}, s32[]{:T(128)}, bf16[8,4096,128]{2,1,0:T(8,128)(2,1)}, ...), branch_computations={%region_7.7_spmd, %region_8.30_spmd.clone} | conditional | flops 10617929728 | bytes 284038912 | solution.py:195
  326.6 5.8 %multiply_add_fusion.10 = f32[8,512,128]{2,1,0:T(8,128)} fusion(f32[8,512,128]{2,1,0:T(8,128)} %get-tuple-element.1539, f32[8,512,512]{2,1,0:T(8,128)S(1)} %get-tuple-element.2160, f32[8,512]{1,0:T(8,128)S(1)} %max.73, pred[512,512]{0,1:T(8,128)(4,1)S(1)} %broadcast_compare_fusion.5, bf16[8,128,4096]{2,1,0:T(8,128)(2,1)} %get-tuple-element.2039, ...), kind=kOutput, calls=%fused_computation.122 | convolution fusion | flops 546308096 | bytes 13926404 | tf_op jit(solution)/shard_map/cond/branch_1_fun/cond/branch_1_fun/hqk,hdk->hqd/dot_general | solution.py:156
  336.3 37.2 %conditional.11 = ((f32[8,512]{1,0:T(8,128)S(1)}, f32[8,512,128]{2,1,0:T(8,128)})) conditional(s32[]{:T(128)} %convert_element_type.221, (f32[8,512]{1,0:T(8,128)S(1)}, f32[8,512,128]{2,1,0:T(8,128)}) %tuple.114, (pred[]{:T(512)}, f32[512]{0:T(512)S(1)}, f32[512]{0:T(512)S(1)}, s32[]{:T(128)}, bf16[8,4096,128]{2,1,0:T(8,128)(2,1)}, ...), branch_computations={%region_11.10_spmd, %region_12.29_spmd.clone.clone} | conditional | flops 8713969664 | bytes 232928624 | solution.py:195
  337.8 3.5 fusion.78
  343.1 5.7 %multiply_add_fusion.8 = f32[8,512,128]{2,1,0:T(8,128)} fusion(f32[8,512,128]{2,1,0:T(8,128)} %get-tuple-element.1988, f32[8,512,512]{2,1,0:T(8,128)S(1)} %get-tuple-element.2158, f32[8,512]{1,0:T(8,128)S(1)} %max.85, pred[512,512]{0,1:T(8,128)(4,1)S(1)} %broadcast_compare_fusion.4, bf16[8,128,4096]{2,1,0:T(8,128)(2,1)} %get-tuple-element.2016, ...), kind=kOutput, calls=%fused_computation.99 | convolution fusion | flops 546308096 | bytes 13926404 | tf_op jit(solution)/shard_map/cond/branch_1_fun/cond/branch_1_fun/cond/branch_1_fun/hqk,hdk->hqd/dot_general | solution.py:156
  353.4 19.1 %conditional.17 = ((f32[8,512]{1,0:T(8,128)S(1)}, f32[8,512,128]{2,1,0:T(8,128)})) conditional(s32[]{:T(128)} %convert_element_type.241, (f32[8,512]{1,0:T(8,128)S(1)}, f32[8,512,128]{2,1,0:T(8,128)}) %tuple.148, (pred[]{:T(512)}, f32[512]{0:T(512)S(1)}, f32[512]{0:T(512)S(1)}, s32[]{:T(128)}, bf16[8,4096,128]{2,1,0:T(8,128)(2,1)}, ...), branch_computations={%region_15.13_spmd, %region_16.28_spmd.clone.clone} | conditional | flops 6810009600 | bytes 181818352 | solution.py:195
  355.1 3.5 fusion.59
  360.4 5.7 %multiply_add_fusion.6 = f32[8,512,128]{2,1,0:T(8,128)} fusion(f32[8,512,128]{2,1,0:T(8,128)} %get-tuple-element.1920, f32[8,512,512]{2,1,0:T(8,128)S(1)} %get-tuple-element.2156, f32[8,512]{1,0:T(8,128)S(1)} %max.83, pred[512,512]{0,1:T(8,128)(4,1)S(1)} %broadcast_compare_fusion.3, bf16[8,128,4096]{2,1,0:T(8,128)(2,1)} %get-tuple-element.1946, ...), kind=kOutput, calls=%fused_computation.76 | convolution fusion | flops 546308096 | bytes 13926404 | tf_op jit(solution)/shard_map/cond/branch_1_fun/cond/branch_1_fun/cond/branch_1_fun/cond/branch_1_fun/hqk,hdk->hqd/dot_general | solution.py:156
  381.6 6.9 %fusion.148 = f32[2,2,128,4096]{3,2,1,0:T(8,128)S(1)} fusion(bf16[2,2,128,1024]{3,2,1,0:T(8,128)(2,1)S(1)} %dot_general.204, bf16[1024,4096]{1,0:T(8,128)(2,1)} %param.27), kind=kOutput, calls=%fused_computation.175 | convolution fusion | flops 4294967296 | bytes 17825792 | tf_op jit(solution)/shard_map/dot_general | solution.py:200
  392.2 4.2 collective-permute-done.7
  403.4 23.7 %collective-permute-done.8 = bf16[128,4096]{1,0:T(8,128)(2,1)S(1)} collective-permute-done((bf16[128,4096]{1,0:T(8,128)(2,1)S(1)}, bf16[128,4096]{1,0:T(8,128)(2,1)S(1)}, u32[]{:S(2)}, u32[]{:S(2)}) %collective-permute-start.8) | collective-permute-done | bytes 1048608 | tf_op jit(solution)/shard_map/ppermute | solution.py:224
  (172 shorter events, 142.5 us)
Async XLA Ops:
  6.5 129.2 %all-gather.3.cloned.1.call-start = ((), (), s32[]{:S(2)}) async-start(), calls=%async_computation | async-start | bytes 9437184 | tf_op jit(solution)/shard_map/all_gather | solution.py:120
  10.0 4.8 %copy-start.1 = (f32[512,8,128]{2,0,1:T(8,128)}, f32[512,8,128]{2,0,1:T(8,128)S(1)}, u32[]{:S(2)}) copy-start(f32[512,8,128]{2,0,1:T(8,128)S(1)} %copy.41) | copy-start | bytes 6291460
  10.0 290.5 %all-gather.5.cloned.1.call-start = ((), (), s32[]{:S(2)}) async-start(), calls=%async_computation.1 | async-start | bytes 9437184 | tf_op jit(solution)/shard_map/all_gather | solution.py:173
  54.6 7.0 %copy-start.18 = (f32[8,128,128]{2,1,0:T(8,128)}, f32[8,128,128]{2,1,0:T(8,128)S(1)}, u32[]{:S(2)}) copy-start(f32[8,128,128]{2,1,0:T(8,128)S(1)} %get-tuple-element.2170) | copy-start | bytes 1572868
  94.4 41.4 %copy-start.22 = (s32[512]{0:T(512)S(1)}, s32[512]{0:T(512)}, u32[]{:S(2)}) copy-start(s32[512]{0:T(512)} %param.26) | copy-start | bytes 6148
  142.7 58.2 %collective-permute-start = (bf16[1032,128]{1,0:T(8,128)(2,1)}, bf16[1032,128]{1,0:T(8,128)(2,1)}, u32[]{:S(2)}, u32[]{:S(2)}) collective-permute-start(bf16[1032,128]{1,0:T(8,128)(2,1)} %concatenate.48), channel_id=1, source_target_pairs={{0,4},{4,8},{8,12},{12,16},{16,20},{20,24},{24,28},{1,5},{5,9},{9,... | collective-permute-start | bytes 792584 | tf_op jit(solution)/shard_map/ppermute | solution.py:178
  145.2 58.7 %collective-permute-start.1 = (bf16[1032,128]{1,0:T(8,128)(2,1)}, bf16[1032,128]{1,0:T(8,128)(2,1)}, u32[]{:S(2)}, u32[]{:S(2)}) collective-permute-start(bf16[1032,128]{1,0:T(8,128)(2,1)} %concatenate.48), channel_id=1, source_target_pairs={{0,8},{4,12},{8,16},{12,20},{16,24},{20,28},{1,9},{5,13},{9,17},{1... | collective-permute-start | bytes 792584 | tf_op jit(solution)/shard_map/ppermute | solution.py:178
  147.6 61.1 %collective-permute-start.3 = (bf16[1032,128]{1,0:T(8,128)(2,1)}, bf16[1032,128]{1,0:T(8,128)(2,1)}, u32[]{:S(2)}, u32[]{:S(2)}) collective-permute-start(bf16[1032,128]{1,0:T(8,128)(2,1)} %concatenate.48), channel_id=1, source_target_pairs={{0,16},{4,20},{8,24},{12,28},{1,17},{5,21},{9,25},{13,29},{2,18},{... | collective-permute-start | bytes 792584 | tf_op jit(solution)/shard_map/ppermute | solution.py:178
  148.9 61.6 %collective-permute-start.4 = (bf16[1032,128]{1,0:T(8,128)(2,1)}, bf16[1032,128]{1,0:T(8,128)(2,1)}, u32[]{:S(2)}, u32[]{:S(2)}) collective-permute-start(bf16[1032,128]{1,0:T(8,128)(2,1)} %concatenate.48), channel_id=1, source_target_pairs={{0,20},{4,24},{8,28},{1,21},{5,25},{9,29},{2,22},{6,26},{10,30},{3... | collective-permute-start | bytes 792584 | tf_op jit(solution)/shard_map/ppermute | solution.py:178
  150.3 62.1 %collective-permute-start.5 = (bf16[1032,128]{1,0:T(8,128)(2,1)}, bf16[1032,128]{1,0:T(8,128)(2,1)}, u32[]{:S(2)}, u32[]{:S(2)}) collective-permute-start(bf16[1032,128]{1,0:T(8,128)(2,1)} %concatenate.48), channel_id=1, source_target_pairs={{0,24},{4,28},{1,25},{5,29},{2,26},{6,30},{3,27},{7,31}} | collective-permute-start | bytes 792584 | tf_op jit(solution)/shard_map/ppermute | solution.py:178
  163.9 18.3 %copy-start.8 = (bf16[512,1024]{0,1:T(8,128)(2,1)S(1)}, bf16[512,1024]{0,1:T(8,128)(2,1)}, u32[]{:S(2)}) copy-start(bf16[512,1024]{0,1:T(8,128)(2,1)} %copy.55) | copy-start | bytes 3145732
  163.9 18.3 %copy-start.19 = (pred[512,512]{0,1:T(8,128)(4,1)S(1)}, pred[512,512]{0,1:T(8,128)(4,1)}, u32[]{:S(2)}) copy-start(pred[512,512]{0,1:T(8,128)(4,1)} %copy.54) | copy-start | bytes 786436
  188.6 10.8 %copy-start.9 = (bf16[512,1024]{0,1:T(8,128)(2,1)S(1)}, bf16[512,1024]{0,1:T(8,128)(2,1)}, u32[]{:S(2)}) copy-start(bf16[512,1024]{0,1:T(8,128)(2,1)} %copy.55) | copy-start | bytes 3145732
  201.0 24.6 %collective-permute-start.2 = (bf16[1032,128]{1,0:T(8,128)(2,1)}, bf16[1032,128]{1,0:T(8,128)(2,1)}, u32[]{:S(2)}, u32[]{:S(2)}) collective-permute-start(bf16[1032,128]{1,0:T(8,128)(2,1)} %concatenate.48), channel_id=1, source_target_pairs={{0,12},{4,16},{8,20},{12,24},{16,28},{1,13},{5,17},{9,21},{13,25},... | collective-permute-start | bytes 792584 | tf_op jit(solution)/shard_map/ppermute | solution.py:178
  203.9 22.7 %collective-permute-start.6 = (bf16[1032,128]{1,0:T(8,128)(2,1)}, bf16[1032,128]{1,0:T(8,128)(2,1)}, u32[]{:S(2)}, u32[]{:S(2)}) collective-permute-start(bf16[1032,128]{1,0:T(8,128)(2,1)} %concatenate.48), channel_id=1, source_target_pairs={{0,28},{1,29},{2,30},{3,31}} | collective-permute-start | bytes 792584 | tf_op jit(solution)/shard_map/ppermute | solution.py:178
  310.3 5.7 %copy-start.7 = (f32[8,512,128]{2,1,0:T(8,128)S(1)}, f32[8,512,128]{2,1,0:T(8,128)}, u32[]{:S(2)}) copy-start(f32[8,512,128]{2,1,0:T(8,128)} %copy.89) | copy-start | bytes 6291460 | tf_op jit(solution)/shard_map/cond
  316.0 3.9 copy-start.13
  326.5 5.9 %copy-start.2 = (f32[8,512,128]{2,1,0:T(8,128)S(1)}, f32[8,512,128]{2,1,0:T(8,128)}, u32[]{:S(2)}) copy-start(f32[8,512,128]{2,1,0:T(8,128)} %get-tuple-element.1538) | copy-start | bytes 6291460 | tf_op jit(solution)/shard_map/cond/branch_1_fun/cond
  332.4 3.9 copy-start.14
  343.1 5.7 %copy-start.16 = (f32[1032,128]{1,0:T(8,128)S(1)}, f32[1032,128]{1,0:T(8,128)}, u32[]{:S(2)}) copy-start(f32[1032,128]{1,0:T(8,128)} %get-tuple-element.1991) | copy-start | bytes 1585156 | tf_op jit(solution)/shard_map/cond/branch_1_fun/cond/branch_1_fun/cond
  343.1 5.7 %copy-start.3 = (f32[8,512,128]{2,1,0:T(8,128)S(1)}, f32[8,512,128]{2,1,0:T(8,128)}, u32[]{:S(2)}) copy-start(f32[8,512,128]{2,1,0:T(8,128)} %get-tuple-element.1987) | copy-start | bytes 6291460 | tf_op jit(solution)/shard_map/cond/branch_1_fun/cond/branch_1_fun/cond
  360.4 5.7 %copy-start.4 = (f32[8,512,128]{2,1,0:T(8,128)S(1)}, f32[8,512,128]{2,1,0:T(8,128)}, u32[]{:S(2)}) copy-start(f32[8,512,128]{2,1,0:T(8,128)} %get-tuple-element.1919) | copy-start | bytes 6291460 | tf_op jit(solution)/shard_map/cond/branch_1_fun/cond/branch_1_fun/cond/branch_1_fun/cond
  392.1 4.4 collective-permute-start.7
  401.8 25.3 %collective-permute-start.8 = (bf16[128,4096]{1,0:T(8,128)(2,1)S(1)}, bf16[128,4096]{1,0:T(8,128)(2,1)S(1)}, u32[]{:S(2)}, u32[]{:S(2)}) collective-permute-start(bf16[128,4096]{1,0:T(8,128)(2,1)S(1)} %fusion.219), channel_id=1, source_target_pairs={{0,2},{1,3},{2,0},{3,1},{4,6},{5,7},{6,4},{7,5},{8,10},{9,11},{10,... | collective-permute-start | bytes 3145736 | tf_op jit(solution)/shard_map/ppermute | solution.py:224
  (7 other events, 17.0 us)
Sparse Core Ops, SparseCore 0:
  10.1 125.5 all-gather.2
  137.9 162.5 all-gather.4

commit v3 on v2

--- a/solution.py
+++ b/solution.py
@@ -181,20 +181,15 @@
         is_live = is_live & (ctx_index - offset >= 0) & (key_docs[block_rows - 1] == first_doc)
         steps.append((offset, transfer_in, key_docs, is_live))
 
-    def chain(index, inner):
-        if index == len(steps):
-            return inner
-        offset, transfer_in, key_docs, step_live = steps[index]
-
-        def take(inner):
+    for offset, transfer_in, key_docs, step_live in steps:
+
+        def take(inner, offset=offset, transfer_in=transfer_in, key_docs=key_docs):
             source = jnp.maximum(ctx_index - offset, 0)
             value_pair = lax.dynamic_slice_in_dim(every_value, source * block_rows, block_rows, 2)
             key_pair = lax.dynamic_slice_in_dim(every_key, source * block_rows, block_rows, 1)
-            return chain(index + 1, attend(inner, key_pair, value_pair, transfer_in, key_docs))
-
-        return lax.cond(step_live, take, lambda inner: inner, inner)
-
-    carried = chain(0, carried)
+            return attend(inner, key_pair, value_pair, transfer_in, key_docs)
+
+        carried = lax.cond(step_live, take, lambda inner: inner, carried)
     attended = (carried[3] / carried[2][..., None]).astype(jnp.bfloat16)
     token_rows = jnp.transpose(attended, (1, 0, 2)).reshape(block_rows, head_count * head_width)
     projected = jnp.dot(token_rows, out_weight, preferred_element_type=jnp.float32)

time: 440 us -> 427 us (0.970)
  waiting for transfers between devices: 136 us -> 120 us
  matrix products: 192 us -> 181 us
  local copies, waits for them, and re-layouts: 32 us -> 41.8 us
  between operations: 15.5 us -> 23.5 us
  other arithmetic: 34.9 us -> 29.3 us
    ppermute x7, waiting for transfers between devices: 11.4 us -> 0.02 us  [on_device(): meta_in = lax.ppermute(meta_rows, 'ctx', pairs).astype(jnp.float32)]
    slice x4 -> x5, local copies, waits for them, and re-layouts: 0.14 us -> 8.05 us  [on_device(): meta_in[:head_count * head_width]]
    cond x14 -> x32, local copies, waits for them, and re-layouts: 0.03 us -> 5.94 us
    dot_general x4, matrix products: 13.2 us -> 7.69 us  [attend(): turned = jnp.einsum('hqd,hde->hqe', turned, transfer_in, precision=highest)]
    dot_general x4, matrix products: 22.8 us -> 17.4 us  [attend(): jnp.einsum('hqk,hdk->hqd', weights.astype(jnp.bfloat16), value_pair, pref...]
    convert_element_type x7 -> x6, other arithmetic: 10.3 us -> 4.97 us  [on_device(): meta_in = lax.ppermute(meta_rows, 'ctx', pairs).astype(jnp.float32)]
    unnamed x30 -> x28, local copies, waits for them, and re-layouts: 16.6 us -> 13.3 us
    another operation x5 -> x7, loops' own time: 13 us -> 13.9 us  [on_device(): carried = lax.cond(step_live, take, lambda inner: inner, carried)]
  transfers between devices with their start and end apart: 11 -> 11, of which waited for: 5 -> 4; matrix products, arithmetic and copies ran while one was open for 38% -> 42% of each run, Pallas kernels for 0% -> 0%
where the time goes in v3:
time: 427 us; the launch traced here: 423 us
  matrix products  181 us (42%)
  waiting for transfers between devices  120 us (28%)
  local copies, waits for them, and re-layouts  41.8 us (10%)
  other arithmetic  29.3 us (7%)
  between operations  23.5 us (6%)
  loops' own time  13.9 us (3%)
  starting transfers between devices  13.8 us (3%)
    all_gather x1, waiting for transfers between devices, on_device(): every_key = lax.all_gather(keys_end, 'ctx', axis=1, tiled=True)  67.8 us
    dot_general x1, matrix products, lower_solve(): return jnp.dot(unit_lower_inverse(strict_lower), right, precision=highest)  24.3 us
    all_gather x1, waiting for transfers between devices, on_device(): every_value = lax.all_gather(value_columns, 'ctx', axis=2, tiled=True)  24.3 us
    ppermute x1, waiting for transfers between devices, scatter_sum(): lax.ppermute(outgoing.astype(jnp.bfloat16), 'head', pairs)  23.7 us
    dot_general x1, matrix products, shard_operators(): jnp.dot(scaled_dots, key_solve, precision=highest)  18.4 us
    dot_general x1, matrix products, shard_operators(): jnp.dot(key_solve.T, weighted, precision=highest)  17.5 us
    dot_general x4, matrix products, attend(): jnp.einsum('hqk,hdk->hqd', weights.astype(jnp.bfloat16), value_pair, pref...  17.4 us
    another operation x7, loops' own time, on_device(): carried = lax.cond(step_live, take, lambda inner: inner, carried)  13.9 us
  transfers between devices with their start and end apart: 11, of which 4 were waited for; matrix products, arithmetic and copies ran while one was open for 42% of the time, Pallas kernels for 0%

profile of v3, /device:TPU:16, one launch (start us, length us, event | category | flops | bytes accessed | tf_op | source)
XLA Modules:
  0.0 423.3 jit_solution(15330681264167811306)
XLA Ops:
  18.1 7.3 %multiply_select_fusion.1 = f32[8,512,512]{2,1,0:T(8,128)S(1)} fusion(f32[8,512]{1,0:T(8,128)S(1)} %multiply_bitcast_fusion, pred[512,512]{1,0:T(8,128)(4,1)S(1)} %iota_compare_fusion.4, f32[8,512,128]{2,1,0:T(8,128)S(1)} %broadcast_divide_fusion), kind=kOutput, calls=%fused_computation.174 | convolution fusion | flops 3225419776 | bytes 10764288 | tf_op jit(solution)/shard_map/vmap()/dot_general | solution.py:79
  63.5 6.1 %broadcast_select_fusion = f32[8,512,512]{2,1,0:T(8,128)} fusion(pred[512,512]{1,0:T(8,128)(4,1)S(1)} %iota_compare_fusion.4, f32[8,512,128]{2,1,0:T(8,128)S(1)} %broadcast_divide_fusion, bf16[512,8,128]{2,0,1:T(8,128)(2,1)S(1)} %copy.52), kind=kOutput, calls=%fused_computation.190 | convolution fusion | flops 3223322624 | bytes 11796480 | tf_op jit(solution)/shard_map/vmap()/dot_general | solution.py:81
  69.6 24.3 %fusion.133 = f32[8,512,640]{2,1,0:T(8,128)} fusion(f32[8,512,128]{2,1,0:T(8,128)S(1)} %broadcast_divide_fusion, f32[8,512,512]{2,1,0:T(8,128)} %broadcast_select_fusion, f32[8,256,256]{2,1,0:T(8,128)S(1)} %select_maximum_fusion.2, f32[8,128,128]{2,1,0:T(8,128)} %copy-done.25, f32[8,128,128]{2,1,0:T(8,128)S(1)} %convolution_negate_fusion, ...), kind=kOutput, calls=%fused_computation.154 | convolution fusion | flops 16121331712 | bytes 27262976 | tf_op jit(solution)/shard_map/vmap()/dot_general | solution.py:70
  93.9 17.5 %subtract_convert_fusion = bf16[8,512,128]{2,1,0:T(8,128)(2,1)} fusion(f32[8,512,128]{2,1,0:T(8,128)S(1)} %broadcast_divide_fusion, f32[8,512,640]{2,1,0:T(8,128)} %fusion.133, bf16[512,8,128]{2,0,1:T(8,128)(2,1)S(1)} %copy.52, f32[8,512]{1,0:T(8,128)S(1)} %multiply_bitcast_fusion), kind=kOutput, calls=%fused_computation.226 | convolution fusion | flops 3223322624 | bytes 12599296 | tf_op jit(solution)/shard_map/vmap()/dot_general | solution.py:86
  111.4 24.3 %all-gather.3.cloned.1.call-done = bf16[8,128,4096]{2,1,0:T(8,128)(2,1)} async-done(((bf16[8,128,512]{2,1,0:T(8,128)(2,1)}), bf16[8,128,4096]{2,1,0:T(8,128)(2,1)}) %all-gather.3.cloned.1.call-update) | async-done | bytes 8388624 | tf_op jit(solution)/shard_map/all_gather | solution.py:120
  135.8 5.6 %fusion.217 = bf16[8,128,128]{2,1,0:T(8,128)(2,1)S(1)} fusion(f32[8,512,128]{2,1,0:T(8,128)S(1)} %broadcast_divide_fusion, f32[8,512,640]{2,1,0:T(8,128)} %fusion.133, f32[8,512]{1,0:T(8,128)S(1)} %multiply_bitcast_fusion, f32[128,128]{1,0:T(8,128)S(1)} %get-tuple-element.384), kind=kOutput, calls=%fused_computation.246 | convolution fusion | flops 806092800 | bytes 4538368 | tf_op jit(solution)/shard_map/vmap()/dot_general | solution.py:87
  159.7 4.8 %fusion.222 = f32[8,512,512]{1,2,0:T(8,128)S(1)} fusion(f32[8,512,128]{2,1,0:T(8,128)S(1)} %broadcast_divide_fusion, bf16[512,8,128]{2,0,1:T(8,128)(2,1)} %copy.55), kind=kOutput, calls=%fused_computation.249 | convolution fusion | flops 3221225472 | bytes 11534336 | tf_op jit(solution)/shard_map/vmap()/dot_general | solution.py:90
  164.6 18.4 %fusion.150 = f32[8,512,512]{1,2,0:T(8,128)} fusion(f32[8,512,640]{2,1,0:T(8,128)} %fusion.133, f32[8,512,512]{1,2,0:T(8,128)S(1)} %fusion.222, f32[8,512]{1,0:T(8,128)S(1)} %multiply_bitcast_fusion, pred[512,512]{1,0:T(8,128)(4,1)S(1)} %iota_compare_fusion.3), kind=kOutput, calls=%fused_computation.177 | convolution fusion | flops 12889096192 | bytes 25444352 | tf_op jit(solution)/shard_map/vmap()/dot_general | solution.py:92
  183.0 5.3 %fusion.246 = (f32[8,512]{1,0:T(8,128)S(1)}, f32[8,512,512]{1,2,0:T(8,128)S(1)}) fusion(f32[8,512,512]{1,2,0:T(8,128)} %fusion.150, bf16[512,8,128]{2,0,1:T(8,128)(2,1)S(1)} %copy.52, bf16[512,8,128]{2,0,1:T(8,128)(2,1)S(1)} %copy-done.1, pred[512,512]{0,1:T(8,128)(4,1)S(1)} %copy-done.26), kind=kOutput, calls=%fused_computation.344 | convolution fusion | flops 545255424 | bytes 19152896 | tf_op jit(solution)/shard_map/vmap()/dot_general | solution.py:92
  191.6 9.6 %convert_subtract_fusion = f32[8,512,128]{2,1,0:T(8,128)S(1)} fusion(f32[8,512,640]{2,1,0:T(8,128)} %fusion.133, f32[8,512,512]{1,2,0:T(8,128)S(1)} %fusion.222, f32[8,512]{1,0:T(8,128)S(1)} %multiply_bitcast_fusion, pred[512,512]{1,0:T(8,128)(4,1)S(1)} %iota_compare_fusion.3, bf16[512,8,128]{2,0,1:T(8,128)(2,1)S(1)} %copy-done.2), kind=kOutput, calls=%fused_computation.228 | convolution fusion | flops 3226468352 | bytes 13910016 | tf_op jit(solution)/shard_map/vmap()/dot_general | solution.py:95
  232.7 67.8 %all-gather.5.cloned.1.call-done = bf16[8,4096,128]{2,1,0:T(8,128)(2,1)} async-done(((bf16[8,512,128]{2,1,0:T(8,128)(2,1)}), bf16[8,4096,128]{2,1,0:T(8,128)(2,1)}) %all-gather.5.cloned.1.call-update) | async-done | bytes 8388624 | tf_op jit(solution)/shard_map/all_gather | solution.py:173
  300.5 12.6 %conditional.7 = ((f32[8,512,128]{2,1,0:T(8,128)S(1)}, f32[8,512]{1,0:T(8,128)S(1)}, f32[8,512]{1,0:T(8,128)S(1)}, f32[8,512,128]{2,1,0:T(8,128)})) conditional(s32[]{:T(128)} %convert_element_type.166, (f32[8,512,128]{2,1,0:T(8,128)S(1)}, f32[8,512]{1,0:T(8,128)S(1)}, f32[8,512]{1,0:T(8,128)S(1)}, f32[8,512,128]{2,1,0:T(8,128)}) %tuple.52, ...), branch_computations={%region_3.4_spmd, %region_4.7_spmd} | conditional | flops 1903960064 | bytes 62656712 | solution.py:192
  305.5 4.4 %multiply_add_fusion = f32[8,512,128]{2,1,0:T(8,128)S(1)} fusion(f32[8,512,128]{2,1,0:T(8,128)S(1)} %copy-done.5, f32[8,512,512]{2,1,0:T(8,128)S(1)} %get-tuple-element.343, f32[8,512]{1,0:T(8,128)S(1)} %max.29, pred[512,512]{0,1:T(8,128)(4,1)S(1)} %broadcast_compare_fusion, bf16[8,128,4096]{2,1,0:T(8,128)(2,1)} %get-tuple-element.206, s32[]{:T(128)S(6)} %select_n.248, ...), kind=kOutput, calls=%fused_computation.10 | convolution fusion | flops 546308096 | bytes 13926404 | tf_op jit(solution)/shard_map/cond/branch_1_fun/hqk,hdk->hqd/dot_general | solution.py:156
  313.2 13.1 %conditional.8 = ((f32[8,512,128]{2,1,0:T(8,128)S(1)}, f32[8,512]{1,0:T(8,128)S(1)}, f32[8,512]{1,0:T(8,128)S(1)}, f32[8,512,128]{2,1,0:T(8,128)})) conditional(s32[]{:T(128)} %convert_element_type.165, (f32[8,512,128]{2,1,0:T(8,128)S(1)}, f32[8,512]{1,0:T(8,128)S(1)}, f32[8,512]{1,0:T(8,128)S(1)}, f32[8,512,128]{2,1,0:T(8,128)}) %get-tuple-element.438, ...), branch_computations={%region_7.8_spmd, %region_8.11_spmd} | conditional | flops 1903960064 | bytes 62656712 | solution.py:192
  318.2 4.4 %multiply_add_fusion.2 = f32[8,512,128]{2,1,0:T(8,128)S(1)} fusion(f32[8,512,128]{2,1,0:T(8,128)S(1)} %copy-done.7, f32[8,512,512]{2,1,0:T(8,128)S(1)} %get-tuple-element.345, f32[8,512]{1,0:T(8,128)S(1)} %max.31, pred[512,512]{0,1:T(8,128)(4,1)S(1)} %broadcast_compare_fusion.1, bf16[8,128,4096]{2,1,0:T(8,128)(2,1)} %get-tuple-element.216, ...), kind=kOutput, calls=%fused_computation.32 | convolution fusion | flops 546308096 | bytes 13926404 | tf_op jit(solution)/shard_map/cond/branch_1_fun/hqk,hdk->hqd/dot_general | solution.py:156
  326.2 12.7 %conditional.9 = ((f32[8,512,128]{2,1,0:T(8,128)S(1)}, f32[8,512]{1,0:T(8,128)S(1)}, f32[8,512]{1,0:T(8,128)S(1)}, f32[8,512,128]{2,1,0:T(8,128)})) conditional(s32[]{:T(128)} %convert_element_type.164, (f32[8,512,128]{2,1,0:T(8,128)S(1)}, f32[8,512]{1,0:T(8,128)S(1)}, f32[8,512]{1,0:T(8,128)S(1)}, ...), branch_computations={%region_11.12_spmd, %region_12.15_spmd} | conditional | flops 1903960064 | bytes 62656712 | solution.py:192
  331.3 4.4 %multiply_add_fusion.4 = f32[8,512,128]{2,1,0:T(8,128)S(1)} fusion(f32[8,512,128]{2,1,0:T(8,128)S(1)} %copy-done.9, f32[8,512,512]{2,1,0:T(8,128)S(1)} %get-tuple-element.347, f32[8,512]{1,0:T(8,128)S(1)} %max.33, pred[512,512]{0,1:T(8,128)(4,1)S(1)} %broadcast_compare_fusion.2, bf16[8,128,4096]{2,1,0:T(8,128)(2,1)} %get-tuple-element.226, ...), kind=kOutput, calls=%fused_computation.54 | convolution fusion | flops 546308096 | bytes 13926404 | tf_op jit(solution)/shard_map/cond/branch_1_fun/hqk,hdk->hqd/dot_general | solution.py:156
  338.9 12.8 %conditional.10 = ((f32[8,512,128]{2,1,0:T(8,128)S(1)}, f32[8,512]{1,0:T(8,128)S(1)}, f32[8,512]{1,0:T(8,128)S(1)}, f32[8,512,128]{2,1,0:T(8,128)})) conditional(s32[]{:T(128)} %convert_element_type.163, (f32[8,512,128]{2,1,0:T(8,128)S(1)}, f32[8,512]{1,0:T(8,128)S(1)}, f32[8,512]{1,0:T(8,128)S(1)}, ...), branch_computations={%region_15.16_spmd, %region_16.19_spmd} | conditional | flops 1903960064 | bytes 62656712 | solution.py:192
  344.1 4.4 %multiply_add_fusion.6 = f32[8,512,128]{2,1,0:T(8,128)S(1)} fusion(f32[8,512,128]{2,1,0:T(8,128)S(1)} %copy-done.11, f32[8,512,512]{2,1,0:T(8,128)S(1)} %get-tuple-element.349, f32[8,512]{1,0:T(8,128)S(1)} %max.35, pred[512,512]{0,1:T(8,128)(4,1)S(1)} %broadcast_compare_fusion.3, bf16[8,128,4096]{2,1,0:T(8,128)(2,1)} %get-tuple-element.236, ...), kind=kOutput, calls=%fused_computation.76 | convolution fusion | flops 546308096 | bytes 13926404 | tf_op jit(solution)/shard_map/cond/branch_1_fun/hqk,hdk->hqd/dot_general | solution.py:156
  352.0 5.6 %conditional.12 = ((f32[8,512,128]{2,1,0:T(8,128)S(1)}, f32[8,512]{1,0:T(8,128)S(1)}, f32[8,512]{1,0:T(8,128)S(1)}, f32[8,512,128]{2,1,0:T(8,128)})) conditional(s32[]{:T(128)} %convert_element_type.161, (f32[8,512,128]{2,1,0:T(8,128)S(1)}, f32[8,512]{1,0:T(8,128)S(1)}, f32[8,512]{1,0:T(8,128)S(1)}, ...), branch_computations={%region_23.24_spmd, %region_24.27_spmd} | conditional | flops 1903960064 | bytes 61608112 | solution.py:192
  357.6 7.1 %conditional.13 = ((f32[8,512]{1,0:T(8,128)S(1)}, f32[8,512,128]{2,1,0:T(8,128)})) conditional(s32[]{:T(128)} %convert_element_type.160, (f32[8,512]{1,0:T(8,128)S(1)}, f32[8,512,128]{2,1,0:T(8,128)}) %tuple.60, (f32[512]{0:T(512)S(1)}, f32[512]{0:T(512)S(1)}, s32[]{:T(128)}, bf16[8,4096,128]{2,1,0:T(8,128)(2,1)}, f32[8,512,128]{2,1,0:T(8,128)S(1)}, ...), branch_computations={%region_27.28_spmd, %region_28.31_spmd} | conditional | flops 1098653696 | bytes 51613852 | solution.py:192
  367.9 6.9 %fusion.145 = f32[2,2,128,4096]{3,2,1,0:T(8,128)S(1)} fusion(bf16[2,2,128,1024]{3,2,1,0:T(8,128)(2,1)S(1)} %dot_general.180, bf16[1024,4096]{1,0:T(8,128)(2,1)} %param.27), kind=kOutput, calls=%fused_computation.168 | convolution fusion | flops 4294967296 | bytes 17825792 | tf_op jit(solution)/shard_map/dot_general | solution.py:195
  378.5 4.2 %collective-permute-done.7 = bf16[2,128,4096]{2,1,0:T(8,128)(2,1)} collective-permute-done((bf16[2,128,4096]{2,1,0:T(8,128)(2,1)S(1)}, bf16[2,128,4096]{2,1,0:T(8,128)(2,1)}, u32[]{:S(2)}, u32[]{:S(2)}) %collective-permute-start.7) | collective-permute-done | bytes 2097184 | tf_op jit(solution)/shard_map/ppermute | solution.py:212
  389.7 23.7 %collective-permute-done.8 = bf16[128,4096]{1,0:T(8,128)(2,1)S(1)} collective-permute-done((bf16[128,4096]{1,0:T(8,128)(2,1)S(1)}, bf16[128,4096]{1,0:T(8,128)(2,1)S(1)}, u32[]{:S(2)}, u32[]{:S(2)}) %collective-permute-start.8) | collective-permute-done | bytes 1048608 | tf_op jit(solution)/shard_map/ppermute | solution.py:219
  (190 shorter events, 142.8 us)
Async XLA Ops:
  6.5 129.2 %all-gather.3.cloned.1.call-start = ((), (), s32[]{:S(2)}) async-start(), calls=%async_computation | async-start | bytes 9437184 | tf_op jit(solution)/shard_map/all_gather | solution.py:120
  10.0 4.8 %copy-start = (f32[512,8,128]{2,0,1:T(8,128)}, f32[512,8,128]{2,0,1:T(8,128)S(1)}, u32[]{:S(2)}) copy-start(f32[512,8,128]{2,0,1:T(8,128)S(1)} %copy.41) | copy-start | bytes 6291460
  10.0 290.5 %all-gather.5.cloned.1.call-start = ((), (), s32[]{:S(2)}) async-start(), calls=%async_computation.1 | async-start | bytes 9437184 | tf_op jit(solution)/shard_map/all_gather | solution.py:173
  13.0 2.9 copy-start.29
  54.4 7.0 %copy-start.25 = (f32[8,128,128]{2,1,0:T(8,128)}, f32[8,128,128]{2,1,0:T(8,128)S(1)}, u32[]{:S(2)}) copy-start(f32[8,128,128]{2,1,0:T(8,128)S(1)} %get-tuple-element.363) | copy-start | bytes 1572868
  93.9 41.8 %copy-start.30 = (s32[512]{0:T(512)S(1)}, s32[512]{0:T(512)}, u32[]{:S(2)}) copy-start(s32[512]{0:T(512)} %param.26) | copy-start | bytes 6148
  142.8 60.3 %collective-permute-start = (bf16[1032,128]{1,0:T(8,128)(2,1)}, bf16[1032,128]{1,0:T(8,128)(2,1)S(1)}, u32[]{:S(2)}, u32[]{:S(2)}) collective-permute-start(bf16[1032,128]{1,0:T(8,128)(2,1)} %concatenate.48), channel_id=1, source_target_pairs={{0,4},{4,8},{8,12},{12,16},{16,20},{20,24},{24,28},{1,5},{5,9},{9,... | collective-permute-start | bytes 792584 | tf_op jit(solution)/shard_map/ppermute | solution.py:178
  145.3 59.2 %collective-permute-start.1 = (bf16[1032,128]{1,0:T(8,128)(2,1)}, bf16[1032,128]{1,0:T(8,128)(2,1)}, u32[]{:S(2)}, u32[]{:S(2)}) collective-permute-start(bf16[1032,128]{1,0:T(8,128)(2,1)} %concatenate.48), channel_id=1, source_target_pairs={{0,8},{4,12},{8,16},{12,20},{16,24},{20,28},{1,9},{5,13},{9,17},{1... | collective-permute-start | bytes 792584 | tf_op jit(solution)/shard_map/ppermute | solution.py:178
  147.7 59.2 %collective-permute-start.2 = (bf16[1032,128]{1,0:T(8,128)(2,1)}, bf16[1032,128]{1,0:T(8,128)(2,1)}, u32[]{:S(2)}, u32[]{:S(2)}) collective-permute-start(bf16[1032,128]{1,0:T(8,128)(2,1)} %concatenate.48), channel_id=1, source_target_pairs={{0,12},{4,16},{8,20},{12,24},{16,28},{1,13},{5,17},{9,21},{13,25},... | collective-permute-start | bytes 792584 | tf_op jit(solution)/shard_map/ppermute | solution.py:178
  149.6 58.3 %collective-permute-start.3 = (bf16[1032,128]{1,0:T(8,128)(2,1)}, bf16[1032,128]{1,0:T(8,128)(2,1)}, u32[]{:S(2)}, u32[]{:S(2)}) collective-permute-start(bf16[1032,128]{1,0:T(8,128)(2,1)} %concatenate.48), channel_id=1, source_target_pairs={{0,16},{4,20},{8,24},{12,28},{1,17},{5,21},{9,25},{13,29},{2,18},{... | collective-permute-start | bytes 792584 | tf_op jit(solution)/shard_map/ppermute | solution.py:178
  150.9 58.0 %collective-permute-start.4 = (bf16[1032,128]{1,0:T(8,128)(2,1)}, bf16[1032,128]{1,0:T(8,128)(2,1)}, u32[]{:S(2)}, u32[]{:S(2)}) collective-permute-start(bf16[1032,128]{1,0:T(8,128)(2,1)} %concatenate.48), channel_id=1, source_target_pairs={{0,20},{4,24},{8,28},{1,21},{5,25},{9,29},{2,22},{6,26},{10,30},{3... | collective-permute-start | bytes 792584 | tf_op jit(solution)/shard_map/ppermute | solution.py:178
  164.6 18.4 %copy-start.1 = (bf16[512,8,128]{2,0,1:T(8,128)(2,1)S(1)}, bf16[512,8,128]{2,0,1:T(8,128)(2,1)}, u32[]{:S(2)}) copy-start(bf16[512,8,128]{2,0,1:T(8,128)(2,1)} %copy.55) | copy-start | bytes 3145732
  164.6 18.4 %copy-start.26 = (pred[512,512]{0,1:T(8,128)(4,1)S(1)}, pred[512,512]{0,1:T(8,128)(4,1)}, u32[]{:S(2)}) copy-start(pred[512,512]{0,1:T(8,128)(4,1)} %copy.57) | copy-start | bytes 786436
  183.0 5.4 %copy-start.4 = (bf16[512,1024]{0,1:T(8,128)(2,1)S(1)}, bf16[512,1024]{0,1:T(8,128)(2,1)}, u32[]{:S(2)}) copy-start(bf16[512,1024]{0,1:T(8,128)(2,1)} %copy.39) | copy-start | bytes 3145732
  188.4 3.2 copy-start.2
  203.1 16.2 %collective-permute-start.5 = (bf16[1032,128]{1,0:T(8,128)(2,1)S(1)}, bf16[1032,128]{1,0:T(8,128)(2,1)}, u32[]{:S(2)}, u32[]{:S(2)}) collective-permute-start(bf16[1032,128]{1,0:T(8,128)(2,1)S(1)} %copy-done.28), channel_id=1, source_target_pairs={{0,24},{4,28},{1,25},{5,29},{2,26},{6,30},{3,27},{7,31}} | collective-permute-start | bytes 792584 | tf_op jit(solution)/shard_map/ppermute | solution.py:178
  204.5 17.6 %collective-permute-start.6 = (bf16[1032,128]{1,0:T(8,128)(2,1)S(1)}, bf16[1032,128]{1,0:T(8,128)(2,1)}, u32[]{:S(2)}, u32[]{:S(2)}) collective-permute-start(bf16[1032,128]{1,0:T(8,128)(2,1)S(1)} %copy-done.28), channel_id=1, source_target_pairs={{0,28},{1,29},{2,30},{3,31}} | collective-permute-start | bytes 792584 | tf_op jit(solution)/shard_map/ppermute | solution.py:178
  305.5 5.7 %copy-start.24 = (f32[8,128,128]{2,1,0:T(8,128)S(1)}, f32[8,128,128]{2,1,0:T(8,128)}, u32[]{:S(2)}) copy-start(f32[8,128,128]{2,1,0:T(8,128)} %get-tuple-element.198) | copy-start | bytes 1572868 | tf_op jit(solution)/shard_map/cond
  318.2 5.7 %copy-start.23 = (f32[8,128,128]{2,1,0:T(8,128)S(1)}, f32[8,128,128]{2,1,0:T(8,128)}, u32[]{:S(2)}) copy-start(f32[8,128,128]{2,1,0:T(8,128)} %get-tuple-element.208) | copy-start | bytes 1572868 | tf_op jit(solution)/shard_map/cond
  331.3 5.7 %copy-start.22 = (f32[8,128,128]{2,1,0:T(8,128)S(1)}, f32[8,128,128]{2,1,0:T(8,128)}, u32[]{:S(2)}) copy-start(f32[8,128,128]{2,1,0:T(8,128)} %get-tuple-element.218) | copy-start | bytes 1572868 | tf_op jit(solution)/shard_map/cond
  344.1 5.7 %copy-start.21 = (f32[8,128,128]{2,1,0:T(8,128)S(1)}, f32[8,128,128]{2,1,0:T(8,128)}, u32[]{:S(2)}) copy-start(f32[8,128,128]{2,1,0:T(8,128)} %get-tuple-element.228) | copy-start | bytes 1572868 | tf_op jit(solution)/shard_map/cond
  374.8 3.3 copy-start.19
  378.3 4.4 %collective-permute-start.7 = (bf16[2,128,4096]{2,1,0:T(8,128)(2,1)S(1)}, bf16[2,128,4096]{2,1,0:T(8,128)(2,1)}, u32[]{:S(2)}, u32[]{:S(2)}) collective-permute-start(bf16[2,128,4096]{2,1,0:T(8,128)(2,1)S(1)} %fusion.168), channel_id=1, source_target_pairs={{0,1},{1,0},{2,3},{3,2},{4,5},{5,4},{6,7},{7,6},{8,9},{9,8},{10,11... | collective-permute-start | bytes 6291464 | tf_op jit(solution)/shard_map/ppermute | solution.py:212
  388.1 25.3 %collective-permute-start.8 = (bf16[128,4096]{1,0:T(8,128)(2,1)S(1)}, bf16[128,4096]{1,0:T(8,128)(2,1)S(1)}, u32[]{:S(2)}, u32[]{:S(2)}) collective-permute-start(bf16[128,4096]{1,0:T(8,128)(2,1)S(1)} %fusion.220), channel_id=1, source_target_pairs={{0,2},{1,3},{2,0},{3,1},{4,6},{5,7},{6,4},{7,5},{8,10},{9,11},{10,... | collective-permute-start | bytes 3145736 | tf_op jit(solution)/shard_map/ppermute | solution.py:219
  (11 other events, 18.8 us)
Sparse Core Ops, SparseCore 0:
  10.2 125.5 all-gather.2
  137.9 162.5 all-gather.4

commit v4 on v3

--- a/solution.py
+++ b/solution.py
@@ -117,11 +117,14 @@
         jnp.sum(vector_heads * vector_heads, axis=2, keepdims=True) + epsilon
     )
     strength = 2.0 * jax.nn.sigmoid(beta_logit.T)
-    every_value = lax.all_gather(value_columns, "ctx", axis=2, tiled=True)
+    ctx_total = lax.axis_size("ctx")
+    every_value = lax.all_to_all(
+        jnp.broadcast_to(value_columns[None], (ctx_total,) + value_columns.shape), "ctx", 0, 0
+    )
     intra_scores, keys_end, transfer, rotated = jax.vmap(shard_operators)(
         query_heads, key_heads, unit_vectors, strength
     )
-    every_value, keys_end = lax.optimization_barrier((every_value, keys_end))
+    every_value, rotated = lax.optimization_barrier((every_value, rotated))
     row_ids = jnp.arange(block_rows)
     causal = row_ids[:, None] >= row_ids[None, :]
     doc_float = (document_ids + 1).astype(jnp.float32)
@@ -185,7 +188,7 @@
 
         def take(inner, offset=offset, transfer_in=transfer_in, key_docs=key_docs):
             source = jnp.maximum(ctx_index - offset, 0)
-            value_pair = lax.dynamic_slice_in_dim(every_value, source * block_rows, block_rows, 2)
+            value_pair = lax.dynamic_index_in_dim(every_value, source, 0, keepdims=False)
             key_pair = lax.dynamic_slice_in_dim(every_key, source * block_rows, block_rows, 1)
             return attend(inner, key_pair, value_pair, transfer_in, key_docs)
 

time: 427 us -> 492 us (1.15)
  the two profiles are of different devices: /device:TPU:16 before, /device:TPU:10 now
where the time goes in v4:
time: 492 us; the launch traced here: 488 us
  waiting for transfers between devices  175 us (36%)
  matrix products  174 us (35%)
  local copies, waits for them, and re-layouts  44.4 us (9%)
  other arithmetic  29 us (6%)
  between operations  23.2 us (5%)
  starting transfers between devices  22.9 us (5%)
  loops' own time  19.2 us (4%)
    ppermute x7, waiting for transfers between devices, on_device(): meta_in = lax.ppermute(meta_rows, 'ctx', pairs).astype(jnp.float32)  147 us
    dot_general x1, matrix products, lower_solve(): return jnp.dot(unit_lower_inverse(strict_lower), right, precision=highest)  24.2 us
    ppermute x1, waiting for transfers between devices, scatter_sum(): lax.ppermute(outgoing.astype(jnp.bfloat16), 'head', pairs)  23.7 us
    another operation x7, loops' own time, on_device(): carried = lax.cond(step_live, take, lambda inner: inner, carried)  19.2 us
    dot_general x1, matrix products, shard_operators(): jnp.dot(scaled_dots, key_solve, precision=highest)  18.4 us
    dot_general x1, matrix products, shard_operators(): jnp.dot(key_solve.T, weighted, precision=highest)  17.4 us
    ppermute x7, starting transfers between devices, on_device(): meta_in = lax.ppermute(meta_rows, 'ctx', pairs).astype(jnp.float32)  15 us
    unnamed x34, local copies, waits for them, and re-layouts  14.6 us
  transfers between devices with their start and end apart: 11, of which 6 were waited for; matrix products, arithmetic and copies ran while one was open for 37% of the time, Pallas kernels for 0%

profile of v4, /device:TPU:10, one launch (start us, length us, event | category | flops | bytes accessed | tf_op | source)
XLA Modules:
  0.0 487.8 jit_solution(17383395796204239716)
XLA Ops:
  17.7 6.2 %all-to-all-start = ((bf16[8,8,128,512]{3,2,1,0:T(8,128)(2,1)}), bf16[8,8,128,512]{3,2,1,0:T(8,128)(2,1)}, u32[]{:S(2)}, u32[]{:S(2)}) async-start(bf16[8,8,128,512]{3,2,1,0:T(8,128)(2,1)} %broadcast_in_dim.200), calls=%async_computation | async-start | bytes 16777216 | tf_op jit(solution)/shard_map/all_to_all | solution.py:121
  27.0 7.3 %multiply_select_fusion.1 = f32[8,512,512]{2,1,0:T(8,128)S(1)} fusion(f32[8,512]{1,0:T(8,128)S(1)} %multiply_bitcast_fusion, pred[512,512]{1,0:T(8,128)(4,1)S(1)} %iota_compare_fusion.4, f32[8,512,128]{2,1,0:T(8,128)S(1)} %broadcast_divide_fusion), kind=kOutput, calls=%fused_computation.181 | convolution fusion | flops 3225419776 | bytes 10764288 | tf_op jit(solution)/shard_map/vmap()/dot_general | solution.py:79
  78.9 6.1 %broadcast_select_fusion = f32[8,512,512]{2,1,0:T(8,128)} fusion(pred[512,512]{1,0:T(8,128)(4,1)S(1)} %iota_compare_fusion.4, f32[8,512,128]{2,1,0:T(8,128)S(1)} %broadcast_divide_fusion, bf16[512,8,128]{2,0,1:T(8,128)(2,1)S(1)} %copy.52), kind=kOutput, calls=%fused_computation.197 | convolution fusion | flops 3223322624 | bytes 11796480 | tf_op jit(solution)/shard_map/vmap()/dot_general | solution.py:81
  87.3 24.2 %fusion.140 = f32[8,512,640]{2,1,0:T(8,128)} fusion(f32[8,512,128]{2,1,0:T(8,128)S(1)} %broadcast_divide_fusion, f32[8,512,512]{2,1,0:T(8,128)} %broadcast_select_fusion, f32[8,256,256]{2,1,0:T(8,128)S(1)} %copy-done.22, f32[8,128,128]{2,1,0:T(8,128)S(1)} %copy-done.28, f32[8,128,128]{2,1,0:T(8,128)S(1)} %copy-done.21, ...), kind=kOutput, calls=%fused_computation.161 | convolution fusion | flops 16121331712 | bytes 27262976 | tf_op jit(solution)/shard_map/vmap()/dot_general | solution.py:70
  111.5 17.4 %subtract_convert_fusion = bf16[8,512,128]{2,1,0:T(8,128)(2,1)} fusion(f32[8,512,128]{2,1,0:T(8,128)S(1)} %broadcast_divide_fusion, f32[8,512,640]{2,1,0:T(8,128)} %fusion.140, bf16[512,8,128]{2,0,1:T(8,128)(2,1)S(1)} %copy.52, f32[8,512]{1,0:T(8,128)S(1)} %multiply_bitcast_fusion), kind=kOutput, calls=%fused_computation.233 | convolution fusion | flops 3223322624 | bytes 12599296 | tf_op jit(solution)/shard_map/vmap()/dot_general | solution.py:86
  129.0 5.6 %fusion.224 = bf16[8,128,128]{2,1,0:T(8,128)(2,1)S(1)} fusion(f32[8,512,128]{2,1,0:T(8,128)S(1)} %broadcast_divide_fusion, f32[8,512,640]{2,1,0:T(8,128)} %fusion.140, f32[8,512]{1,0:T(8,128)S(1)} %multiply_bitcast_fusion, f32[128,128]{1,0:T(8,128)S(1)} %get-tuple-element.384), kind=kOutput, calls=%fused_computation.253 | convolution fusion | flops 806092800 | bytes 4538368 | tf_op jit(solution)/shard_map/vmap()/dot_general | solution.py:87
  154.2 4.8 fusion.230
  159.1 18.4 %fusion.157 = f32[8,512,512]{1,2,0:T(8,128)} fusion(f32[8,512,640]{2,1,0:T(8,128)} %fusion.140, f32[8,512,512]{1,2,0:T(8,128)S(1)} %fusion.230, f32[8,512]{1,0:T(8,128)S(1)} %multiply_bitcast_fusion, pred[512,512]{1,0:T(8,128)(4,1)S(1)} %iota_compare_fusion.3), kind=kOutput, calls=%fused_computation.184 | convolution fusion | flops 12889096192 | bytes 25444352 | tf_op jit(solution)/shard_map/vmap()/dot_general | solution.py:92
  177.6 5.4 %fusion.254 = (f32[8,512]{1,0:T(8,128)S(1)}, f32[8,512,512]{1,2,0:T(8,128)S(1)}) fusion(f32[8,512,512]{1,2,0:T(8,128)} %fusion.157, bf16[512,8,128]{2,0,1:T(8,128)(2,1)S(1)} %copy.52, bf16[512,8,128]{2,0,1:T(8,128)(2,1)S(1)} %copy-done.1, pred[512,512]{0,1:T(8,128)(4,1)S(1)} %copy-done.30), kind=kOutput, calls=%fused_computation.353 | convolution fusion | flops 545255424 | bytes 19152896 | tf_op jit(solution)/shard_map/vmap()/dot_general | solution.py:92
  186.2 9.6 %convert_subtract_fusion = f32[8,512,128]{2,1,0:T(8,128)S(1)} fusion(f32[8,512,640]{2,1,0:T(8,128)} %fusion.140, f32[8,512,512]{1,2,0:T(8,128)S(1)} %fusion.230, f32[8,512]{1,0:T(8,128)S(1)} %multiply_bitcast_fusion, pred[512,512]{1,0:T(8,128)(4,1)S(1)} %iota_compare_fusion.3, bf16[512,8,128]{2,0,1:T(8,128)(2,1)S(1)} %copy-done.2), kind=kOutput, calls=%fused_computation.235 | convolution fusion | flops 3226468352 | bytes 13910016 | tf_op jit(solution)/shard_map/vmap()/dot_general | solution.py:95
  197.7 127.5 %collective-permute-done = bf16[1032,128]{1,0:T(8,128)(2,1)} collective-permute-done((bf16[1032,128]{1,0:T(8,128)(2,1)}, bf16[1032,128]{1,0:T(8,128)(2,1)}, u32[]{:S(2)}, u32[]{:S(2)}) %collective-permute-start) | collective-permute-done | bytes 264224 | tf_op jit(solution)/shard_map/ppermute | solution.py:181
  327.6 9.0 %collective-permute-done.1 = bf16[1032,128]{1,0:T(8,128)(2,1)} collective-permute-done((bf16[1032,128]{1,0:T(8,128)(2,1)}, bf16[1032,128]{1,0:T(8,128)(2,1)}, u32[]{:S(2)}, u32[]{:S(2)}) %collective-permute-start.1) | collective-permute-done | bytes 264224 | tf_op jit(solution)/shard_map/ppermute | solution.py:181
  338.9 6.1 %collective-permute-done.2 = bf16[1032,128]{1,0:T(8,128)(2,1)} collective-permute-done((bf16[1032,128]{1,0:T(8,128)(2,1)}, bf16[1032,128]{1,0:T(8,128)(2,1)}, u32[]{:S(2)}, u32[]{:S(2)}) %collective-permute-start.2) | collective-permute-done | bytes 264224 | tf_op jit(solution)/shard_map/ppermute | solution.py:181
  346.0 4.6 collective-permute-done.3
  375.9 11.4 %conditional.7 = ((f32[8,512,128]{2,1,0:T(8,128)S(1)}, f32[8,512]{1,0:T(8,128)S(1)}, f32[8,512]{1,0:T(8,128)S(1)}, f32[8,512,128]{2,1,0:T(8,128)})) conditional(s32[]{:T(128)} %convert_element_type.166, (f32[8,512,128]{2,1,0:T(8,128)S(1)}, f32[8,512]{1,0:T(8,128)S(1)}, f32[8,512]{1,0:T(8,128)S(1)}, f32[8,512,128]{2,1,0:T(8,128)}) %tuple.53, ...), branch_computations={%region_3.4_spmd, %region_4.7_spmd} | conditional | flops 1903960064 | bytes 62656712 | solution.py:195
  381.0 4.4 multiply_add_fusion
  387.4 11.9 %conditional.8 = ((f32[8,512,128]{2,1,0:T(8,128)S(1)}, f32[8,512]{1,0:T(8,128)S(1)}, f32[8,512]{1,0:T(8,128)S(1)}, f32[8,512,128]{2,1,0:T(8,128)})) conditional(s32[]{:T(128)} %convert_element_type.165, (f32[8,512,128]{2,1,0:T(8,128)S(1)}, f32[8,512]{1,0:T(8,128)S(1)}, f32[8,512]{1,0:T(8,128)S(1)}, f32[8,512,128]{2,1,0:T(8,128)}) %get-tuple-element.438, ...), branch_computations={%region_7.8_spmd, %region_8.11_spmd} | conditional | flops 1903960064 | bytes 62656712 | solution.py:195
  392.4 4.4 multiply_add_fusion.2
  399.2 11.4 %conditional.9 = ((f32[8,512,128]{2,1,0:T(8,128)S(1)}, f32[8,512]{1,0:T(8,128)S(1)}, f32[8,512]{1,0:T(8,128)S(1)}, f32[8,512,128]{2,1,0:T(8,128)})) conditional(s32[]{:T(128)} %convert_element_type.164, (f32[8,512,128]{2,1,0:T(8,128)S(1)}, f32[8,512]{1,0:T(8,128)S(1)}, f32[8,512]{1,0:T(8,128)S(1)}, ...), branch_computations={%region_11.12_spmd, %region_12.15_spmd} | conditional | flops 1903960064 | bytes 62656712 | solution.py:195
  410.9 5.6 %conditional.11 = ((f32[8,512,128]{2,1,0:T(8,128)S(1)}, f32[8,512]{1,0:T(8,128)S(1)}, f32[8,512]{1,0:T(8,128)S(1)}, f32[8,512,128]{2,1,0:T(8,128)})) conditional(s32[]{:T(128)} %convert_element_type.162, (f32[8,512,128]{2,1,0:T(8,128)S(1)}, f32[8,512]{1,0:T(8,128)S(1)}, f32[8,512]{1,0:T(8,128)S(1)}, ...), branch_computations={%region_19.20_spmd, %region_20.23_spmd} | conditional | flops 1903960064 | bytes 62656712 | solution.py:195
  416.4 5.6 %conditional.12 = ((f32[8,512,128]{2,1,0:T(8,128)S(1)}, f32[8,512]{1,0:T(8,128)S(1)}, f32[8,512]{1,0:T(8,128)S(1)}, f32[8,512,128]{2,1,0:T(8,128)})) conditional(s32[]{:T(128)} %convert_element_type.161, (f32[8,512,128]{2,1,0:T(8,128)S(1)}, f32[8,512]{1,0:T(8,128)S(1)}, f32[8,512]{1,0:T(8,128)S(1)}, ...), branch_computations={%region_23.24_spmd, %region_24.27_spmd} | conditional | flops 1903960064 | bytes 61608112 | solution.py:195
  422.1 7.1 %conditional.13 = ((f32[8,512]{1,0:T(8,128)S(1)}, f32[8,512,128]{2,1,0:T(8,128)})) conditional(s32[]{:T(128)} %convert_element_type.160, (f32[8,512]{1,0:T(8,128)S(1)}, f32[8,512,128]{2,1,0:T(8,128)}) %tuple.60, (f32[512]{0:T(512)S(1)}, f32[512]{0:T(512)S(1)}, s32[]{:T(128)}, bf16[8,4096,128]{2,1,0:T(8,128)(2,1)}, f32[8,512,128]{2,1,0:T(8,128)S(1)}, ...), branch_computations={%region_27.28_spmd, %region_28.31_spmd} | conditional | flops 1098653696 | bytes 51613852 | solution.py:195
  432.3 6.9 %fusion.152 = f32[2,2,128,4096]{3,2,1,0:T(8,128)S(1)} fusion(bf16[2,2,128,1024]{3,2,1,0:T(8,128)(2,1)S(1)} %dot_general.180, bf16[1024,4096]{1,0:T(8,128)(2,1)} %param.27), kind=kOutput, calls=%fused_computation.175 | convolution fusion | flops 4294967296 | bytes 17825792 | tf_op jit(solution)/shard_map/dot_general | solution.py:198
  454.1 23.7 %collective-permute-done.8 = bf16[128,4096]{1,0:T(8,128)(2,1)S(1)} collective-permute-done((bf16[128,4096]{1,0:T(8,128)(2,1)S(1)}, bf16[128,4096]{1,0:T(8,128)(2,1)S(1)}, u32[]{:S(2)}, u32[]{:S(2)}) %collective-permute-start.8) | collective-permute-done | bytes 1048608 | tf_op jit(solution)/shard_map/ppermute | solution.py:222
  (182 shorter events, 153.9 us)
Async XLA Ops:
  8.6 15.6 %copy-start = (f32[512,8,128]{2,0,1:T(8,128)}, f32[512,8,128]{2,0,1:T(8,128)S(1)}, u32[]{:S(2)}) copy-start(f32[512,8,128]{2,0,1:T(8,128)S(1)} %copy.41) | copy-start | bytes 6291460
  17.7 358.2 %all-to-all-start = ((bf16[8,8,128,512]{3,2,1,0:T(8,128)(2,1)}), bf16[8,8,128,512]{3,2,1,0:T(8,128)(2,1)}, u32[]{:S(2)}, u32[]{:S(2)}) async-start(bf16[8,8,128,512]{3,2,1,0:T(8,128)(2,1)} %broadcast_in_dim.200), calls=%async_computation | async-start | bytes 16777216 | tf_op jit(solution)/shard_map/all_to_all | solution.py:121
  24.0 351.9 %all-gather.2.cloned.1.call-start = ((), (), s32[]{:S(2)}) async-start(), calls=%async_computation.1 | async-start | bytes 9437184 | tf_op jit(solution)/shard_map/all_gather | solution.py:176
  78.9 6.1 %copy-start.29 = (f32[8,128,128]{2,1,0:T(8,128)S(1)}, f32[8,128,128]{2,1,0:T(8,128)}, u32[]{:S(2)}) copy-start(f32[8,128,128]{2,1,0:T(8,128)} %get-tuple-element.360) | copy-start | bytes 1572868
  78.9 6.2 %copy-start.4 = (f32[8,256,256]{2,1,0:T(8,128)S(1)}, f32[8,256,256]{2,1,0:T(8,128)}, u32[]{:S(2)}) copy-start(f32[8,256,256]{2,1,0:T(8,128)} %fusion.176) | copy-start | bytes 6291460
  78.9 6.2 %copy-start.21 = (f32[8,128,128]{2,1,0:T(8,128)S(1)}, f32[8,128,128]{2,1,0:T(8,128)}, u32[]{:S(2)}) copy-start(f32[8,128,128]{2,1,0:T(8,128)} %convolution_negate_fusion) | copy-start | bytes 1572868
  78.9 6.2 %copy-start.28 = (f32[8,128,128]{2,1,0:T(8,128)S(1)}, f32[8,128,128]{2,1,0:T(8,128)}, u32[]{:S(2)}) copy-start(f32[8,128,128]{2,1,0:T(8,128)} %get-tuple-element.363) | copy-start | bytes 1572868
  111.5 17.5 %copy-start.33 = (s32[512]{0:T(512)S(1)}, s32[512]{0:T(512)}, u32[]{:S(2)}) copy-start(s32[512]{0:T(512)} %param.26) | copy-start | bytes 6148
  136.0 189.2 %collective-permute-start = (bf16[1032,128]{1,0:T(8,128)(2,1)}, bf16[1032,128]{1,0:T(8,128)(2,1)}, u32[]{:S(2)}, u32[]{:S(2)}) collective-permute-start(bf16[1032,128]{1,0:T(8,128)(2,1)} %concatenate.48), channel_id=1, source_target_pairs={{0,4},{4,8},{8,12},{12,16},{16,20},{20,24},{24,28},{1,5},{5,9},{9,... | collective-permute-start | bytes 792584 | tf_op jit(solution)/shard_map/ppermute | solution.py:181
  139.4 197.2 %collective-permute-start.1 = (bf16[1032,128]{1,0:T(8,128)(2,1)}, bf16[1032,128]{1,0:T(8,128)(2,1)}, u32[]{:S(2)}, u32[]{:S(2)}) collective-permute-start(bf16[1032,128]{1,0:T(8,128)(2,1)} %concatenate.48), channel_id=1, source_target_pairs={{0,8},{4,12},{8,16},{12,20},{16,24},{20,28},{1,9},{5,13},{9,17},{1... | collective-permute-start | bytes 792584 | tf_op jit(solution)/shard_map/ppermute | solution.py:181
  142.7 202.3 %collective-permute-start.2 = (bf16[1032,128]{1,0:T(8,128)(2,1)}, bf16[1032,128]{1,0:T(8,128)(2,1)}, u32[]{:S(2)}, u32[]{:S(2)}) collective-permute-start(bf16[1032,128]{1,0:T(8,128)(2,1)} %concatenate.48), channel_id=1, source_target_pairs={{0,12},{4,16},{8,20},{12,24},{16,28},{1,13},{5,17},{9,21},{13,25},... | collective-permute-start | bytes 792584 | tf_op jit(solution)/shard_map/ppermute | solution.py:181
  144.9 205.7 %collective-permute-start.3 = (bf16[1032,128]{1,0:T(8,128)(2,1)}, bf16[1032,128]{1,0:T(8,128)(2,1)}, u32[]{:S(2)}, u32[]{:S(2)}) collective-permute-start(bf16[1032,128]{1,0:T(8,128)(2,1)} %concatenate.48), channel_id=1, source_target_pairs={{0,16},{4,20},{8,24},{12,28},{1,17},{5,21},{9,25},{13,29},{2,18},{... | collective-permute-start | bytes 792584 | tf_op jit(solution)/shard_map/ppermute | solution.py:181
  147.0 204.7 %collective-permute-start.4 = (bf16[1032,128]{1,0:T(8,128)(2,1)}, bf16[1032,128]{1,0:T(8,128)(2,1)}, u32[]{:S(2)}, u32[]{:S(2)}) collective-permute-start(bf16[1032,128]{1,0:T(8,128)(2,1)} %concatenate.48), channel_id=1, source_target_pairs={{0,20},{4,24},{8,28},{1,21},{5,25},{9,29},{2,22},{6,26},{10,30},{3... | collective-permute-start | bytes 792584 | tf_op jit(solution)/shard_map/ppermute | solution.py:181
  159.0 18.5 %copy-start.1 = (bf16[512,8,128]{2,0,1:T(8,128)(2,1)S(1)}, bf16[512,8,128]{2,0,1:T(8,128)(2,1)}, u32[]{:S(2)}) copy-start(bf16[512,8,128]{2,0,1:T(8,128)(2,1)} %copy.55) | copy-start | bytes 3145732
  159.1 18.5 %copy-start.30 = (pred[512,512]{0,1:T(8,128)(4,1)S(1)}, pred[512,512]{0,1:T(8,128)(4,1)}, u32[]{:S(2)}) copy-start(pred[512,512]{0,1:T(8,128)(4,1)} %copy.57) | copy-start | bytes 786436
  177.5 5.4 %copy-start.20 = (bf16[512,1024]{1,0:T(8,128)(2,1)S(1)}, bf16[512,1024]{1,0:T(8,128)(2,1)}, u32[]{:S(2)}) copy-start(bf16[512,1024]{1,0:T(8,128)(2,1)} %param.23) | copy-start | bytes 3145732
  195.8 129.4 %copy-start.31 = (bf16[1032,128]{1,0:T(8,128)(2,1)S(1)}, bf16[1032,128]{1,0:T(8,128)(2,1)}, u32[]{:S(2)}) copy-start(bf16[1032,128]{1,0:T(8,128)(2,1)} %concatenate.48) | copy-start | bytes 792580
  325.2 36.4 %collective-permute-start.5 = (bf16[1032,128]{1,0:T(8,128)(2,1)S(1)}, bf16[1032,128]{1,0:T(8,128)(2,1)}, u32[]{:S(2)}, u32[]{:S(2)}) collective-permute-start(bf16[1032,128]{1,0:T(8,128)(2,1)S(1)} %copy-done.31), channel_id=1, source_target_pairs={{0,24},{4,28},{1,25},{5,29},{2,26},{6,30},{3,27},{7,31}} | collective-permute-start | bytes 792584 | tf_op jit(solution)/shard_map/ppermute | solution.py:181
  336.6 28.0 %collective-permute-start.6 = (bf16[1032,128]{1,0:T(8,128)(2,1)S(1)}, bf16[1032,128]{1,0:T(8,128)(2,1)}, u32[]{:S(2)}, u32[]{:S(2)}) collective-permute-start(bf16[1032,128]{1,0:T(8,128)(2,1)S(1)} %copy-done.31), channel_id=1, source_target_pairs={{0,28},{1,29},{2,30},{3,31}} | collective-permute-start | bytes 792584 | tf_op jit(solution)/shard_map/ppermute | solution.py:181
  381.0 4.4 copy-start.27
  392.4 4.4 copy-start.26
  404.3 4.4 copy-start.25
  442.8 4.4 collective-permute-start.7
  452.6 25.3 %collective-permute-start.8 = (bf16[128,4096]{1,0:T(8,128)(2,1)S(1)}, bf16[128,4096]{1,0:T(8,128)(2,1)S(1)}, u32[]{:S(2)}, u32[]{:S(2)}) collective-permute-start(bf16[128,4096]{1,0:T(8,128)(2,1)S(1)} %fusion.227), channel_id=1, source_target_pairs={{0,2},{1,3},{2,0},{3,1},{4,6},{5,7},{6,4},{7,5},{8,10},{9,11},{10,... | collective-permute-start | bytes 3145736 | tf_op jit(solution)/shard_map/ppermute | solution.py:222
  (11 other events, 24.2 us)
Sparse Core Ops, SparseCore 0:
  129.1 213.0 all-gather.1

commit v5 on v3

--- a/solution.py
+++ b/solution.py
@@ -170,7 +170,11 @@
         [transfer.reshape(head_count * head_width, head_width), doc_rows], axis=0
     ).astype(jnp.bfloat16)
     first_doc = doc_float[0]
-    every_key = lax.all_gather(keys_end, "ctx", axis=1, tiled=True)
+    half = head_count // 2 if head_count % 2 == 0 else head_count
+    head_groups = [(0, half), (half, head_count)] if half < head_count else [(0, head_count)]
+    every_keys = [
+        lax.all_gather(keys_end[lo:hi], "ctx", axis=1, tiled=True) for lo, hi in head_groups
+    ]
     is_live = jnp.bool_(True)
     steps = []
     for offset in range(1, ctx_count):
@@ -181,15 +185,20 @@
         is_live = is_live & (ctx_index - offset >= 0) & (key_docs[block_rows - 1] == first_doc)
         steps.append((offset, transfer_in, key_docs, is_live))
 
-    for offset, transfer_in, key_docs, step_live in steps:
-
-        def take(inner, offset=offset, transfer_in=transfer_in, key_docs=key_docs):
-            source = jnp.maximum(ctx_index - offset, 0)
-            value_pair = lax.dynamic_slice_in_dim(every_value, source * block_rows, block_rows, 2)
-            key_pair = lax.dynamic_slice_in_dim(every_key, source * block_rows, block_rows, 1)
-            return attend(inner, key_pair, value_pair, transfer_in, key_docs)
-
-        carried = lax.cond(step_live, take, lambda inner: inner, carried)
+    results = []
+    for (lo, hi), every_key in zip(head_groups, every_keys):
+        group = tuple(part[lo:hi] for part in carried)
+        for offset, transfer_in, key_docs, step_live in steps:
+
+            def take(inner, offset=offset, transfer_in=transfer_in, key_docs=key_docs, lo=lo, hi=hi, every_key=every_key):
+                source = jnp.maximum(ctx_index - offset, 0)
+                value_pair = lax.dynamic_slice_in_dim(every_value[lo:hi], source * block_rows, block_rows, 2)
+                key_pair = lax.dynamic_slice_in_dim(every_key, source * block_rows, block_rows, 1)
+                return attend(inner, key_pair, value_pair, transfer_in[lo:hi], key_docs)
+
+            group = lax.cond(step_live, take, lambda inner: inner, group)
+        results.append(group)
+    carried = tuple(jnp.concatenate(parts, axis=0) for parts in zip(*results))
     attended = (carried[3] / carried[2][..., None]).astype(jnp.bfloat16)
     token_rows = jnp.transpose(attended, (1, 0, 2)).reshape(block_rows, head_count * head_width)
     projected = jnp.dot(token_rows, out_weight, preferred_element_type=jnp.float32)

time: 427 us -> 459 us (1.075)
  matrix products: 181 us -> 199 us
  local copies, waits for them, and re-layouts: 41.8 us -> 52.3 us
  loops' own time: 13.9 us -> 18.8 us
    dot_general x4 -> x8, matrix products: 7.69 us -> 19.7 us  [attend(): turned = jnp.einsum('hqd,hde->hqe', turned, transfer_in, precision=highest)]
    slice x0 -> x13, local copies, waits for them, and re-layouts: none -> 7.77 us  [the longest x8 3.89 us: take(): every_value[lo:hi]]
    dot_general x4 -> x8, matrix products: 11.3 us -> 16.7 us  [attend(): jnp.einsum('hqd,hkd->hqk', turned.astype(jnp.bfloat16), key_pair, preferr...]
    dot_general x4 -> x8, matrix products: 17.4 us -> 22.4 us  [attend(): jnp.einsum('hqk,hdk->hqd', weights.astype(jnp.bfloat16), value_pair, pref...]
    another operation x7 -> x14, loops' own time: 13.9 us -> 18.8 us  [on_device(): group = lax.cond(step_live, take, lambda inner: inner, group)]
    all_gather x1 -> x2, waiting for transfers between devices: 67.8 us -> 67.3 us  [on_device(): lax.all_gather(keys_end[lo:hi], 'ctx', axis=1, tiled=True)]
  transfers between devices with their start and end apart: 11 -> 12, of which waited for: 4 -> 5; matrix products, arithmetic and copies ran while one was open for 42% -> 42% of each run, Pallas kernels for 0% -> 0%
where the time goes in v5:
time: 459 us; the launch traced here: 456 us
  matrix products  199 us (43%)
  waiting for transfers between devices  120 us (26%)
  local copies, waits for them, and re-layouts  52.3 us (11%)
  other arithmetic  29.5 us (6%)
  between operations  22.9 us (5%)
  loops' own time  18.8 us (4%)
  starting transfers between devices  13.3 us (3%)
    all_gather x2, waiting for transfers between devices, on_device(): lax.all_gather(keys_end[lo:hi], 'ctx', axis=1, tiled=True)  67.3 us
    all_gather x1, waiting for transfers between devices, on_device(): every_value = lax.all_gather(value_columns, 'ctx', axis=2, tiled=True)  24.6 us
    dot_general x1, matrix products, lower_solve(): return jnp.dot(unit_lower_inverse(strict_lower), right, precision=highest)  24.5 us
    ppermute x1, waiting for transfers between devices, scatter_sum(): lax.ppermute(outgoing.astype(jnp.bfloat16), 'head', pairs)  23.7 us
    dot_general x8, matrix products, attend(): jnp.einsum('hqk,hdk->hqd', weights.astype(jnp.bfloat16), value_pair, pref...  22.4 us
    dot_general x8, matrix products, attend(): turned = jnp.einsum('hqd,hde->hqe', turned, transfer_in, precision=highest)  19.7 us
    another operation x14, loops' own time, on_device(): group = lax.cond(step_live, take, lambda inner: inner, group)  18.8 us
    dot_general x1, matrix products, shard_operators(): jnp.dot(scaled_dots, key_solve, precision=highest)  18.2 us
  transfers between devices with their start and end apart: 12, of which 5 were waited for; matrix products, arithmetic and copies ran while one was open for 42% of the time, Pallas kernels for 0%

profile of v5, /device:TPU:16, one launch (start us, length us, event | category | flops | bytes accessed | tf_op | source)
XLA Modules:
  0.0 455.7 jit_solution(6530214347985753272)
XLA Ops:
  19.0 7.3 %multiply_select_fusion.1 = f32[8,512,512]{2,1,0:T(8,128)S(1)} fusion(f32[8,512]{1,0:T(8,128)S(1)} %multiply_bitcast_fusion, pred[512,512]{1,0:T(8,128)(4,1)S(1)} %iota_compare_fusion.4, f32[8,512,128]{2,1,0:T(8,128)S(1)} %broadcast_divide_fusion), kind=kOutput, calls=%fused_computation.352 | convolution fusion | flops 3225419776 | bytes 10764288 | tf_op jit(solution)/shard_map/vmap()/dot_general | solution.py:79
  64.4 6.1 %broadcast_select_fusion = f32[8,512,512]{2,1,0:T(8,128)} fusion(pred[512,512]{1,0:T(8,128)(4,1)S(1)} %iota_compare_fusion.4, f32[8,512,128]{2,1,0:T(8,128)S(1)} %broadcast_divide_fusion, bf16[512,8,128]{2,0,1:T(8,128)(2,1)S(1)} %copy.66), kind=kOutput, calls=%fused_computation.368 | convolution fusion | flops 3223322624 | bytes 11796480 | tf_op jit(solution)/shard_map/vmap()/dot_general | solution.py:81
  70.5 24.5 %fusion.304 = f32[8,512,640]{2,1,0:T(8,128)} fusion(f32[8,512,128]{2,1,0:T(8,128)S(1)} %broadcast_divide_fusion, f32[8,512,512]{2,1,0:T(8,128)} %broadcast_select_fusion, f32[8,256,256]{2,1,0:T(8,128)S(1)} %select_maximum_fusion.2, f32[8,128,128]{2,1,0:T(8,128)} %copy-done.34, f32[8,128,128]{2,1,0:T(8,128)S(1)} %convolution_negate_fusion, ...), kind=kOutput, calls=%fused_computation.332 | convolution fusion | flops 16121331712 | bytes 27262976 | tf_op jit(solution)/shard_map/vmap()/dot_general | solution.py:70
  95.0 17.0 %subtract_convert_fusion = bf16[8,512,128]{2,1,0:T(8,128)(2,1)} fusion(f32[8,512,128]{2,1,0:T(8,128)S(1)} %broadcast_divide_fusion, f32[8,512,640]{2,1,0:T(8,128)} %fusion.304, bf16[512,8,128]{2,0,1:T(8,128)(2,1)S(1)} %copy.66, f32[8,512]{1,0:T(8,128)S(1)} %multiply_bitcast_fusion), kind=kOutput, calls=%fused_computation.405 | convolution fusion | flops 3223322624 | bytes 12599296 | tf_op jit(solution)/shard_map/vmap()/dot_general | solution.py:86
  112.0 24.6 %all-gather.4.cloned.1.call-done = bf16[8,128,4096]{2,1,0:T(8,128)(2,1)} async-done(((bf16[8,128,512]{2,1,0:T(8,128)(2,1)}), bf16[8,128,4096]{2,1,0:T(8,128)(2,1)}) %all-gather.4.cloned.1.call-update) | async-done | bytes 8388624 | tf_op jit(solution)/shard_map/all_gather | solution.py:120
  139.6 5.6 %fusion.389 = bf16[8,128,128]{2,1,0:T(8,128)(2,1)S(1)} fusion(f32[8,512,128]{2,1,0:T(8,128)S(1)} %broadcast_divide_fusion, f32[8,512,640]{2,1,0:T(8,128)} %fusion.304, f32[8,512]{1,0:T(8,128)S(1)} %multiply_bitcast_fusion, f32[128,128]{1,0:T(8,128)S(1)} %get-tuple-element.731), kind=kOutput, calls=%fused_computation.425 | convolution fusion | flops 806092800 | bytes 4538368 | tf_op jit(solution)/shard_map/vmap()/dot_general | solution.py:87
  166.7 9.9 %convert_subtract_fusion = f32[8,512,128]{2,1,0:T(8,128)S(1)} fusion(f32[8,512,640]{2,1,0:T(8,128)} %fusion.304, f32[8,512,512]{1,2,0:T(8,128)S(1)} %fusion.394, f32[8,512]{1,0:T(8,128)S(1)} %multiply_bitcast_fusion, pred[512,512]{1,0:T(8,128)(4,1)S(1)} %iota_compare_fusion.3, bf16[512,8,128]{2,0,1:T(8,128)(2,1)S(1)} %copy.69), kind=kOutput, calls=%fused_computation.407 | convolution fusion | flops 3226468352 | bytes 13910016 | tf_op jit(solution)/shard_map/vmap()/dot_general | solution.py:95
  176.8 18.2 %fusion.321 = f32[8,512,512]{1,2,0:T(8,128)S(1)} fusion(f32[8,512,640]{2,1,0:T(8,128)} %fusion.304, f32[8,512,512]{1,2,0:T(8,128)S(1)} %fusion.394, f32[8,512]{1,0:T(8,128)S(1)} %multiply_bitcast_fusion, pred[512,512]{1,0:T(8,128)(4,1)S(1)} %iota_compare_fusion.3), kind=kOutput, calls=%fused_computation.355 | convolution fusion | flops 12889096192 | bytes 25444352 | tf_op jit(solution)/shard_map/vmap()/dot_general | solution.py:92
  232.0 11.2 %all-gather.8.cloned.1.call-done = bf16[4,4096,128]{2,1,0:T(8,128)(2,1)} async-done(((bf16[4,512,128]{2,1,0:T(8,128)(2,1)}), bf16[4,4096,128]{2,1,0:T(8,128)(2,1)}) %all-gather.8.cloned.1.call-update) | async-done | bytes 4194320 | tf_op jit(solution)/shard_map/all_gather | solution.py:176
  243.3 10.1 %conditional.21 = ((f32[4,512,128]{2,1,0:T(8,128)S(1)}, f32[4,512]{1,0:T(4,128)S(1)}, f32[4,512]{1,0:T(4,128)S(1)}, f32[4,512,128]{2,1,0:T(8,128)})) conditional(s32[]{:T(128)} %convert_element_type.215, (f32[4,512,128]{2,1,0:T(8,128)S(1)}, f32[4,512]{1,0:T(4,128)S(1)}, f32[4,512]{1,0:T(4,128)S(1)}, f32[4,512,128]{2,1,0:T(8,128)}) %tuple.106, ...), branch_computations={%region_31.32_spmd, %region_32.35_spmd} | conditional | flops 952111104 | bytes 64360596 | solution.py:199
  253.4 10.9 %conditional.22 = ((f32[4,512,128]{2,1,0:T(8,128)S(1)}, f32[4,512]{1,0:T(4,128)S(1)}, f32[4,512]{1,0:T(4,128)S(1)}, f32[4,512,128]{2,1,0:T(8,128)})) conditional(s32[]{:T(128)} %convert_element_type.214, (f32[4,512,128]{2,1,0:T(8,128)S(1)}, f32[4,512]{1,0:T(4,128)S(1)}, f32[4,512]{1,0:T(4,128)S(1)}, ...), branch_computations={%region_35.36_spmd, %region_36.39_spmd} | conditional | flops 952111104 | bytes 64360596 | solution.py:199
  264.3 56.0 %all-gather.6.cloned.1.call-done = bf16[4,4096,128]{2,1,0:T(8,128)(2,1)} async-done(((bf16[4,512,128]{2,1,0:T(8,128)(2,1)}), bf16[4,4096,128]{2,1,0:T(8,128)(2,1)}) %all-gather.6.cloned.1.call-update) | async-done | bytes 4194320 | tf_op jit(solution)/shard_map/all_gather | solution.py:176
  320.4 9.8 %conditional.14 = ((f32[4,512,128]{2,1,0:T(8,128)S(1)}, f32[4,512]{1,0:T(4,128)S(1)}, f32[4,512]{1,0:T(4,128)S(1)}, f32[4,512,128]{2,1,0:T(8,128)})) conditional(s32[]{:T(128)} %convert_element_type.215, (f32[4,512,128]{2,1,0:T(8,128)S(1)}, f32[4,512]{1,0:T(4,128)S(1)}, f32[4,512]{1,0:T(4,128)S(1)}, f32[4,512,128]{2,1,0:T(8,128)}) %tuple.96, ...), branch_computations={%region_3.4_spmd, %region_4.7_spmd} | conditional | flops 952111104 | bytes 72749248 | solution.py:199
  330.2 9.8 %conditional.15 = ((f32[4,512,128]{2,1,0:T(8,128)S(1)}, f32[4,512]{1,0:T(4,128)S(1)}, f32[4,512]{1,0:T(4,128)S(1)}, f32[4,512,128]{2,1,0:T(8,128)})) conditional(s32[]{:T(128)} %convert_element_type.214, (f32[4,512,128]{2,1,0:T(8,128)S(1)}, f32[4,512]{1,0:T(4,128)S(1)}, f32[4,512]{1,0:T(4,128)S(1)}, f32[4,512,128]{2,1,0:T(8,128)}) %get-tuple-element.837, ...), branch_computations={%region_7.8_spmd, %region_8.11_spmd} | conditional | flops 952111104 | bytes 72749248 | solution.py:199
  340.0 10.3 %conditional.23 = ((f32[4,512,128]{2,1,0:T(8,128)S(1)}, f32[4,512]{1,0:T(4,128)S(1)}, f32[4,512]{1,0:T(4,128)S(1)}, f32[4,512,128]{2,1,0:T(8,128)})) conditional(s32[]{:T(128)} %convert_element_type.213, (f32[4,512,128]{2,1,0:T(8,128)S(1)}, f32[4,512]{1,0:T(4,128)S(1)}, f32[4,512]{1,0:T(4,128)S(1)}, ...), branch_computations={%region_39.40_spmd, %region_40.43_spmd} | conditional | flops 952111104 | bytes 64360596 | solution.py:199
  350.3 9.8 %conditional.16 = ((f32[4,512,128]{2,1,0:T(8,128)S(1)}, f32[4,512]{1,0:T(4,128)S(1)}, f32[4,512]{1,0:T(4,128)S(1)}, f32[4,512,128]{2,1,0:T(8,128)})) conditional(s32[]{:T(128)} %convert_element_type.213, (f32[4,512,128]{2,1,0:T(8,128)S(1)}, f32[4,512]{1,0:T(4,128)S(1)}, f32[4,512]{1,0:T(4,128)S(1)}, ...), branch_computations={%region_11.12_spmd, %region_12.15_spmd} | conditional | flops 952111104 | bytes 72749248 | solution.py:199
  360.1 10.3 %conditional.24 = ((f32[4,512,128]{2,1,0:T(8,128)S(1)}, f32[4,512]{1,0:T(4,128)S(1)}, f32[4,512]{1,0:T(4,128)S(1)}, f32[4,512,128]{2,1,0:T(8,128)})) conditional(s32[]{:T(128)} %convert_element_type.212, (f32[4,512,128]{2,1,0:T(8,128)S(1)}, f32[4,512]{1,0:T(4,128)S(1)}, f32[4,512]{1,0:T(4,128)S(1)}, ...), branch_computations={%region_43.44_spmd, %region_44.47_spmd} | conditional | flops 952111104 | bytes 64360596 | solution.py:199
  366.6 3.8 fusion.227
  370.4 9.8 %conditional.17 = ((f32[4,512,128]{2,1,0:T(8,128)S(1)}, f32[4,512]{1,0:T(4,128)S(1)}, f32[4,512]{1,0:T(4,128)S(1)}, f32[4,512,128]{2,1,0:T(8,128)})) conditional(s32[]{:T(128)} %convert_element_type.212, (f32[4,512,128]{2,1,0:T(8,128)S(1)}, f32[4,512]{1,0:T(4,128)S(1)}, f32[4,512]{1,0:T(4,128)S(1)}, ...), branch_computations={%region_15.16_spmd, %region_16.19_spmd} | conditional | flops 952111104 | bytes 72749248 | solution.py:199
  380.6 7.2 %conditional.26 = ((f32[4,512,128]{2,1,0:T(8,128)S(1)}, f32[4,512]{1,0:T(4,128)S(1)}, f32[4,512]{1,0:T(4,128)S(1)}, f32[4,512,128]{2,1,0:T(8,128)})) conditional(s32[]{:T(128)} %convert_element_type.210, (f32[4,512,128]{2,1,0:T(8,128)S(1)}, f32[4,512]{1,0:T(4,128)S(1)}, f32[4,512]{1,0:T(4,128)S(1)}, ...), branch_computations={%region_51.52_spmd, %region_52.55_spmd} | conditional | flops 952111104 | bytes 64360596 | solution.py:199
  387.9 5.9 %conditional.27 = ((f32[4,512]{1,0:T(4,128)S(1)}, f32[4,512,128]{2,1,0:T(8,128)})) conditional(s32[]{:T(128)} %convert_element_type.209, (f32[4,512]{1,0:T(4,128)S(1)}, f32[4,512,128]{2,1,0:T(8,128)}) %tuple.113, (f32[512]{0:T(512)S(1)}, f32[512]{0:T(512)S(1)}, s32[]{:T(128)}, bf16[4,4096,128]{2,1,0:T(8,128)(2,1)}, f32[4,512,128]{2,1,0:T(8,128)S(1)}, ...), branch_computations={%region_55.56_spmd, %region_56.59_spmd} | conditional | flops 549457920 | bytes 59887748 | solution.py:199
  400.6 6.9 %fusion.316 = f32[2,2,128,4096]{3,2,1,0:T(8,128)S(1)} fusion(bf16[2,2,128,1024]{3,2,1,0:T(8,128)(2,1)S(1)} %dot_general.240, bf16[1024,4096]{1,0:T(8,128)(2,1)} %param.41), kind=kOutput, calls=%fused_computation.346 | convolution fusion | flops 4294967296 | bytes 17825792 | tf_op jit(solution)/shard_map/dot_general | solution.py:204
  411.2 4.2 collective-permute-done.7
  422.4 23.7 %collective-permute-done.8 = bf16[128,4096]{1,0:T(8,128)(2,1)S(1)} collective-permute-done((bf16[128,4096]{1,0:T(8,128)(2,1)S(1)}, bf16[128,4096]{1,0:T(8,128)(2,1)S(1)}, u32[]{:S(2)}, u32[]{:S(2)}) %collective-permute-start.8) | collective-permute-done | bytes 1048608 | tf_op jit(solution)/shard_map/ppermute | solution.py:228
  (259 shorter events, 199.0 us)
Async XLA Ops:
  6.5 130.1 %all-gather.4.cloned.1.call-start = ((), (), s32[]{:S(2)}) async-start(), calls=%async_computation | async-start | bytes 9437184 | tf_op jit(solution)/shard_map/all_gather | solution.py:120
  10.8 5.9 %copy-start.14 = (f32[512,8,128]{2,0,1:T(8,128)}, f32[512,8,128]{2,0,1:T(8,128)S(1)}, u32[]{:S(2)}) copy-start(f32[512,8,128]{2,0,1:T(8,128)S(1)} %copy.55) | copy-start | bytes 6291460
  10.9 5.8 %copy-start.36 = (f32[512,8]{0,1:T(8,128)S(1)}, f32[512,8]{0,1:T(8,128)}, u32[]{:S(2)}) copy-start(f32[512,8]{0,1:T(8,128)} %param.39) | copy-start | bytes 49156
  10.9 232.4 %all-gather.8.cloned.1.call-start = ((), (), s32[]{:S(2)}) async-start(), calls=%async_computation.2 | async-start | bytes 4718592 | tf_op jit(solution)/shard_map/all_gather | solution.py:176
  15.4 79.6 %copy-start.15 = (bf16[512,8,128]{2,0,1:T(8,128)(2,1)}, bf16[512,8,128]{2,0,1:T(8,128)(2,1)S(1)}, u32[]{:S(2)}) copy-start(bf16[512,8,128]{2,0,1:T(8,128)(2,1)S(1)} %copy.66) | copy-start | bytes 3145732
  55.2 7.0 %copy-start.34 = (f32[8,128,128]{2,1,0:T(8,128)}, f32[8,128,128]{2,1,0:T(8,128)S(1)}, u32[]{:S(2)}) copy-start(f32[8,128,128]{2,1,0:T(8,128)S(1)} %get-tuple-element.704) | copy-start | bytes 1572868
  95.0 44.6 %copy-start.37 = (s32[512]{0:T(512)S(1)}, s32[512]{0:T(512)}, u32[]{:S(2)}) copy-start(s32[512]{0:T(512)} %param.40) | copy-start | bytes 6148
  138.9 181.5 %all-gather.6.cloned.1.call-start = ((), (), s32[]{:S(2)}) async-start(), calls=%async_computation.1 | async-start | bytes 4718592 | tf_op jit(solution)/shard_map/all_gather | solution.py:176
  146.6 56.8 %collective-permute-start = (bf16[1032,128]{1,0:T(8,128)(2,1)}, bf16[1032,128]{1,0:T(8,128)(2,1)S(1)}, u32[]{:S(2)}, u32[]{:S(2)}) collective-permute-start(bf16[1032,128]{1,0:T(8,128)(2,1)} %concatenate.54), channel_id=1, source_target_pairs={{0,4},{4,8},{8,12},{12,16},{16,20},{20,24},{24,28},{1,5},{5,9},{9,... | collective-permute-start | bytes 792584 | tf_op jit(solution)/shard_map/ppermute | solution.py:182
  149.1 55.0 %collective-permute-start.1 = (bf16[1032,128]{1,0:T(8,128)(2,1)}, bf16[1032,128]{1,0:T(8,128)(2,1)}, u32[]{:S(2)}, u32[]{:S(2)}) collective-permute-start(bf16[1032,128]{1,0:T(8,128)(2,1)} %concatenate.54), channel_id=1, source_target_pairs={{0,8},{4,12},{8,16},{12,20},{16,24},{20,28},{1,9},{5,13},{9,17},{1... | collective-permute-start | bytes 792584 | tf_op jit(solution)/shard_map/ppermute | solution.py:182
  151.5 55.0 %collective-permute-start.2 = (bf16[1032,128]{1,0:T(8,128)(2,1)}, bf16[1032,128]{1,0:T(8,128)(2,1)}, u32[]{:S(2)}, u32[]{:S(2)}) collective-permute-start(bf16[1032,128]{1,0:T(8,128)(2,1)} %concatenate.54), channel_id=1, source_target_pairs={{0,12},{4,16},{8,20},{12,24},{16,28},{1,13},{5,17},{9,21},{13,25},... | collective-permute-start | bytes 792584 | tf_op jit(solution)/shard_map/ppermute | solution.py:182
  153.4 54.1 %collective-permute-start.3 = (bf16[1032,128]{1,0:T(8,128)(2,1)}, bf16[1032,128]{1,0:T(8,128)(2,1)}, u32[]{:S(2)}, u32[]{:S(2)}) collective-permute-start(bf16[1032,128]{1,0:T(8,128)(2,1)} %concatenate.54), channel_id=1, source_target_pairs={{0,16},{4,20},{8,24},{12,28},{1,17},{5,21},{9,25},{13,29},{2,18},{... | collective-permute-start | bytes 792584 | tf_op jit(solution)/shard_map/ppermute | solution.py:182
  154.7 53.8 %collective-permute-start.4 = (bf16[1032,128]{1,0:T(8,128)(2,1)}, bf16[1032,128]{1,0:T(8,128)(2,1)}, u32[]{:S(2)}, u32[]{:S(2)}) collective-permute-start(bf16[1032,128]{1,0:T(8,128)(2,1)} %concatenate.54), channel_id=1, source_target_pairs={{0,20},{4,24},{8,28},{1,21},{5,25},{9,29},{2,22},{6,26},{10,30},{3... | collective-permute-start | bytes 792584 | tf_op jit(solution)/shard_map/ppermute | solution.py:182
  160.0 6.7 %copy-start.17 = (bf16[512,8,128]{2,0,1:T(8,128)(2,1)}, bf16[512,8,128]{2,0,1:T(8,128)(2,1)S(1)}, u32[]{:S(2)}) copy-start(bf16[512,8,128]{2,0,1:T(8,128)(2,1)S(1)} %copy.69) | copy-start | bytes 3145732
  176.7 18.2 %copy-start.16 = (bf16[512,8,128]{2,0,1:T(8,128)(2,1)S(1)}, bf16[512,8,128]{2,0,1:T(8,128)(2,1)}, u32[]{:S(2)}) copy-start(bf16[512,8,128]{2,0,1:T(8,128)(2,1)} %copy-done.15) | copy-start | bytes 3145732
  176.8 18.2 %copy-start.35 = (pred[512,512]{0,1:T(8,128)(4,1)S(1)}, pred[512,512]{0,1:T(8,128)(4,1)}, u32[]{:S(2)}) copy-start(pred[512,512]{0,1:T(8,128)(4,1)} %copy.71) | copy-start | bytes 786436
  203.4 15.4 %collective-permute-start.5 = (bf16[1032,128]{1,0:T(8,128)(2,1)}, bf16[1032,128]{1,0:T(8,128)(2,1)S(1)}, u32[]{:S(2)}, u32[]{:S(2)}) collective-permute-start(bf16[1032,128]{1,0:T(8,128)(2,1)} %concatenate.54), channel_id=1, source_target_pairs={{0,24},{4,28},{1,25},{5,29},{2,26},{6,30},{3,27},{7,31}} | collective-permute-start | bytes 792584 | tf_op jit(solution)/shard_map/ppermute | solution.py:182
  204.1 16.5 %collective-permute-start.6 = (bf16[1032,128]{1,0:T(8,128)(2,1)}, bf16[1032,128]{1,0:T(8,128)(2,1)}, u32[]{:S(2)}, u32[]{:S(2)}) collective-permute-start(bf16[1032,128]{1,0:T(8,128)(2,1)} %concatenate.54), channel_id=1, source_target_pairs={{0,28},{1,29},{2,30},{3,31}} | collective-permute-start | bytes 792584 | tf_op jit(solution)/shard_map/ppermute | solution.py:182
  243.6 5.5 %copy-start = (bf16[8,128,4096]{2,1,0:T(8,128)(2,1)S(1)}, bf16[8,128,4096]{2,1,0:T(8,128)(2,1)}, u32[]{:S(2)}) copy-start(bf16[8,128,4096]{2,1,0:T(8,128)(2,1)} %get-tuple-element.463) | copy-start | bytes 25165828 | tf_op jit(solution)/shard_map/cond
  253.7 5.9 %copy-start.1 = (bf16[8,128,4096]{2,1,0:T(8,128)(2,1)S(1)}, bf16[8,128,4096]{2,1,0:T(8,128)(2,1)}, u32[]{:S(2)}) copy-start(bf16[8,128,4096]{2,1,0:T(8,128)(2,1)} %get-tuple-element.473) | copy-start | bytes 25165828 | tf_op jit(solution)/shard_map/cond
  340.4 5.5 %copy-start.4 = (bf16[8,128,4096]{2,1,0:T(8,128)(2,1)S(1)}, bf16[8,128,4096]{2,1,0:T(8,128)(2,1)}, u32[]{:S(2)}) copy-start(bf16[8,128,4096]{2,1,0:T(8,128)(2,1)} %get-tuple-element.483) | copy-start | bytes 25165828 | tf_op jit(solution)/shard_map/cond
  387.9 6.0 %copy-start.33 = (f32[4,512,128]{2,1,0:T(8,128)S(1)}, f32[4,512,128]{2,1,0:T(8,128)}, u32[]{:S(2)}) copy-start(f32[4,512,128]{2,1,0:T(8,128)} %get-tuple-element.604) | copy-start | bytes 3145732
  411.0 4.4 collective-permute-start.7
  420.9 25.3 %collective-permute-start.8 = (bf16[128,4096]{1,0:T(8,128)(2,1)S(1)}, bf16[128,4096]{1,0:T(8,128)(2,1)S(1)}, u32[]{:S(2)}, u32[]{:S(2)}) collective-permute-start(bf16[128,4096]{1,0:T(8,128)(2,1)S(1)} %fusion.392), channel_id=1, source_target_pairs={{0,2},{1,3},{2,0},{3,1},{4,6},{5,7},{6,4},{7,5},{8,10},{9,11},{10,... | collective-permute-start | bytes 3145736 | tf_op jit(solution)/shard_map/ppermute | solution.py:228
  (16 other events, 45.0 us)
Sparse Core Ops, SparseCore 0:
  11.0 125.5 all-gather.3
  139.0 104.2 all-gather.7
  245.5 74.8 all-gather.5

commit v6 on v3

--- a/solution.py
+++ b/solution.py
@@ -192,24 +192,36 @@
         carried = lax.cond(step_live, take, lambda inner: inner, carried)
     attended = (carried[3] / carried[2][..., None]).astype(jnp.bfloat16)
     token_rows = jnp.transpose(attended, (1, 0, 2)).reshape(block_rows, head_count * head_width)
-    projected = jnp.dot(token_rows, out_weight, preferred_element_type=jnp.float32)
-    return scatter_sum(projected).astype(jnp.bfloat16)
-
-
-def scatter_sum(projected):
+    return scatter_sum(token_rows, out_weight).astype(jnp.bfloat16)
+
+
+def scatter_sum(token_rows, out_weight):
     head_count = lax.axis_size("head")
     if head_count % 2:
+        projected = jnp.dot(token_rows, out_weight, preferred_element_type=jnp.float32)
         return lax.psum_scatter(projected, "head", scatter_dimension=0, tiled=True)
     chips = head_count // 2
-    rows = projected.shape[0] // head_count
+    rows = token_rows.shape[0] // head_count
     head_index = lax.axis_index("head")
     core = head_index % 2
     chip = head_index // 2
-    grouped = projected.reshape(chips, 2, rows, projected.shape[1])
-    mine = lax.dynamic_index_in_dim(grouped, core, 1, keepdims=False)
-    other = lax.dynamic_index_in_dim(grouped, 1 - core, 1, keepdims=False)
+    grouped = token_rows.reshape(chips, 2, rows, token_rows.shape[1])
+    other = jnp.einsum(
+        "crk,kf->crf",
+        lax.dynamic_index_in_dim(grouped, 1 - core, 1, keepdims=False),
+        out_weight,
+        preferred_element_type=jnp.float32,
+    )
     partner = [(h, h ^ 1) for h in range(head_count)]
-    chip_sum = mine + lax.ppermute(other.astype(jnp.bfloat16), "head", partner).astype(jnp.float32)
+    received = lax.ppermute(other.astype(jnp.bfloat16), "head", partner)
+    mine = jnp.einsum(
+        "crk,kf->crf",
+        lax.dynamic_index_in_dim(grouped, core, 1, keepdims=False),
+        out_weight,
+        preferred_element_type=jnp.float32,
+    )
+    mine, received = lax.optimization_barrier((mine, received))
+    chip_sum = mine + received.astype(jnp.float32)
     total = lax.dynamic_index_in_dim(chip_sum, chip, 0, keepdims=False)
     for shift in range(1, chips):
         pairs = [

time: 427 us -> 426 us (level)
  matrix products: 181 us -> 187 us
    dot_general x1 -> x2, matrix products: 6.9 us -> 12.8 us  [the longest x1 7.08 us: scatter_sum(): jnp.einsum('crk,kf->crf', lax.dynamic_index_in_dim(grouped, 1 - core, 1,...]
    unnamed x28 -> x26, local copies, waits for them, and re-layouts: 13.3 us -> 10.1 us
  transfers between devices with their start and end apart: 11 -> 11, of which waited for: 4 -> 3; matrix products, arithmetic and copies ran while one was open for 42% -> 43% of each run, Pallas kernels for 0% -> 0%
where the time goes in v6:
time: 426 us; the launch traced here: 422 us
  matrix products  187 us (44%)
  waiting for transfers between devices  116 us (27%)
  local copies, waits for them, and re-layouts  38.4 us (9%)
  other arithmetic  28.3 us (7%)
  between operations  23.9 us (6%)
  loops' own time  14.9 us (3%)
  starting transfers between devices  13.7 us (3%)
    all_gather x1, waiting for transfers between devices, on_device(): every_key = lax.all_gather(keys_end, 'ctx', axis=1, tiled=True)  67.2 us
    all_gather x1, waiting for transfers between devices, on_device(): every_value = lax.all_gather(value_columns, 'ctx', axis=2, tiled=True)  24.3 us
    dot_general x1, matrix products, lower_solve(): return jnp.dot(unit_lower_inverse(strict_lower), right, precision=highest)  24.3 us
    ppermute x1, waiting for transfers between devices, scatter_sum(): lax.ppermute(outgoing.astype(jnp.bfloat16), 'head', pairs)  24.1 us
    dot_general x1, matrix products, shard_operators(): jnp.dot(scaled_dots, key_solve, precision=highest)  18.4 us
    dot_general x1, matrix products, shard_operators(): jnp.dot(key_solve.T, weighted, precision=highest)  17.5 us
    dot_general x4, matrix products, attend(): jnp.einsum('hqk,hdk->hqd', weights.astype(jnp.bfloat16), value_pair, pref...  17.4 us
    another operation x7, loops' own time, on_device(): carried = lax.cond(step_live, take, lambda inner: inner, carried)  14.9 us
  transfers between devices with their start and end apart: 11, of which 3 were waited for; matrix products, arithmetic and copies ran while one was open for 43% of the time, Pallas kernels for 0%

profile of v6, /device:TPU:16, one launch (start us, length us, event | category | flops | bytes accessed | tf_op | source)
XLA Modules:
  0.0 421.7 jit_solution(6092170109194587536)
XLA Ops:
  18.1 7.3 %multiply_select_fusion.1 = f32[8,512,512]{2,1,0:T(8,128)S(1)} fusion(f32[8,512]{1,0:T(8,128)S(1)} %multiply_bitcast_fusion, pred[512,512]{1,0:T(8,128)(4,1)S(1)} %iota_compare_fusion.4, f32[8,512,128]{2,1,0:T(8,128)S(1)} %broadcast_divide_fusion), kind=kOutput, calls=%fused_computation.176 | convolution fusion | flops 3225419776 | bytes 10764288 | tf_op jit(solution)/shard_map/vmap()/dot_general | solution.py:79
  63.5 6.1 %broadcast_select_fusion = f32[8,512,512]{2,1,0:T(8,128)} fusion(pred[512,512]{1,0:T(8,128)(4,1)S(1)} %iota_compare_fusion.4, f32[8,512,128]{2,1,0:T(8,128)S(1)} %broadcast_divide_fusion, bf16[512,8,128]{2,0,1:T(8,128)(2,1)S(1)} %copy.52), kind=kOutput, calls=%fused_computation.192 | convolution fusion | flops 3223322624 | bytes 11796480 | tf_op jit(solution)/shard_map/vmap()/dot_general | solution.py:81
  69.6 24.3 %fusion.133 = f32[8,512,640]{2,1,0:T(8,128)} fusion(f32[8,512,128]{2,1,0:T(8,128)S(1)} %broadcast_divide_fusion, f32[8,512,512]{2,1,0:T(8,128)} %broadcast_select_fusion, f32[8,256,256]{2,1,0:T(8,128)S(1)} %select_maximum_fusion.2, f32[8,128,128]{2,1,0:T(8,128)} %copy-done.24, f32[8,128,128]{2,1,0:T(8,128)S(1)} %convolution_negate_fusion, ...), kind=kOutput, calls=%fused_computation.154 | convolution fusion | flops 16121331712 | bytes 27262976 | tf_op jit(solution)/shard_map/vmap()/dot_general | solution.py:70
  93.9 17.5 %subtract_convert_fusion = bf16[8,512,128]{2,1,0:T(8,128)(2,1)} fusion(f32[8,512,128]{2,1,0:T(8,128)S(1)} %broadcast_divide_fusion, f32[8,512,640]{2,1,0:T(8,128)} %fusion.133, bf16[512,8,128]{2,0,1:T(8,128)(2,1)S(1)} %copy.52, f32[8,512]{1,0:T(8,128)S(1)} %multiply_bitcast_fusion), kind=kOutput, calls=%fused_computation.227 | convolution fusion | flops 3223322624 | bytes 12599296 | tf_op jit(solution)/shard_map/vmap()/dot_general | solution.py:86
  111.4 24.3 %all-gather.3.cloned.1.call-done = bf16[8,128,4096]{2,1,0:T(8,128)(2,1)} async-done(((bf16[8,128,512]{2,1,0:T(8,128)(2,1)}), bf16[8,128,4096]{2,1,0:T(8,128)(2,1)}) %all-gather.3.cloned.1.call-update) | async-done | bytes 8388624 | tf_op jit(solution)/shard_map/all_gather | solution.py:120
  135.8 5.6 %fusion.221 = bf16[8,128,128]{2,1,0:T(8,128)(2,1)S(1)} fusion(f32[8,512,128]{2,1,0:T(8,128)S(1)} %broadcast_divide_fusion, f32[8,512,640]{2,1,0:T(8,128)} %fusion.133, f32[8,512]{1,0:T(8,128)S(1)} %multiply_bitcast_fusion, f32[128,128]{1,0:T(8,128)S(1)} %get-tuple-element.388), kind=kOutput, calls=%fused_computation.247 | convolution fusion | flops 806092800 | bytes 4538368 | tf_op jit(solution)/shard_map/vmap()/dot_general | solution.py:87
  159.7 4.8 %fusion.226 = f32[8,512,512]{1,2,0:T(8,128)S(1)} fusion(f32[8,512,128]{2,1,0:T(8,128)S(1)} %broadcast_divide_fusion, bf16[512,8,128]{2,0,1:T(8,128)(2,1)} %copy.55), kind=kOutput, calls=%fused_computation.250 | convolution fusion | flops 3221225472 | bytes 11534336 | tf_op jit(solution)/shard_map/vmap()/dot_general | solution.py:90
  164.6 18.4 %fusion.152 = f32[8,512,512]{1,2,0:T(8,128)} fusion(f32[8,512,640]{2,1,0:T(8,128)} %fusion.133, f32[8,512,512]{1,2,0:T(8,128)S(1)} %fusion.226, f32[8,512]{1,0:T(8,128)S(1)} %multiply_bitcast_fusion, pred[512,512]{1,0:T(8,128)(4,1)S(1)} %iota_compare_fusion.3), kind=kOutput, calls=%fused_computation.179 | convolution fusion | flops 12889096192 | bytes 25444352 | tf_op jit(solution)/shard_map/vmap()/dot_general | solution.py:92
  183.0 5.3 %fusion.256 = (f32[8,512]{1,0:T(8,128)S(1)}, f32[8,512,512]{1,2,0:T(8,128)S(1)}) fusion(f32[8,512,512]{1,2,0:T(8,128)} %fusion.152, bf16[512,8,128]{2,0,1:T(8,128)(2,1)S(1)} %copy.52, bf16[512,8,128]{2,0,1:T(8,128)(2,1)S(1)} %copy-done.1, pred[512,512]{0,1:T(8,128)(4,1)S(1)} %copy-done.25), kind=kOutput, calls=%fused_computation.351 | convolution fusion | flops 545255424 | bytes 19152896 | tf_op jit(solution)/shard_map/vmap()/dot_general | solution.py:92
  191.6 9.6 %convert_subtract_fusion = f32[8,512,128]{2,1,0:T(8,128)S(1)} fusion(f32[8,512,640]{2,1,0:T(8,128)} %fusion.133, f32[8,512,512]{1,2,0:T(8,128)S(1)} %fusion.226, f32[8,512]{1,0:T(8,128)S(1)} %multiply_bitcast_fusion, pred[512,512]{1,0:T(8,128)(4,1)S(1)} %iota_compare_fusion.3, bf16[512,8,128]{2,0,1:T(8,128)(2,1)S(1)} %copy-done.2), kind=kOutput, calls=%fused_computation.229 | convolution fusion | flops 3226468352 | bytes 13910016 | tf_op jit(solution)/shard_map/vmap()/dot_general | solution.py:95
  233.3 67.2 %all-gather.5.cloned.1.call-done = bf16[8,4096,128]{2,1,0:T(8,128)(2,1)} async-done(((bf16[8,512,128]{2,1,0:T(8,128)(2,1)}), bf16[8,4096,128]{2,1,0:T(8,128)(2,1)}) %all-gather.5.cloned.1.call-update) | async-done | bytes 8388624 | tf_op jit(solution)/shard_map/all_gather | solution.py:173
  300.5 12.7 %conditional.7 = ((f32[8,512,128]{2,1,0:T(8,128)S(1)}, f32[8,512]{1,0:T(8,128)S(1)}, f32[8,512]{1,0:T(8,128)S(1)}, f32[8,512,128]{2,1,0:T(8,128)})) conditional(s32[]{:T(128)} %convert_element_type.163, (f32[8,512,128]{2,1,0:T(8,128)S(1)}, f32[8,512]{1,0:T(8,128)S(1)}, f32[8,512]{1,0:T(8,128)S(1)}, f32[8,512,128]{2,1,0:T(8,128)}) %tuple.53, ...), branch_computations={%region_3.4_spmd, %region_4.7_spmd} | conditional | flops 1903960064 | bytes 62656712 | solution.py:192
  305.5 4.4 %multiply_add_fusion = f32[8,512,128]{2,1,0:T(8,128)S(1)} fusion(f32[8,512,128]{2,1,0:T(8,128)S(1)} %copy-done.5, f32[8,512,512]{2,1,0:T(8,128)S(1)} %get-tuple-element.347, f32[8,512]{1,0:T(8,128)S(1)} %max.29, pred[512,512]{0,1:T(8,128)(4,1)S(1)} %broadcast_compare_fusion, bf16[8,128,4096]{2,1,0:T(8,128)(2,1)} %get-tuple-element.206, s32[]{:T(128)S(6)} %select_n.248, ...), kind=kOutput, calls=%fused_computation.10 | convolution fusion | flops 546308096 | bytes 13926404 | tf_op jit(solution)/shard_map/cond/branch_1_fun/hqk,hdk->hqd/dot_general | solution.py:156
  313.1 13.1 %conditional.8 = ((f32[8,512,128]{2,1,0:T(8,128)S(1)}, f32[8,512]{1,0:T(8,128)S(1)}, f32[8,512]{1,0:T(8,128)S(1)}, f32[8,512,128]{2,1,0:T(8,128)})) conditional(s32[]{:T(128)} %convert_element_type.162, (f32[8,512,128]{2,1,0:T(8,128)S(1)}, f32[8,512]{1,0:T(8,128)S(1)}, f32[8,512]{1,0:T(8,128)S(1)}, f32[8,512,128]{2,1,0:T(8,128)}) %get-tuple-element.442, ...), branch_computations={%region_7.8_spmd, %region_8.11_spmd} | conditional | flops 1903960064 | bytes 62656712 | solution.py:192
  318.2 4.4 %multiply_add_fusion.2 = f32[8,512,128]{2,1,0:T(8,128)S(1)} fusion(f32[8,512,128]{2,1,0:T(8,128)S(1)} %copy-done.7, f32[8,512,512]{2,1,0:T(8,128)S(1)} %get-tuple-element.349, f32[8,512]{1,0:T(8,128)S(1)} %max.31, pred[512,512]{0,1:T(8,128)(4,1)S(1)} %broadcast_compare_fusion.1, bf16[8,128,4096]{2,1,0:T(8,128)(2,1)} %get-tuple-element.216, ...), kind=kOutput, calls=%fused_computation.32 | convolution fusion | flops 546308096 | bytes 13926404 | tf_op jit(solution)/shard_map/cond/branch_1_fun/hqk,hdk->hqd/dot_general | solution.py:156
  326.2 12.7 %conditional.9 = ((f32[8,512,128]{2,1,0:T(8,128)S(1)}, f32[8,512]{1,0:T(8,128)S(1)}, f32[8,512]{1,0:T(8,128)S(1)}, f32[8,512,128]{2,1,0:T(8,128)})) conditional(s32[]{:T(128)} %convert_element_type.161, (f32[8,512,128]{2,1,0:T(8,128)S(1)}, f32[8,512]{1,0:T(8,128)S(1)}, f32[8,512]{1,0:T(8,128)S(1)}, ...), branch_computations={%region_11.12_spmd, %region_12.15_spmd} | conditional | flops 1903960064 | bytes 62656712 | solution.py:192
  331.3 4.4 %multiply_add_fusion.4 = f32[8,512,128]{2,1,0:T(8,128)S(1)} fusion(f32[8,512,128]{2,1,0:T(8,128)S(1)} %copy-done.9, f32[8,512,512]{2,1,0:T(8,128)S(1)} %get-tuple-element.351, f32[8,512]{1,0:T(8,128)S(1)} %max.33, pred[512,512]{0,1:T(8,128)(4,1)S(1)} %broadcast_compare_fusion.2, bf16[8,128,4096]{2,1,0:T(8,128)(2,1)} %get-tuple-element.226, ...), kind=kOutput, calls=%fused_computation.54 | convolution fusion | flops 546308096 | bytes 13926404 | tf_op jit(solution)/shard_map/cond/branch_1_fun/hqk,hdk->hqd/dot_general | solution.py:156
  338.9 12.9 %conditional.10 = ((f32[8,512,128]{2,1,0:T(8,128)S(1)}, f32[8,512]{1,0:T(8,128)S(1)}, f32[8,512]{1,0:T(8,128)S(1)}, f32[8,512,128]{2,1,0:T(8,128)})) conditional(s32[]{:T(128)} %convert_element_type.160, (f32[8,512,128]{2,1,0:T(8,128)S(1)}, f32[8,512]{1,0:T(8,128)S(1)}, f32[8,512]{1,0:T(8,128)S(1)}, ...), branch_computations={%region_15.16_spmd, %region_16.19_spmd} | conditional | flops 1903960064 | bytes 62656712 | solution.py:192
  344.1 4.4 %multiply_add_fusion.6 = f32[8,512,128]{2,1,0:T(8,128)S(1)} fusion(f32[8,512,128]{2,1,0:T(8,128)S(1)} %copy-done.11, f32[8,512,512]{2,1,0:T(8,128)S(1)} %get-tuple-element.353, f32[8,512]{1,0:T(8,128)S(1)} %max.35, pred[512,512]{0,1:T(8,128)(4,1)S(1)} %broadcast_compare_fusion.3, bf16[8,128,4096]{2,1,0:T(8,128)(2,1)} %get-tuple-element.236, ...), kind=kOutput, calls=%fused_computation.76 | convolution fusion | flops 546308096 | bytes 13926404 | tf_op jit(solution)/shard_map/cond/branch_1_fun/hqk,hdk->hqd/dot_general | solution.py:156
  352.0 5.6 %conditional.12 = ((f32[8,512,128]{2,1,0:T(8,128)S(1)}, f32[8,512]{1,0:T(8,128)S(1)}, f32[8,512]{1,0:T(8,128)S(1)}, f32[8,512,128]{2,1,0:T(8,128)})) conditional(s32[]{:T(128)} %convert_element_type.158, (f32[8,512,128]{2,1,0:T(8,128)S(1)}, f32[8,512]{1,0:T(8,128)S(1)}, f32[8,512]{1,0:T(8,128)S(1)}, ...), branch_computations={%region_23.24_spmd, %region_24.27_spmd} | conditional | flops 1903960064 | bytes 61608112 | solution.py:192
  357.6 8.1 %conditional.13 = ((f32[8,512]{1,0:T(8,128)S(1)}, f32[8,512,128]{2,1,0:T(8,128)})) conditional(s32[]{:T(128)} %convert_element_type.157, (f32[8,512]{1,0:T(8,128)S(1)}, f32[8,512,128]{2,1,0:T(8,128)}) %tuple.61, (f32[512]{0:T(512)S(1)}, f32[512]{0:T(512)S(1)}, s32[]{:T(128)}, bf16[8,4096,128]{2,1,0:T(8,128)(2,1)}, f32[8,512,128]{2,1,0:T(8,128)S(1)}, ...), branch_computations={%region_27.28_spmd, %region_28.31_spmd} | conditional | flops 1098653696 | bytes 51613852 | solution.py:192
  368.9 7.1 %fusion.159 = bf16[2,128,4096]{2,1,0:T(8,128)(2,1)} fusion(bf16[1024,4096]{1,0:T(8,128)(2,1)} %param.27, bf16[2,2,128,1024]{3,2,1,0:T(8,128)(2,1)S(1)} %reshape_reshape.3, s32[]{:T(128)S(6)} %select_n.311), kind=kOutput, calls=%fused_computation.184 | convolution fusion | flops 2148532224 | bytes 11010052 | tf_op jit(solution)/shard_map/crk,kf->crf/dot_general | solution.py:209
  376.0 5.7 %fusion.147 = f32[2,128,4096]{2,1,0:T(8,128)S(1)} fusion(bf16[1024,4096]{1,0:T(8,128)(2,1)} %param.27, bf16[2,2,128,1024]{3,2,1,0:T(8,128)(2,1)S(1)} %reshape_reshape.3, s32[]{:T(128)S(6)} %select_n.310), kind=kOutput, calls=%fused_computation.170 | convolution fusion | flops 2147483648 | bytes 13107204 | tf_op jit(solution)/shard_map/crk,kf->crf/dot_general | solution.py:217
  387.7 24.1 %collective-permute-done.8 = bf16[128,4096]{1,0:T(8,128)(2,1)S(1)} collective-permute-done((bf16[128,4096]{1,0:T(8,128)(2,1)S(1)}, bf16[128,4096]{1,0:T(8,128)(2,1)S(1)}, u32[]{:S(2)}, u32[]{:S(2)}) %collective-permute-start.8) | collective-permute-done | bytes 1048608 | tf_op jit(solution)/shard_map/ppermute | solution.py:231
  (188 shorter events, 138.3 us)
Async XLA Ops:
  6.5 2.4 copy-start.26
  6.5 129.2 %all-gather.3.cloned.1.call-start = ((), (), s32[]{:S(2)}) async-start(), calls=%async_computation | async-start | bytes 9437184 | tf_op jit(solution)/shard_map/all_gather | solution.py:120
  10.0 4.8 %copy-start = (f32[512,8,128]{2,0,1:T(8,128)}, f32[512,8,128]{2,0,1:T(8,128)S(1)}, u32[]{:S(2)}) copy-start(f32[512,8,128]{2,0,1:T(8,128)S(1)} %copy.41) | copy-start | bytes 6291460
  10.0 290.5 %all-gather.5.cloned.1.call-start = ((), (), s32[]{:S(2)}) async-start(), calls=%async_computation.1 | async-start | bytes 9437184 | tf_op jit(solution)/shard_map/all_gather | solution.py:173
  13.0 2.9 copy-start.28
  54.4 7.0 %copy-start.24 = (f32[8,128,128]{2,1,0:T(8,128)}, f32[8,128,128]{2,1,0:T(8,128)S(1)}, u32[]{:S(2)}) copy-start(f32[8,128,128]{2,1,0:T(8,128)S(1)} %get-tuple-element.367) | copy-start | bytes 1572868
  93.9 41.9 %copy-start.29 = (s32[512]{0:T(512)S(1)}, s32[512]{0:T(512)}, u32[]{:S(2)}) copy-start(s32[512]{0:T(512)} %param.26) | copy-start | bytes 6148
  142.8 60.4 %collective-permute-start = (bf16[1032,128]{1,0:T(8,128)(2,1)}, bf16[1032,128]{1,0:T(8,128)(2,1)S(1)}, u32[]{:S(2)}, u32[]{:S(2)}) collective-permute-start(bf16[1032,128]{1,0:T(8,128)(2,1)} %concatenate.48), channel_id=1, source_target_pairs={{0,4},{4,8},{8,12},{12,16},{16,20},{20,24},{24,28},{1,5},{5,9},{9,... | collective-permute-start | bytes 792584 | tf_op jit(solution)/shard_map/ppermute | solution.py:178
  145.2 59.3 %collective-permute-start.1 = (bf16[1032,128]{1,0:T(8,128)(2,1)}, bf16[1032,128]{1,0:T(8,128)(2,1)}, u32[]{:S(2)}, u32[]{:S(2)}) collective-permute-start(bf16[1032,128]{1,0:T(8,128)(2,1)} %concatenate.48), channel_id=1, source_target_pairs={{0,8},{4,12},{8,16},{12,20},{16,24},{20,28},{1,9},{5,13},{9,17},{1... | collective-permute-start | bytes 792584 | tf_op jit(solution)/shard_map/ppermute | solution.py:178
  147.6 59.3 %collective-permute-start.2 = (bf16[1032,128]{1,0:T(8,128)(2,1)}, bf16[1032,128]{1,0:T(8,128)(2,1)}, u32[]{:S(2)}, u32[]{:S(2)}) collective-permute-start(bf16[1032,128]{1,0:T(8,128)(2,1)} %concatenate.48), channel_id=1, source_target_pairs={{0,12},{4,16},{8,20},{12,24},{16,28},{1,13},{5,17},{9,21},{13,25},... | collective-permute-start | bytes 792584 | tf_op jit(solution)/shard_map/ppermute | solution.py:178
  149.6 58.4 %collective-permute-start.3 = (bf16[1032,128]{1,0:T(8,128)(2,1)}, bf16[1032,128]{1,0:T(8,128)(2,1)}, u32[]{:S(2)}, u32[]{:S(2)}) collective-permute-start(bf16[1032,128]{1,0:T(8,128)(2,1)} %concatenate.48), channel_id=1, source_target_pairs={{0,16},{4,20},{8,24},{12,28},{1,17},{5,21},{9,25},{13,29},{2,18},{... | collective-permute-start | bytes 792584 | tf_op jit(solution)/shard_map/ppermute | solution.py:178
  150.9 58.1 %collective-permute-start.4 = (bf16[1032,128]{1,0:T(8,128)(2,1)}, bf16[1032,128]{1,0:T(8,128)(2,1)}, u32[]{:S(2)}, u32[]{:S(2)}) collective-permute-start(bf16[1032,128]{1,0:T(8,128)(2,1)} %concatenate.48), channel_id=1, source_target_pairs={{0,20},{4,24},{8,28},{1,21},{5,25},{9,29},{2,22},{6,26},{10,30},{3... | collective-permute-start | bytes 792584 | tf_op jit(solution)/shard_map/ppermute | solution.py:178
  164.5 18.4 %copy-start.1 = (bf16[512,8,128]{2,0,1:T(8,128)(2,1)S(1)}, bf16[512,8,128]{2,0,1:T(8,128)(2,1)}, u32[]{:S(2)}) copy-start(bf16[512,8,128]{2,0,1:T(8,128)(2,1)} %copy.55) | copy-start | bytes 3145732
  164.6 18.4 %copy-start.25 = (pred[512,512]{0,1:T(8,128)(4,1)S(1)}, pred[512,512]{0,1:T(8,128)(4,1)}, u32[]{:S(2)}) copy-start(pred[512,512]{0,1:T(8,128)(4,1)} %copy.57) | copy-start | bytes 786436
  183.0 5.4 %copy-start.4 = (bf16[512,1024]{0,1:T(8,128)(2,1)S(1)}, bf16[512,1024]{0,1:T(8,128)(2,1)}, u32[]{:S(2)}) copy-start(bf16[512,1024]{0,1:T(8,128)(2,1)} %copy.39) | copy-start | bytes 3145732
  188.4 3.2 copy-start.2
  203.1 16.5 %collective-permute-start.5 = (bf16[1032,128]{1,0:T(8,128)(2,1)S(1)}, bf16[1032,128]{1,0:T(8,128)(2,1)}, u32[]{:S(2)}, u32[]{:S(2)}) collective-permute-start(bf16[1032,128]{1,0:T(8,128)(2,1)S(1)} %copy-done.27), channel_id=1, source_target_pairs={{0,24},{4,28},{1,25},{5,29},{2,26},{6,30},{3,27},{7,31}} | collective-permute-start | bytes 792584 | tf_op jit(solution)/shard_map/ppermute | solution.py:178
  204.6 18.0 %collective-permute-start.6 = (bf16[1032,128]{1,0:T(8,128)(2,1)S(1)}, bf16[1032,128]{1,0:T(8,128)(2,1)}, u32[]{:S(2)}, u32[]{:S(2)}) collective-permute-start(bf16[1032,128]{1,0:T(8,128)(2,1)S(1)} %copy-done.27), channel_id=1, source_target_pairs={{0,28},{1,29},{2,30},{3,31}} | collective-permute-start | bytes 792584 | tf_op jit(solution)/shard_map/ppermute | solution.py:178
  305.5 5.7 %copy-start.23 = (f32[8,128,128]{2,1,0:T(8,128)S(1)}, f32[8,128,128]{2,1,0:T(8,128)}, u32[]{:S(2)}) copy-start(f32[8,128,128]{2,1,0:T(8,128)} %get-tuple-element.198) | copy-start | bytes 1572868 | tf_op jit(solution)/shard_map/cond
  318.2 5.7 %copy-start.22 = (f32[8,128,128]{2,1,0:T(8,128)S(1)}, f32[8,128,128]{2,1,0:T(8,128)}, u32[]{:S(2)}) copy-start(f32[8,128,128]{2,1,0:T(8,128)} %get-tuple-element.208) | copy-start | bytes 1572868 | tf_op jit(solution)/shard_map/cond
  331.2 5.7 %copy-start.21 = (f32[8,128,128]{2,1,0:T(8,128)S(1)}, f32[8,128,128]{2,1,0:T(8,128)}, u32[]{:S(2)}) copy-start(f32[8,128,128]{2,1,0:T(8,128)} %get-tuple-element.218) | copy-start | bytes 1572868 | tf_op jit(solution)/shard_map/cond
  344.1 5.7 %copy-start.20 = (f32[8,128,128]{2,1,0:T(8,128)S(1)}, f32[8,128,128]{2,1,0:T(8,128)}, u32[]{:S(2)}) copy-start(f32[8,128,128]{2,1,0:T(8,128)} %get-tuple-element.228) | copy-start | bytes 1572868 | tf_op jit(solution)/shard_map/cond
  376.0 5.7 %collective-permute-start.7 = (bf16[2,128,4096]{2,1,0:T(8,128)(2,1)}, bf16[2,128,4096]{2,1,0:T(8,128)(2,1)}, u32[]{:S(2)}, u32[]{:S(2)}) collective-permute-start(bf16[2,128,4096]{2,1,0:T(8,128)(2,1)} %fusion.159), channel_id=1, source_target_pairs={{0,1},{1,0},{2,3},{3,2},{4,5},{5,4},{6,7},{7,6},{8,9},{9,8},{10,11... | collective-permute-start | bytes 6291464 | tf_op jit(solution)/shard_map/ppermute | solution.py:216
  386.2 25.6 %collective-permute-start.8 = (bf16[128,4096]{1,0:T(8,128)(2,1)S(1)}, bf16[128,4096]{1,0:T(8,128)(2,1)S(1)}, u32[]{:S(2)}, u32[]{:S(2)}) collective-permute-start(bf16[128,4096]{1,0:T(8,128)(2,1)S(1)} %fusion.224), channel_id=1, source_target_pairs={{0,2},{1,3},{2,0},{3,1},{4,6},{5,7},{6,4},{7,5},{8,10},{9,11},{10,... | collective-permute-start | bytes 3145736 | tf_op jit(solution)/shard_map/ppermute | solution.py:231
  (10 other events, 16.5 us)
Sparse Core Ops, SparseCore 0:
  10.1 125.5 all-gather.2
  137.9 162.5 all-gather.4

commit v7 on v6

--- a/solution.py
+++ b/solution.py
@@ -121,7 +121,7 @@
     intra_scores, keys_end, transfer, rotated = jax.vmap(shard_operators)(
         query_heads, key_heads, unit_vectors, strength
     )
-    every_value, keys_end = lax.optimization_barrier((every_value, keys_end))
+    every_value, rotated = lax.optimization_barrier((every_value, rotated))
     row_ids = jnp.arange(block_rows)
     causal = row_ids[:, None] >= row_ids[None, :]
     doc_float = (document_ids + 1).astype(jnp.float32)

time: 426 us -> 417 us (0.979)
  waiting for transfers between devices: 116 us -> 105 us
    all_gather x1, waiting for transfers between devices: 24.3 us -> 0.01 us  [on_device(): every_value = lax.all_gather(value_columns, 'ctx', axis=2, tiled=True)]
    all_gather x1, waiting for transfers between devices: 67.2 us -> 81.3 us  [on_device(): every_key = lax.all_gather(keys_end, 'ctx', axis=1, tiled=True)]
  transfers between devices with their start and end apart: 11 -> 11, of which waited for: 3 -> 2; matrix products, arithmetic and copies ran while one was open for 43% -> 44% of each run, Pallas kernels for 0% -> 0%
where the time goes in v7:
time: 417 us; the launch traced here: 413 us
  matrix products  187 us (45%)
  waiting for transfers between devices  105 us (25%)
  local copies, waits for them, and re-layouts  38.3 us (9%)
  other arithmetic  28.3 us (7%)
  between operations  24 us (6%)
  starting transfers between devices  15.8 us (4%)
  loops' own time  14.9 us (4%)
    all_gather x1, waiting for transfers between devices, on_device(): every_key = lax.all_gather(keys_end, 'ctx', axis=1, tiled=True)  81.3 us
    dot_general x1, matrix products, lower_solve(): return jnp.dot(unit_lower_inverse(strict_lower), right, precision=highest)  24.3 us
    ppermute x1, waiting for transfers between devices, scatter_sum(): lax.ppermute(outgoing.astype(jnp.bfloat16), 'head', pairs)  24 us
    dot_general x1, matrix products, shard_operators(): jnp.dot(scaled_dots, key_solve, precision=highest)  18.4 us
    dot_general x1, matrix products, shard_operators(): jnp.dot(key_solve.T, weighted, precision=highest)  17.5 us
    dot_general x4, matrix products, attend(): jnp.einsum('hqk,hdk->hqd', weights.astype(jnp.bfloat16), value_pair, pref...  17.4 us
    another operation x7, loops' own time, on_device(): carried = lax.cond(step_live, take, lambda inner: inner, carried)  14.9 us
    ppermute x7, starting transfers between devices, on_device(): meta_in = lax.ppermute(meta_rows, 'ctx', pairs).astype(jnp.float32)  14.2 us
  transfers between devices with their start and end apart: 11, of which 2 were waited for; matrix products, arithmetic and copies ran while one was open for 44% of the time, Pallas kernels for 0%

profile of v7, /device:TPU:16, one launch (start us, length us, event | category | flops | bytes accessed | tf_op | source)
XLA Modules:
  0.0 413.4 jit_solution(7920327604877026703)
XLA Ops:
  18.1 7.3 %multiply_select_fusion.1 = f32[8,512,512]{2,1,0:T(8,128)S(1)} fusion(f32[8,512]{1,0:T(8,128)S(1)} %multiply_bitcast_fusion, pred[512,512]{1,0:T(8,128)(4,1)S(1)} %iota_compare_fusion.4, f32[8,512,128]{2,1,0:T(8,128)S(1)} %broadcast_divide_fusion), kind=kOutput, calls=%fused_computation.176 | convolution fusion | flops 3225419776 | bytes 10764288 | tf_op jit(solution)/shard_map/vmap()/dot_general | solution.py:79
  63.5 6.1 %broadcast_select_fusion = f32[8,512,512]{2,1,0:T(8,128)} fusion(pred[512,512]{1,0:T(8,128)(4,1)S(1)} %iota_compare_fusion.4, f32[8,512,128]{2,1,0:T(8,128)S(1)} %broadcast_divide_fusion, bf16[512,8,128]{2,0,1:T(8,128)(2,1)S(1)} %copy.52), kind=kOutput, calls=%fused_computation.192 | convolution fusion | flops 3223322624 | bytes 11796480 | tf_op jit(solution)/shard_map/vmap()/dot_general | solution.py:81
  69.6 24.3 %fusion.133 = f32[8,512,640]{2,1,0:T(8,128)} fusion(f32[8,512,128]{2,1,0:T(8,128)S(1)} %broadcast_divide_fusion, f32[8,512,512]{2,1,0:T(8,128)} %broadcast_select_fusion, f32[8,256,256]{2,1,0:T(8,128)S(1)} %select_maximum_fusion.2, f32[8,128,128]{2,1,0:T(8,128)} %copy-done.24, f32[8,128,128]{2,1,0:T(8,128)S(1)} %convolution_negate_fusion, ...), kind=kOutput, calls=%fused_computation.154 | convolution fusion | flops 16121331712 | bytes 27262976 | tf_op jit(solution)/shard_map/vmap()/dot_general | solution.py:70
  93.9 17.5 %subtract_convert_fusion = bf16[8,512,128]{2,1,0:T(8,128)(2,1)} fusion(f32[8,512,128]{2,1,0:T(8,128)S(1)} %broadcast_divide_fusion, f32[8,512,640]{2,1,0:T(8,128)} %fusion.133, bf16[512,8,128]{2,0,1:T(8,128)(2,1)S(1)} %copy.52, f32[8,512]{1,0:T(8,128)S(1)} %multiply_bitcast_fusion), kind=kOutput, calls=%fused_computation.227 | convolution fusion | flops 3223322624 | bytes 12599296 | tf_op jit(solution)/shard_map/vmap()/dot_general | solution.py:86
  111.4 5.7 %fusion.221 = bf16[8,128,128]{2,1,0:T(8,128)(2,1)S(1)} fusion(f32[8,512,128]{2,1,0:T(8,128)S(1)} %broadcast_divide_fusion, f32[8,512,640]{2,1,0:T(8,128)} %fusion.133, f32[8,512]{1,0:T(8,128)S(1)} %multiply_bitcast_fusion, f32[128,128]{1,0:T(8,128)S(1)} %get-tuple-element.388), kind=kOutput, calls=%fused_computation.247 | convolution fusion | flops 806092800 | bytes 4538368 | tf_op jit(solution)/shard_map/vmap()/dot_general | solution.py:87
  121.9 3.5 collective-permute-start.1
  137.5 4.8 %fusion.226 = f32[8,512,512]{1,2,0:T(8,128)S(1)} fusion(f32[8,512,128]{2,1,0:T(8,128)S(1)} %broadcast_divide_fusion, bf16[512,8,128]{2,0,1:T(8,128)(2,1)} %copy.55), kind=kOutput, calls=%fused_computation.250 | convolution fusion | flops 3221225472 | bytes 11534336 | tf_op jit(solution)/shard_map/vmap()/dot_general | solution.py:90
  142.3 18.4 %fusion.152 = f32[8,512,512]{1,2,0:T(8,128)} fusion(f32[8,512,640]{2,1,0:T(8,128)} %fusion.133, f32[8,512,512]{1,2,0:T(8,128)S(1)} %fusion.226, f32[8,512]{1,0:T(8,128)S(1)} %multiply_bitcast_fusion, pred[512,512]{1,0:T(8,128)(4,1)S(1)} %iota_compare_fusion.3), kind=kOutput, calls=%fused_computation.179 | convolution fusion | flops 12889096192 | bytes 25444352 | tf_op jit(solution)/shard_map/vmap()/dot_general | solution.py:92
  160.7 5.4 %fusion.256 = (f32[8,512]{1,0:T(8,128)S(1)}, f32[8,512,512]{1,2,0:T(8,128)S(1)}) fusion(f32[8,512,512]{1,2,0:T(8,128)} %fusion.152, bf16[512,8,128]{2,0,1:T(8,128)(2,1)S(1)} %copy.52, bf16[512,8,128]{2,0,1:T(8,128)(2,1)S(1)} %copy-done.1, pred[512,512]{0,1:T(8,128)(4,1)S(1)} %copy-done.25), kind=kOutput, calls=%fused_computation.351 | convolution fusion | flops 545255424 | bytes 19152896 | tf_op jit(solution)/shard_map/vmap()/dot_general | solution.py:92
  169.3 9.6 %convert_subtract_fusion = f32[8,512,128]{2,1,0:T(8,128)S(1)} fusion(f32[8,512,640]{2,1,0:T(8,128)} %fusion.133, f32[8,512,512]{1,2,0:T(8,128)S(1)} %fusion.226, f32[8,512]{1,0:T(8,128)S(1)} %multiply_bitcast_fusion, pred[512,512]{1,0:T(8,128)(4,1)S(1)} %iota_compare_fusion.3, bf16[512,8,128]{2,0,1:T(8,128)(2,1)S(1)} %copy-done.2), kind=kOutput, calls=%fused_computation.229 | convolution fusion | flops 3226468352 | bytes 13910016 | tf_op jit(solution)/shard_map/vmap()/dot_general | solution.py:95
  210.9 81.3 %all-gather.5.cloned.1.call-done = bf16[8,4096,128]{2,1,0:T(8,128)(2,1)} async-done(((bf16[8,512,128]{2,1,0:T(8,128)(2,1)}), bf16[8,4096,128]{2,1,0:T(8,128)(2,1)}) %all-gather.5.cloned.1.call-update) | async-done | bytes 8388624 | tf_op jit(solution)/shard_map/all_gather | solution.py:173
  292.2 12.7 %conditional.7 = ((f32[8,512,128]{2,1,0:T(8,128)S(1)}, f32[8,512]{1,0:T(8,128)S(1)}, f32[8,512]{1,0:T(8,128)S(1)}, f32[8,512,128]{2,1,0:T(8,128)})) conditional(s32[]{:T(128)} %convert_element_type.163, (f32[8,512,128]{2,1,0:T(8,128)S(1)}, f32[8,512]{1,0:T(8,128)S(1)}, f32[8,512]{1,0:T(8,128)S(1)}, f32[8,512,128]{2,1,0:T(8,128)}) %tuple.54, ...), branch_computations={%region_3.4_spmd, %region_4.7_spmd} | conditional | flops 1903960064 | bytes 62656712 | solution.py:192
  297.2 4.4 %multiply_add_fusion = f32[8,512,128]{2,1,0:T(8,128)S(1)} fusion(f32[8,512,128]{2,1,0:T(8,128)S(1)} %copy-done.5, f32[8,512,512]{2,1,0:T(8,128)S(1)} %get-tuple-element.347, f32[8,512]{1,0:T(8,128)S(1)} %max.29, pred[512,512]{0,1:T(8,128)(4,1)S(1)} %broadcast_compare_fusion, bf16[8,128,4096]{2,1,0:T(8,128)(2,1)} %get-tuple-element.206, s32[]{:T(128)S(6)} %select_n.248, ...), kind=kOutput, calls=%fused_computation.10 | convolution fusion | flops 546308096 | bytes 13926404 | tf_op jit(solution)/shard_map/cond/branch_1_fun/hqk,hdk->hqd/dot_general | solution.py:156
  304.9 13.1 %conditional.8 = ((f32[8,512,128]{2,1,0:T(8,128)S(1)}, f32[8,512]{1,0:T(8,128)S(1)}, f32[8,512]{1,0:T(8,128)S(1)}, f32[8,512,128]{2,1,0:T(8,128)})) conditional(s32[]{:T(128)} %convert_element_type.162, (f32[8,512,128]{2,1,0:T(8,128)S(1)}, f32[8,512]{1,0:T(8,128)S(1)}, f32[8,512]{1,0:T(8,128)S(1)}, f32[8,512,128]{2,1,0:T(8,128)}) %get-tuple-element.442, ...), branch_computations={%region_7.8_spmd, %region_8.11_spmd} | conditional | flops 1903960064 | bytes 62656712 | solution.py:192
  309.9 4.4 %multiply_add_fusion.2 = f32[8,512,128]{2,1,0:T(8,128)S(1)} fusion(f32[8,512,128]{2,1,0:T(8,128)S(1)} %copy-done.7, f32[8,512,512]{2,1,0:T(8,128)S(1)} %get-tuple-element.349, f32[8,512]{1,0:T(8,128)S(1)} %max.31, pred[512,512]{0,1:T(8,128)(4,1)S(1)} %broadcast_compare_fusion.1, bf16[8,128,4096]{2,1,0:T(8,128)(2,1)} %get-tuple-element.216, ...), kind=kOutput, calls=%fused_computation.32 | convolution fusion | flops 546308096 | bytes 13926404 | tf_op jit(solution)/shard_map/cond/branch_1_fun/hqk,hdk->hqd/dot_general | solution.py:156
  318.0 12.7 %conditional.9 = ((f32[8,512,128]{2,1,0:T(8,128)S(1)}, f32[8,512]{1,0:T(8,128)S(1)}, f32[8,512]{1,0:T(8,128)S(1)}, f32[8,512,128]{2,1,0:T(8,128)})) conditional(s32[]{:T(128)} %convert_element_type.161, (f32[8,512,128]{2,1,0:T(8,128)S(1)}, f32[8,512]{1,0:T(8,128)S(1)}, f32[8,512]{1,0:T(8,128)S(1)}, ...), branch_computations={%region_11.12_spmd, %region_12.15_spmd} | conditional | flops 1903960064 | bytes 62656712 | solution.py:192
  323.0 4.4 %multiply_add_fusion.4 = f32[8,512,128]{2,1,0:T(8,128)S(1)} fusion(f32[8,512,128]{2,1,0:T(8,128)S(1)} %copy-done.9, f32[8,512,512]{2,1,0:T(8,128)S(1)} %get-tuple-element.351, f32[8,512]{1,0:T(8,128)S(1)} %max.33, pred[512,512]{0,1:T(8,128)(4,1)S(1)} %broadcast_compare_fusion.2, bf16[8,128,4096]{2,1,0:T(8,128)(2,1)} %get-tuple-element.226, ...), kind=kOutput, calls=%fused_computation.54 | convolution fusion | flops 546308096 | bytes 13926404 | tf_op jit(solution)/shard_map/cond/branch_1_fun/hqk,hdk->hqd/dot_general | solution.py:156
  330.6 12.9 %conditional.10 = ((f32[8,512,128]{2,1,0:T(8,128)S(1)}, f32[8,512]{1,0:T(8,128)S(1)}, f32[8,512]{1,0:T(8,128)S(1)}, f32[8,512,128]{2,1,0:T(8,128)})) conditional(s32[]{:T(128)} %convert_element_type.160, (f32[8,512,128]{2,1,0:T(8,128)S(1)}, f32[8,512]{1,0:T(8,128)S(1)}, f32[8,512]{1,0:T(8,128)S(1)}, ...), branch_computations={%region_15.16_spmd, %region_16.19_spmd} | conditional | flops 1903960064 | bytes 62656712 | solution.py:192
  335.8 4.4 %multiply_add_fusion.6 = f32[8,512,128]{2,1,0:T(8,128)S(1)} fusion(f32[8,512,128]{2,1,0:T(8,128)S(1)} %copy-done.11, f32[8,512,512]{2,1,0:T(8,128)S(1)} %get-tuple-element.353, f32[8,512]{1,0:T(8,128)S(1)} %max.35, pred[512,512]{0,1:T(8,128)(4,1)S(1)} %broadcast_compare_fusion.3, bf16[8,128,4096]{2,1,0:T(8,128)(2,1)} %get-tuple-element.236, ...), kind=kOutput, calls=%fused_computation.76 | convolution fusion | flops 546308096 | bytes 13926404 | tf_op jit(solution)/shard_map/cond/branch_1_fun/hqk,hdk->hqd/dot_general | solution.py:156
  343.7 5.6 %conditional.12 = ((f32[8,512,128]{2,1,0:T(8,128)S(1)}, f32[8,512]{1,0:T(8,128)S(1)}, f32[8,512]{1,0:T(8,128)S(1)}, f32[8,512,128]{2,1,0:T(8,128)})) conditional(s32[]{:T(128)} %convert_element_type.158, (f32[8,512,128]{2,1,0:T(8,128)S(1)}, f32[8,512]{1,0:T(8,128)S(1)}, f32[8,512]{1,0:T(8,128)S(1)}, ...), branch_computations={%region_23.24_spmd, %region_24.27_spmd} | conditional | flops 1903960064 | bytes 61608112 | solution.py:192
  349.4 8.1 %conditional.13 = ((f32[8,512]{1,0:T(8,128)S(1)}, f32[8,512,128]{2,1,0:T(8,128)})) conditional(s32[]{:T(128)} %convert_element_type.157, (f32[8,512]{1,0:T(8,128)S(1)}, f32[8,512,128]{2,1,0:T(8,128)}) %tuple.61, (f32[512]{0:T(512)S(1)}, f32[512]{0:T(512)S(1)}, s32[]{:T(128)}, bf16[8,4096,128]{2,1,0:T(8,128)(2,1)}, f32[8,512,128]{2,1,0:T(8,128)S(1)}, ...), branch_computations={%region_27.28_spmd, %region_28.31_spmd} | conditional | flops 1098653696 | bytes 51613852 | solution.py:192
  360.6 7.1 %fusion.159 = bf16[2,128,4096]{2,1,0:T(8,128)(2,1)} fusion(bf16[1024,4096]{1,0:T(8,128)(2,1)} %param.27, bf16[2,2,128,1024]{3,2,1,0:T(8,128)(2,1)S(1)} %reshape_reshape.3, s32[]{:T(128)S(6)} %select_n.311), kind=kOutput, calls=%fused_computation.184 | convolution fusion | flops 2148532224 | bytes 11010052 | tf_op jit(solution)/shard_map/crk,kf->crf/dot_general | solution.py:209
  367.7 5.7 %fusion.147 = f32[2,128,4096]{2,1,0:T(8,128)S(1)} fusion(bf16[1024,4096]{1,0:T(8,128)(2,1)} %param.27, bf16[2,2,128,1024]{3,2,1,0:T(8,128)(2,1)S(1)} %reshape_reshape.3, s32[]{:T(128)S(6)} %select_n.310), kind=kOutput, calls=%fused_computation.170 | convolution fusion | flops 2147483648 | bytes 13107204 | tf_op jit(solution)/shard_map/crk,kf->crf/dot_general | solution.py:217
  379.5 24.0 %collective-permute-done.8 = bf16[128,4096]{1,0:T(8,128)(2,1)S(1)} collective-permute-done((bf16[128,4096]{1,0:T(8,128)(2,1)S(1)}, bf16[128,4096]{1,0:T(8,128)(2,1)S(1)}, u32[]{:S(2)}, u32[]{:S(2)}) %collective-permute-start.8) | collective-permute-done | bytes 1048608 | tf_op jit(solution)/shard_map/ppermute | solution.py:231
  (188 shorter events, 136.8 us)
Async XLA Ops:
  6.5 2.4 copy-start.26
  6.5 204.4 %all-gather.3.cloned.1.call-start = ((), (), s32[]{:S(2)}) async-start(), calls=%async_computation | async-start | bytes 9437184 | tf_op jit(solution)/shard_map/all_gather | solution.py:120
  10.0 4.8 %copy-start = (f32[512,8,128]{2,0,1:T(8,128)}, f32[512,8,128]{2,0,1:T(8,128)S(1)}, u32[]{:S(2)}) copy-start(f32[512,8,128]{2,0,1:T(8,128)S(1)} %copy.41) | copy-start | bytes 6291460
  10.0 282.2 %all-gather.5.cloned.1.call-start = ((), (), s32[]{:S(2)}) async-start(), calls=%async_computation.1 | async-start | bytes 9437184 | tf_op jit(solution)/shard_map/all_gather | solution.py:173
  13.0 2.9 copy-start.28
  54.4 7.0 %copy-start.24 = (f32[8,128,128]{2,1,0:T(8,128)}, f32[8,128,128]{2,1,0:T(8,128)S(1)}, u32[]{:S(2)}) copy-start(f32[8,128,128]{2,1,0:T(8,128)S(1)} %get-tuple-element.367) | copy-start | bytes 1572868
  93.9 17.5 %copy-start.29 = (s32[512]{0:T(512)S(1)}, s32[512]{0:T(512)}, u32[]{:S(2)}) copy-start(s32[512]{0:T(512)} %param.26) | copy-start | bytes 6148
  118.5 62.4 %collective-permute-start = (bf16[1032,128]{1,0:T(8,128)(2,1)}, bf16[1032,128]{1,0:T(8,128)(2,1)S(1)}, u32[]{:S(2)}, u32[]{:S(2)}) collective-permute-start(bf16[1032,128]{1,0:T(8,128)(2,1)} %concatenate.48), channel_id=1, source_target_pairs={{0,4},{4,8},{8,12},{12,16},{16,20},{20,24},{24,28},{1,5},{5,9},{9,... | collective-permute-start | bytes 792584 | tf_op jit(solution)/shard_map/ppermute | solution.py:178
  121.9 60.4 %collective-permute-start.1 = (bf16[1032,128]{1,0:T(8,128)(2,1)}, bf16[1032,128]{1,0:T(8,128)(2,1)}, u32[]{:S(2)}, u32[]{:S(2)}) collective-permute-start(bf16[1032,128]{1,0:T(8,128)(2,1)} %concatenate.48), channel_id=1, source_target_pairs={{0,8},{4,12},{8,16},{12,20},{16,24},{20,28},{1,9},{5,13},{9,17},{1... | collective-permute-start | bytes 792584 | tf_op jit(solution)/shard_map/ppermute | solution.py:178
  125.4 59.3 %collective-permute-start.2 = (bf16[1032,128]{1,0:T(8,128)(2,1)}, bf16[1032,128]{1,0:T(8,128)(2,1)}, u32[]{:S(2)}, u32[]{:S(2)}) collective-permute-start(bf16[1032,128]{1,0:T(8,128)(2,1)} %concatenate.48), channel_id=1, source_target_pairs={{0,12},{4,16},{8,20},{12,24},{16,28},{1,13},{5,17},{9,21},{13,25},... | collective-permute-start | bytes 792584 | tf_op jit(solution)/shard_map/ppermute | solution.py:178
  127.3 58.4 %collective-permute-start.3 = (bf16[1032,128]{1,0:T(8,128)(2,1)}, bf16[1032,128]{1,0:T(8,128)(2,1)}, u32[]{:S(2)}, u32[]{:S(2)}) collective-permute-start(bf16[1032,128]{1,0:T(8,128)(2,1)} %concatenate.48), channel_id=1, source_target_pairs={{0,16},{4,20},{8,24},{12,28},{1,17},{5,21},{9,25},{13,29},{2,18},{... | collective-permute-start | bytes 792584 | tf_op jit(solution)/shard_map/ppermute | solution.py:178
  128.6 58.1 %collective-permute-start.4 = (bf16[1032,128]{1,0:T(8,128)(2,1)}, bf16[1032,128]{1,0:T(8,128)(2,1)}, u32[]{:S(2)}, u32[]{:S(2)}) collective-permute-start(bf16[1032,128]{1,0:T(8,128)(2,1)} %concatenate.48), channel_id=1, source_target_pairs={{0,20},{4,24},{8,28},{1,21},{5,25},{9,29},{2,22},{6,26},{10,30},{3... | collective-permute-start | bytes 792584 | tf_op jit(solution)/shard_map/ppermute | solution.py:178
  142.3 18.4 %copy-start.1 = (bf16[512,8,128]{2,0,1:T(8,128)(2,1)S(1)}, bf16[512,8,128]{2,0,1:T(8,128)(2,1)}, u32[]{:S(2)}) copy-start(bf16[512,8,128]{2,0,1:T(8,128)(2,1)} %copy.55) | copy-start | bytes 3145732
  142.3 18.4 %copy-start.25 = (pred[512,512]{0,1:T(8,128)(4,1)S(1)}, pred[512,512]{0,1:T(8,128)(4,1)}, u32[]{:S(2)}) copy-start(pred[512,512]{0,1:T(8,128)(4,1)} %copy.57) | copy-start | bytes 786436
  160.7 5.4 %copy-start.4 = (bf16[512,1024]{0,1:T(8,128)(2,1)S(1)}, bf16[512,1024]{0,1:T(8,128)(2,1)}, u32[]{:S(2)}) copy-start(bf16[512,1024]{0,1:T(8,128)(2,1)} %copy.39) | copy-start | bytes 3145732
  166.1 3.2 copy-start.2
  180.9 16.5 %collective-permute-start.5 = (bf16[1032,128]{1,0:T(8,128)(2,1)S(1)}, bf16[1032,128]{1,0:T(8,128)(2,1)}, u32[]{:S(2)}, u32[]{:S(2)}) collective-permute-start(bf16[1032,128]{1,0:T(8,128)(2,1)S(1)} %copy-done.27), channel_id=1, source_target_pairs={{0,24},{4,28},{1,25},{5,29},{2,26},{6,30},{3,27},{7,31}} | collective-permute-start | bytes 792584 | tf_op jit(solution)/shard_map/ppermute | solution.py:178
  182.3 18.0 %collective-permute-start.6 = (bf16[1032,128]{1,0:T(8,128)(2,1)S(1)}, bf16[1032,128]{1,0:T(8,128)(2,1)}, u32[]{:S(2)}, u32[]{:S(2)}) collective-permute-start(bf16[1032,128]{1,0:T(8,128)(2,1)S(1)} %copy-done.27), channel_id=1, source_target_pairs={{0,28},{1,29},{2,30},{3,31}} | collective-permute-start | bytes 792584 | tf_op jit(solution)/shard_map/ppermute | solution.py:178
  297.2 5.7 %copy-start.23 = (f32[8,128,128]{2,1,0:T(8,128)S(1)}, f32[8,128,128]{2,1,0:T(8,128)}, u32[]{:S(2)}) copy-start(f32[8,128,128]{2,1,0:T(8,128)} %get-tuple-element.198) | copy-start | bytes 1572868 | tf_op jit(solution)/shard_map/cond
  309.9 5.7 %copy-start.22 = (f32[8,128,128]{2,1,0:T(8,128)S(1)}, f32[8,128,128]{2,1,0:T(8,128)}, u32[]{:S(2)}) copy-start(f32[8,128,128]{2,1,0:T(8,128)} %get-tuple-element.208) | copy-start | bytes 1572868 | tf_op jit(solution)/shard_map/cond
  323.0 5.7 %copy-start.21 = (f32[8,128,128]{2,1,0:T(8,128)S(1)}, f32[8,128,128]{2,1,0:T(8,128)}, u32[]{:S(2)}) copy-start(f32[8,128,128]{2,1,0:T(8,128)} %get-tuple-element.218) | copy-start | bytes 1572868 | tf_op jit(solution)/shard_map/cond
  335.8 5.7 %copy-start.20 = (f32[8,128,128]{2,1,0:T(8,128)S(1)}, f32[8,128,128]{2,1,0:T(8,128)}, u32[]{:S(2)}) copy-start(f32[8,128,128]{2,1,0:T(8,128)} %get-tuple-element.228) | copy-start | bytes 1572868 | tf_op jit(solution)/shard_map/cond
  367.7 5.7 %collective-permute-start.7 = (bf16[2,128,4096]{2,1,0:T(8,128)(2,1)}, bf16[2,128,4096]{2,1,0:T(8,128)(2,1)}, u32[]{:S(2)}, u32[]{:S(2)}) collective-permute-start(bf16[2,128,4096]{2,1,0:T(8,128)(2,1)} %fusion.159), channel_id=1, source_target_pairs={{0,1},{1,0},{2,3},{3,2},{4,5},{5,4},{6,7},{7,6},{8,9},{9,8},{10,11... | collective-permute-start | bytes 6291464 | tf_op jit(solution)/shard_map/ppermute | solution.py:216
  377.9 25.6 %collective-permute-start.8 = (bf16[128,4096]{1,0:T(8,128)(2,1)S(1)}, bf16[128,4096]{1,0:T(8,128)(2,1)S(1)}, u32[]{:S(2)}, u32[]{:S(2)}) collective-permute-start(bf16[128,4096]{1,0:T(8,128)(2,1)S(1)} %fusion.224), channel_id=1, source_target_pairs={{0,2},{1,3},{2,0},{3,1},{4,6},{5,7},{6,4},{7,5},{8,10},{9,11},{10,... | collective-permute-start | bytes 3145736 | tf_op jit(solution)/shard_map/ppermute | solution.py:231
  (10 other events, 16.5 us)
Sparse Core Ops, SparseCore 0:
  10.1 125.5 all-gather.2
  137.9 154.2 all-gather.4
